TPU v7x, 768 devices: a whole 4x8x12 slice. The times are simulated.
768 devices in a mesh: tm: 8 (over y), rows: 6 (over z_lo), cols: 16 (over z_hi, x, core).
Axes of the slice: x: 4, y: 8, z: 12 (z_hi: 2, z_lo: 6; z = z_hi * 6 + z_lo), core: 2. Of those that a mesh axis runs over, the one named last changes fastest.
Arguments:
- video: bfloat16 [16, 96, 256, 192], P('tm', 'rows', 'cols'), may hold values from -40 to 40, as said below
- cotangent: bfloat16 [16, 96, 256, 192], P('tm', 'rows', 'cols'), may hold values from -40 to 40, as said below
- weight: bfloat16 [5184, 192], P(('rows', 'cols')), may hold values from -0.078125 to 0.078125
- gain: float32 [192], replicated, may hold values from 0.25 to 1.75
- shift: float32 [192], replicated, may hold values from -3 to 3
- conv_bias: float32 [192], replicated, may hold values from -2 to 2
Outputs:
- output: bfloat16 [16, 96, 256, 192], P('tm', 'rows', 'cols')
- grad_video: bfloat16 [16, 96, 256, 192], P('tm', 'rows', 'cols')
- grad_weight: float32 [5184, 192], P(('rows', 'cols'))
- grad_gain: float32 [192], replicated
- grad_shift: float32 [192], replicated
- grad_conv_bias: float32 [192], replicated
Inputs may be any that keep to these rules, and one draw needn't show every extreme that they name: `video`: Real-valued activations; their magnitude varies across frames, rows and columns. `cotangent`: Real-valued gradients; their magnitude varies across frames, rows and columns.
All inputs are finite; a program needn't handle non-finite values.
Results may differ from a plain program's by a relative error of at most 0.0031.
Values may be sent and summed in bfloat16 or wider, within the bound.
No kernel may reach another device: no remote copies, remote signals or barrier semaphores. Data moves between devices by JAX's collectives and lax.ppermute only.
A program may use at most 64 MiB of HBM per device.

v0:
```python
import jax
import jax.numpy as jnp
from jax import lax
from jax.sharding import PartitionSpec as P

CH = 192
GROUPS = 32


def padded_2(block, sides, width):
    for axis, dim in sides:
        count = lax.axis_size(axis)
        forward = [(i, i + 1) for i in range(count - 1)]
        backward = [(target, source) for source, target in forward]
        low = lax.ppermute(
            lax.slice_in_dim(block, block.shape[dim] - width, None, axis=dim), axis, forward
        )
        high = lax.ppermute(lax.slice_in_dim(block, 0, width, axis=dim), axis, backward)
        block = jnp.concatenate([low, block, high], axis=dim)
    return block


def per_group(values):
    return jnp.repeat(values.reshape(GROUPS, -1).sum(axis=1), CH // GROUPS)


def to_pairs(field, pair_count, local_rows, local_cols, channels):
    paired = field.reshape(pair_count, 2, local_rows, local_cols, channels)
    return paired.transpose(0, 2, 3, 1, 4).reshape(pair_count, local_rows, local_cols, 2 * channels)


def from_pairs(field, local_rows, local_cols, channels):
    pair_count = field.shape[0]
    split = field.reshape(pair_count, local_rows + 2, local_cols + 2, 2, channels)
    return split.transpose(0, 3, 1, 2, 4).reshape(
        2 * pair_count, local_rows + 2, local_cols + 2, channels
    )


def per_device(video, cotangent, weight, gain, shift, conv_bias):
    local_frames, local_rows, local_cols, channels = video.shape
    pair_count = local_frames // 2
    packed = jnp.concatenate(
        [
            to_pairs(video, pair_count, local_rows, local_cols, channels),
            to_pairs(cotangent, pair_count, local_rows, local_cols, channels),
        ],
        axis=-1,
    )
    framed = padded_2(packed, (("tm", 0), ("rows", 1), ("cols", 2)), 1)
    video_ext = from_pairs(
        framed[: pair_count + 1, :, :, : 2 * channels], local_rows, local_cols, channels
    )
    grad_ext = from_pairs(framed[1:, :, :, 2 * channels :], local_rows, local_cols, channels)
    video_f = video.astype(jnp.float32)
    sums, squares = lax.psum(
        (jnp.sum(video_f, axis=(0, 1, 2)), jnp.sum(video_f * video_f, axis=(0, 1, 2))),
        ("tm", "rows", "cols"),
    )
    devices_all = lax.axis_size("tm") * lax.axis_size("rows") * lax.axis_size("cols")
    count = float(local_frames * local_rows * local_cols * devices_all * (channels // GROUPS))
    mean_c = per_group(sums) / count
    variance = per_group(squares) / count - mean_c * mean_c
    rstd_c = lax.rsqrt(variance + 1e-06)
    normed_ext = (video_ext.astype(jnp.float32) - mean_c) * rstd_c
    pre_ext = normed_ext * gain + shift
    frame_pos = lax.broadcasted_iota(jnp.int32, (local_frames + 2, 1, 1, 1), 0)
    row_pos = lax.broadcasted_iota(jnp.int32, (1, local_rows + 2, 1, 1), 1)
    col_pos = lax.broadcasted_iota(jnp.int32, (1, 1, local_cols + 2, 1), 2)
    time_index = lax.axis_index("tm")
    row_index = lax.axis_index("rows")
    col_index = lax.axis_index("cols")
    valid = (frame_pos >= 2) | (time_index > 0)
    valid = (
        valid
        & ((row_pos > 0) | (row_index > 0))
        & ((row_pos < local_rows + 1) | (row_index < lax.axis_size("rows") - 1))
    )
    valid = (
        valid
        & ((col_pos > 0) | (col_index > 0))
        & ((col_pos < local_cols + 1) | (col_index < lax.axis_size("cols") - 1))
    )
    padded = jnp.where(valid, jax.nn.silu(pre_ext), 0.0).astype(jnp.bfloat16)
    whole = lax.all_gather(weight, ("rows", "cols"), axis=0, tiled=True)
    cells = local_frames * local_rows * local_cols
    windows = []
    grad_windows = []
    for tap_t in range(3):
        for tap_r in range(3):
            for tap_c in range(3):
                windows.append(
                    padded[
                        tap_t : tap_t + local_frames,
                        tap_r : tap_r + local_rows,
                        tap_c : tap_c + local_cols,
                    ]
                )
                grad_windows.append(
                    grad_ext[
                        2 - tap_t : 2 - tap_t + local_frames,
                        2 - tap_r : 2 - tap_r + local_rows,
                        2 - tap_c : 2 - tap_c + local_cols,
                    ]
                )
    patches = jnp.concatenate(windows, axis=-1).reshape(cells, 27 * channels)
    grad_patches = jnp.concatenate(grad_windows, axis=-1).reshape(cells, 27 * channels)
    conv = jnp.dot(patches, whole, preferred_element_type=jnp.float32) + conv_bias
    output = (video_f + conv.reshape(local_frames, local_rows, local_cols, channels)).astype(
        jnp.bfloat16
    )
    grad_flat = cotangent.reshape(cells, channels)
    kernel_grad = lax.dot_general(
        patches, grad_flat, (((0,), (0,)), ((), ())), preferred_element_type=jnp.float32
    )
    flipped = (
        whole.reshape(27, channels, channels).transpose(0, 2, 1).reshape(27 * channels, channels)
    )
    grad_hidden = jnp.dot(grad_patches, flipped, preferred_element_type=jnp.float32).astype(
        jnp.bfloat16
    )
    grad_hidden = lax.optimization_barrier(grad_hidden).astype(jnp.float32)
    grad_hidden = grad_hidden.reshape(local_frames, local_rows, local_cols, channels)
    normed = normed_ext[2:, 1:-1, 1:-1]
    pre = pre_ext[2:, 1:-1, 1:-1]
    sigma = jax.nn.sigmoid(pre)
    grad_pre = grad_hidden * sigma * (1.0 + pre * (1.0 - sigma))
    grad_f = cotangent.astype(jnp.float32)
    gain_part = jnp.sum(grad_pre * normed, axis=(0, 1, 2))
    shift_part = jnp.sum(grad_pre, axis=(0, 1, 2))
    bias_part = jnp.sum(grad_f, axis=(0, 1, 2))
    grad_gain, grad_shift, grad_conv_bias = lax.psum(
        (gain_part, shift_part, bias_part), ("tm", "rows", "cols")
    )
    band_sum = lax.psum_scatter(kernel_grad, ("rows", "cols"), scatter_dimension=0, tiled=True)
    grad_weight = lax.psum(band_sum, "tm")
    term_a = per_group(gain * grad_shift) / count
    term_b = per_group(gain * grad_gain) / count
    grad_video = (grad_f + rstd_c * (grad_pre * gain - term_a - normed * term_b)).astype(
        jnp.bfloat16
    )
    return (output, grad_video, grad_weight, grad_gain, grad_shift, grad_conv_bias)


def solution(mesh):
    return jax.shard_map(
        per_device,
        mesh=mesh,
        in_specs=(
            P("tm", "rows", "cols", None),
            P("tm", "rows", "cols", None),
            P(("rows", "cols"), None),
            P(),
            P(),
            P(),
        ),
        out_specs=(
            P("tm", "rows", "cols", None),
            P("tm", "rows", "cols", None),
            P(("rows", "cols"), None),
            P(),
            P(),
            P(),
        ),
        check_vma=False,
    )
```

profile of v0, /device:TPU:1, one launch (start us, length us, event | category | flops | bytes accessed | tf_op | source)
XLA Modules:
  0.0 768.2 jit_solution(15259951080217296902)
XLA Ops:
  10.1 4.0 collective-permute-start
  15.9 120.5 %all-reduce.3 = (f32[32,6]{1,0:T(8,128)S(1)}, f32[32,6]{1,0:T(8,128)S(1)}) all-reduce(f32[32,6]{1,0:T(8,128)S(1)} %reshape.206, f32[32,6]{1,0:T(8,128)S(1)} %reshape.205), channel_id=1, replica_groups=mesh['tm'=8,'rows'=6,'cols'=16] {'tm','rows','cols'}, use_global_device_ids=true, to_apply=%region_4.0 | all-reduce | flops 384 | bytes 3072 | tf_op jit(solution)/shard_map/psum | solution.py:56
  137.2 2.5 collective-permute-start.2
  143.0 1.9 collective-permute-done.3
  145.2 5.6 collective-permute-start.4
  150.8 1.9 collective-permute-start.5
  153.2 4.4 collective-permute-done.5
  157.6 4.3 fusion.3
  162.0 2.2 multiply_add_fusion
  164.2 1.9 fusion.10
  166.1 1.4 fusion.11
  167.6 9.7 %concatenate.29 = bf16[2,16,16,5184]{3,2,1,0:T(8,128)(2,1)} concatenate(bf16[2,16,16,192]{3,2,1,0:T(8,128)(2,1)} %get-tuple-element.76, bf16[2,16,16,192]{3,2,1,0:T(8,128)(2,1)} %get-tuple-element.75, bf16[2,16,16,192]{3,2,1,0:T(8,128)(2,1)} %get-tuple-element.74, bf16[2,16,16,192]{3,2,1,0:T(8,128)(2,1)} %get-tuple-element.73, bf16[2,16,16,192]{3,2,1,0:T(8,128)(2,1)} %get-tuple-element.72, ...), dimensions={3} | concatenate | bytes 10616832 | tf_op jit(solution)/shard_map/concatenate | solution.py:106
  177.3 6.5 convolution_bitcast_fusion
  183.8 331.8 %fusion = f32[56,192]{1,0:T(8,128)S(1)} fusion(f32[5184,192]{1,0:T(8,128)} %convolution_bitcast_fusion), kind=kCustom, calls=%all-reduce-scatter | all-reduce-scatter fusion | flops 1032193 | bytes 4028416
  515.6 4.2 collective-permute-start.6
  519.8 14.6 %collective-permute-start.7 = (f32[56,192]{1,0:T(8,128)S(1)}, f32[56,192]{1,0:T(8,128)}, u32[]{:S(2)}, u32[]{:S(2)}) collective-permute-start(f32[56,192]{1,0:T(8,128)S(1)} %fusion), channel_id=1, source_target_pairs={{0,2},{1,3},{2,4},{3,5},{4,6},{5,7},{6,8},{7,9},{8,10},{9,11},{10,... | collective-permute-start | bytes 129032
  534.5 23.3 %collective-permute-start.8 = (f32[56,192]{1,0:T(8,128)S(1)}, f32[56,192]{1,0:T(8,128)}, u32[]{:S(2)}, u32[]{:S(2)}) collective-permute-start(f32[56,192]{1,0:T(8,128)S(1)} %fusion), channel_id=1, source_target_pairs={{0,3},{1,4},{2,5},{3,6},{4,7},{5,8},{6,9},{7,10},{8,11},{9,12},{10... | collective-permute-start | bytes 129032
  558.4 12.0 %collective-permute-start.9 = (f32[22,192]{1,0:T(8,128)}, f32[22,192]{1,0:T(8,128)}, u32[]{:S(2)}, u32[]{:S(2)}) collective-permute-start(f32[22,192]{1,0:T(8,128)} %slice.318), channel_id=1, source_target_pairs={{0,4},{1,5},{2,6},{3,7},{4,8},{5,9},{6,10},{7,11},{8,12},{9,13},{1... | collective-permute-start | bytes 50696
  570.3 3.9 fusion.2
  574.3 1.7 fusion.8
  576.0 1.4 fusion.9
  577.4 9.5 %concatenate.31 = bf16[2,16,16,5184]{3,2,1,0:T(8,128)(2,1)} concatenate(bf16[2,16,16,192]{3,2,1,0:T(8,128)(2,1)} %get-tuple-element.49, bf16[2,16,16,192]{3,2,1,0:T(8,128)(2,1)} %get-tuple-element.48, bf16[2,16,16,192]{3,2,1,0:T(8,128)(2,1)} %get-tuple-element.47, bf16[2,16,16,192]{3,2,1,0:T(8,128)(2,1)} %get-tuple-element.46, bf16[2,16,16,192]{3,2,1,0:T(8,128)(2,1)} %get-tuple-element.45, ...), dimensions={3} | concatenate | bytes 10616832 | tf_op jit(solution)/shard_map/concatenate | solution.py:107
  587.0 2.8 concatenate.32
  589.8 24.2 %psum.46 = f32[54,192]{1,0:T(8,128)} all-reduce(f32[54,192]{1,0:T(8,128)S(1)} %constant_dynamic-slice_fusion), channel_id=1, replica_groups=mesh['tm'=8,'rows'=6,'cols'=16] {'tm'}, use_global_device_ids=true, to_apply=%region_13.14 | all-reduce | flops 10368 | bytes 82944 | tf_op jit(solution)/shard_map/psum | solution.py:136
  614.0 5.3 reshape.211
  619.3 3.8 copy.22
  623.1 4.4 convolution_convert_fusion
  628.5 2.7 fusion.7
  631.2 118.2 %all-reduce.2 = (f32[192]{0:T(256)S(1)}, f32[192]{0:T(256)S(1)}, f32[192]{0:T(256)}) all-reduce(f32[192]{0:T(256)S(1)} %get-tuple-element.7, f32[192]{0:T(256)S(1)} %get-tuple-element.6, f32[192]{0:T(256)S(1)} %convert_reduce_fusion.1), channel_id=1, replica_groups=mesh['tm'=8,'rows'=6,'cols'=16] {'tm','rows','cols'}, use_global_device_ids=true, to_apply=%region_10.11 | all-reduce | flops 576 | bytes 4608 | tf_op jit(solution)/shard_map/psum | solution.py:132
  750.3 2.6 reshape.221
  753.0 5.3 convolution_add_fusion
  759.3 2.0 fusion.4
  (90 shorter events, 12.1 us)
Async XLA Ops:
  7.2 8.3 %copy-start.1 = (bf16[2,16,16,192]{3,2,1,0:T(8,128)(2,1)S(1)}, bf16[2,16,16,192]{3,2,1,0:T(8,128)(2,1)}, u32[]{:S(2)}) copy-start(bf16[2,16,16,192]{3,2,1,0:T(8,128)(2,1)} %param.6) | copy-start | bytes 589828
  7.2 606.8 %all-gather.3.cloned.1.call-start = ((), (), s32[]{:S(2)}) async-start(), calls=%async_computation | async-start | bytes 2781184 | tf_op jit(solution)/shard_map/all_gather | solution.py:85
  10.1 127.0 %collective-permute-start = (bf16[1,16,16,768]{3,2,1,0:T(8,128)(2,1)S(1)}, bf16[1,16,16,768]{3,2,1,0:T(8,128)(2,1)S(1)}, u32[]{:S(2)}, u32[]{:S(2)}) collective-permute-start(bf16[1,16,16,768]{3,2,1,0:T(8,128)(2,1)S(1)} %constant_dynamic-update-slice_fusion), channel_id=1, source_target_pairs={{0,96},{96,192},{192,288},{288,384},{384,480},{480,576},{576,672},... | collective-permute-start | bytes 1179656 | tf_op jit(solution)/shard_map/ppermute | solution.py:15
  14.2 123.0 %collective-permute-start.1 = (bf16[1,16,16,768]{3,2,1,0:T(8,128)(2,1)S(1)}, bf16[1,16,16,768]{3,2,1,0:T(8,128)(2,1)S(1)}, u32[]{:S(2)}, u32[]{:S(2)}) collective-permute-start(bf16[1,16,16,768]{3,2,1,0:T(8,128)(2,1)S(1)} %constant_dynamic-update-slice_fusion), channel_id=1, source_target_pairs={{96,0},{192,96},{288,192},{384,288},{480,384},{576,480},{672,576},... | collective-permute-start | bytes 1179656 | tf_op jit(solution)/shard_map/ppermute | solution.py:18
  15.5 137.2 %copy-start.2 = (bf16[2,16,16,192]{3,2,1,0:T(8,128)(2,1)S(1)}, bf16[2,16,16,192]{3,2,1,0:T(8,128)(2,1)}, u32[]{:S(2)}) copy-start(bf16[2,16,16,192]{3,2,1,0:T(8,128)(2,1)} %param.7) | copy-start | bytes 589828
  137.2 5.8 collective-permute-start.2
  139.7 5.1 collective-permute-start.3
  143.0 19.0 %copy-start.8 = (bf16[3,1,16,768]{3,2,1,0:T(8,128)(2,1)}, bf16[3,1,16,768]{3,2,1,0:T(8,128)(2,1)S(1)}, u32[]{:S(2)}) copy-start(bf16[3,1,16,768]{3,2,1,0:T(8,128)(2,1)S(1)} %collective-permute-done.2) | copy-start | bytes 221188
  144.9 17.1 %copy-start.10 = (bf16[3,1,16,768]{3,2,1,0:T(8,128)(2,1)}, bf16[3,1,16,768]{3,2,1,0:T(8,128)(2,1)S(1)}, u32[]{:S(2)}) copy-start(bf16[3,1,16,768]{3,2,1,0:T(8,128)(2,1)S(1)} %collective-permute-done.3) | copy-start | bytes 221188
  145.1 16.8 %copy-start.12 = (f32[192]{0:T(256)S(1)}, f32[192]{0:T(256)}, u32[]{:S(2)}) copy-start(f32[192]{0:T(256)} %param.9) | copy-start | bytes 2308
  145.2 16.8 %copy-start.16 = (f32[192]{0:T(256)S(1)}, f32[192]{0:T(256)}, u32[]{:S(2)}) copy-start(f32[192]{0:T(256)} %param.10) | copy-start | bytes 2308
  145.2 8.0 %collective-permute-start.4 = (bf16[3,18,1,768]{3,2,1,0:T(2,128)(2,1)S(1)}, bf16[3,18,1,768]{3,2,1,0:T(2,128)(2,1)S(1)}, u32[]{:S(2)}, u32[]{:S(2)}) collective-permute-start(bf16[3,18,1,768]{3,2,1,0:T(2,128)(2,1)S(1)} %get-tuple-element.16), channel_id=1, source_target_pairs={{0,1},{1,2},{2,3},{3,4},{4,5},{5,6},{6,7},{7,8},{8,9},{9,10},{10,1... | collective-permute-start | bytes 248840 | tf_op jit(solution)/shard_map/ppermute | solution.py:15
  150.8 6.9 collective-permute-start.5
  153.2 11.0 %copy-start.4 = (bf16[3,18,1,768]{3,2,1,0:T(2,128)(2,1)}, bf16[3,18,1,768]{3,2,1,0:T(2,128)(2,1)S(1)}, u32[]{:S(2)}) copy-start(bf16[3,18,1,768]{3,2,1,0:T(2,128)(2,1)S(1)} %collective-permute-done.4) | copy-start | bytes 248836
  157.6 6.5 copy-start.6
  183.8 386.5 %copy-start.5 = (bf16[3,18,1,768]{3,2,1,0:T(2,128)(2,1)S(1)}, bf16[3,18,1,768]{3,2,1,0:T(2,128)(2,1)}, u32[]{:S(2)}) copy-start(bf16[3,18,1,768]{3,2,1,0:T(2,128)(2,1)} %copy-done.4) | copy-start | bytes 248836
  183.8 386.5 %copy-start.7 = (bf16[3,18,1,768]{3,2,1,0:T(2,128)(2,1)S(1)}, bf16[3,18,1,768]{3,2,1,0:T(2,128)(2,1)}, u32[]{:S(2)}) copy-start(bf16[3,18,1,768]{3,2,1,0:T(2,128)(2,1)} %copy-done.6) | copy-start | bytes 248836
  183.8 386.5 %copy-start.9 = (bf16[3,1,16,768]{3,2,1,0:T(8,128)(2,1)S(1)}, bf16[3,1,16,768]{3,2,1,0:T(8,128)(2,1)}, u32[]{:S(2)}) copy-start(bf16[3,1,16,768]{3,2,1,0:T(8,128)(2,1)} %copy-done.8) | copy-start | bytes 221188
  183.8 386.5 %copy-start.11 = (bf16[3,1,16,768]{3,2,1,0:T(8,128)(2,1)S(1)}, bf16[3,1,16,768]{3,2,1,0:T(8,128)(2,1)}, u32[]{:S(2)}) copy-start(bf16[3,1,16,768]{3,2,1,0:T(8,128)(2,1)} %copy-done.10) | copy-start | bytes 221188
  515.6 71.4 %collective-permute-start.6 = (f32[56,192]{1,0:T(8,128)S(1)}, f32[56,192]{1,0:T(8,128)S(1)}, u32[]{:S(2)}, u32[]{:S(2)}) collective-permute-start(f32[56,192]{1,0:T(8,128)S(1)} %fusion), channel_id=1, source_target_pairs={{0,1},{1,2},{2,3},{3,4},{4,5},{5,6},{6,7},{7,8},{8,9},{9,10},{10,1... | collective-permute-start | bytes 129032
  519.8 67.2 %collective-permute-start.7 = (f32[56,192]{1,0:T(8,128)S(1)}, f32[56,192]{1,0:T(8,128)}, u32[]{:S(2)}, u32[]{:S(2)}) collective-permute-start(f32[56,192]{1,0:T(8,128)S(1)} %fusion), channel_id=1, source_target_pairs={{0,2},{1,3},{2,4},{3,5},{4,6},{5,7},{6,8},{7,9},{8,10},{9,11},{10,... | collective-permute-start | bytes 129032
  534.5 52.5 %collective-permute-start.8 = (f32[56,192]{1,0:T(8,128)S(1)}, f32[56,192]{1,0:T(8,128)}, u32[]{:S(2)}, u32[]{:S(2)}) collective-permute-start(f32[56,192]{1,0:T(8,128)S(1)} %fusion), channel_id=1, source_target_pairs={{0,3},{1,4},{2,5},{3,6},{4,7},{5,8},{6,9},{7,10},{8,11},{9,12},{10... | collective-permute-start | bytes 129032
  558.4 28.6 %collective-permute-start.9 = (f32[22,192]{1,0:T(8,128)}, f32[22,192]{1,0:T(8,128)}, u32[]{:S(2)}, u32[]{:S(2)}) collective-permute-start(f32[22,192]{1,0:T(8,128)} %slice.318), channel_id=1, source_target_pairs={{0,4},{1,5},{2,6},{3,7},{4,8},{5,9},{6,10},{7,11},{8,12},{9,13},{1... | collective-permute-start | bytes 50696
  627.6 122.7 %copy-start = (bf16[96,54,192]{2,1,0:T(8,128)(2,1)S(1)}, bf16[96,54,192]{2,1,0:T(8,128)(2,1)}, u32[]{:S(2)}) copy-start(bf16[96,54,192]{2,1,0:T(8,128)(2,1)} %all-gather.3.cloned.1.call-done) | copy-start | bytes 5971972
  749.5 3.5 copy-start.14
  749.5 3.5 copy-start.15
  750.3 2.6 copy-start.13
  758.3 1.0 copy-start.3
Sparse Core Ops, SparseCore 0:
  15.6 183.5 all-gather.2
where the time goes:
time: 771 us; the launch traced here: 768 us
  blocking collectives  595 us (77%)
  starting transfers between devices  70.9 us (9%)
  local copies, waits for them, and re-layouts  47.4 us (6%)
  other arithmetic  17.1 us (2%)
  matrix products  16.2 us (2%)
  between operations  15.2 us (2%)
    unnamed x1, blocking collectives  332 us
    psum x1, blocking collectives, per_device(): lax.psum((jnp.sum(video_f, axis=(0, 1, 2)), jnp.sum(video_f * video_f, ax...  120 us
    psum x1, blocking collectives, per_device(): lax.psum((gain_part, shift_part, bias_part), ('tm', 'rows', 'cols'))  118 us
    unnamed x4, starting transfers between devices  54.1 us
    psum x1, blocking collectives, per_device(): grad_weight = lax.psum(band_sum, 'tm')  24.2 us
  transfers between devices with their start and end apart: 11, of which 3 were waited for; matrix products, arithmetic and copies ran while one was open for 50% of the time, Pallas kernels for 0%

commit v1 on v0

--- a/solution.py
+++ b/solution.py
@@ -20,6 +20,47 @@
     return block
 
 
+def xor_sum(x, axis):
+    n = lax.axis_size(axis)
+    step = 1
+    while step < n:
+        x = x + lax.ppermute(x, axis, [(i, i ^ step) for i in range(n)])
+        step *= 2
+    return x
+
+
+def six_sum(x, axis):
+    n = lax.axis_size(axis)
+    x = x + lax.ppermute(x, axis, [(i, i ^ 1) for i in range(n)])
+    here = lax.axis_index(axis) // 2
+    ahead = lax.ppermute(x, axis, [(i, (i + 2) % n) for i in range(n)])
+    behind = lax.ppermute(x, axis, [(i, (i + 4) % n) for i in range(n)])
+    first = jnp.where(here == 0, x, jnp.where(here == 1, ahead, behind))
+    second = jnp.where(here == 1, x, jnp.where(here == 2, ahead, behind))
+    third = jnp.where(here == 2, x, jnp.where(here == 0, ahead, behind))
+    return (first + second) + third
+
+
+def all_sum(x):
+    return xor_sum(six_sum(xor_sum(x, "cols"), "rows"), "tm")
+
+
+def halve_scatter(q, axis, dim):
+    n = lax.axis_size(axis)
+    bits = n.bit_length() - 1
+    here = lax.axis_index(axis)
+    shape = q.shape
+    q = q.reshape(shape[:dim] + (2,) * bits + shape[dim + 1 :])
+    for level in range(bits):
+        step = 1 << level
+        at = dim + bits - 1 - level
+        bit = (here // step) % 2
+        keep = lax.dynamic_index_in_dim(q, bit, axis=at, keepdims=False)
+        send = lax.dynamic_index_in_dim(q, 1 - bit, axis=at, keepdims=False)
+        q = keep + lax.ppermute(send, axis, [(i, i ^ step) for i in range(n)])
+    return q.reshape(shape[:dim] + (1,) + shape[dim + 1 :])
+
+
 def per_group(values):
     return jnp.repeat(values.reshape(GROUPS, -1).sum(axis=1), CH // GROUPS)
 
@@ -53,9 +94,8 @@
     )
     grad_ext = from_pairs(framed[1:, :, :, 2 * channels :], local_rows, local_cols, channels)
     video_f = video.astype(jnp.float32)
-    sums, squares = lax.psum(
-        (jnp.sum(video_f, axis=(0, 1, 2)), jnp.sum(video_f * video_f, axis=(0, 1, 2))),
-        ("tm", "rows", "cols"),
+    sums, squares = all_sum(
+        jnp.stack([jnp.sum(video_f, axis=(0, 1, 2)), jnp.sum(video_f * video_f, axis=(0, 1, 2))])
     )
     devices_all = lax.axis_size("tm") * lax.axis_size("rows") * lax.axis_size("cols")
     count = float(local_frames * local_rows * local_cols * devices_all * (channels // GROUPS))
@@ -129,11 +169,13 @@
     gain_part = jnp.sum(grad_pre * normed, axis=(0, 1, 2))
     shift_part = jnp.sum(grad_pre, axis=(0, 1, 2))
     bias_part = jnp.sum(grad_f, axis=(0, 1, 2))
-    grad_gain, grad_shift, grad_conv_bias = lax.psum(
-        (gain_part, shift_part, bias_part), ("tm", "rows", "cols")
-    )
-    band_sum = lax.psum_scatter(kernel_grad, ("rows", "cols"), scatter_dimension=0, tiled=True)
-    grad_weight = lax.psum(band_sum, "tm")
+    grad_gain, grad_shift, grad_conv_bias = all_sum(jnp.stack([gain_part, shift_part, bias_part]))
+    row_count = lax.axis_size("rows")
+    col_count = lax.axis_size("cols")
+    band = kernel_grad.reshape(row_count, col_count, -1, channels)
+    band = halve_scatter(band, "cols", 1)
+    band = lax.psum_scatter(band, "rows", scatter_dimension=0, tiled=True)
+    grad_weight = xor_sum(band.reshape(-1, channels), "tm")
     term_a = per_group(gain * grad_shift) / count
     term_b = per_group(gain * grad_gain) / count
     grad_video = (grad_f + rstd_c * (grad_pre * gain - term_a - normed * term_b)).astype(

time: 771 us -> 412 us (0.53)
  the two profiles are of different devices: /device:TPU:1 before, /device:TPU:32 now
where the time goes in v1:
time: 412 us; the launch traced here: 409 us
  waiting for transfers between devices  170 us (41%)
  starting transfers between devices  119 us (29%)
  local copies, waits for them, and re-layouts  66 us (16%)
  other arithmetic  24.5 us (6%)
  between operations  16.5 us (4%)
  matrix products  13.1 us (3%)
    ppermute x17, waiting for transfers between devices, xor_sum(): x = x + lax.ppermute(x, axis, [(i, i ^ step) for i in range(n)])  62.1 us
    ppermute x17, starting transfers between devices, xor_sum(): x = x + lax.ppermute(x, axis, [(i, i ^ step) for i in range(n)])  57.1 us
    reduce_scatter x1, waiting for transfers between devices, per_device(): band = lax.psum_scatter(band, 'rows', scatter_dimension=0, tiled=True)  42.8 us
    ppermute x4, waiting for transfers between devices, halve_scatter(): q = keep + lax.ppermute(send, axis, [(i, i ^ step) for i in range(n)])  37.9 us
    ppermute x4, starting transfers between devices, halve_scatter(): q = keep + lax.ppermute(send, axis, [(i, i ^ step) for i in range(n)])  19.7 us
    ppermute x2, starting transfers between devices, six_sum(): behind = lax.ppermute(x, axis, [(i, (i + 4) % n) for i in range(n)])  12.1 us
    all_gather x1, waiting for transfers between devices, per_device(): whole = lax.all_gather(weight, ('rows', 'cols'), axis=0, tiled=True)  10.7 us
    concatenate x1, local copies, waits for them, and re-layouts, per_device(): jnp.concatenate(grad_windows, axis=-1).reshape(cells, 27 * channels)  10.1 us
  transfers between devices with their start and end apart: 35, of which 24 were waited for; matrix products, arithmetic and copies ran while one was open for 20% of the time, Pallas kernels for 0%

profile of v1, /device:TPU:32, one launch (start us, length us, event | category | flops | bytes accessed | tf_op | source)
XLA Modules:
  0.0 408.8 jit_solution(10585794284775516858)
XLA Ops:
  18.0 4.9 %collective-permute-start.8 = (f32[2,192]{1,0:T(2,128)S(1)}, f32[2,192]{1,0:T(2,128)S(1)}, u32[]{:S(2)}, u32[]{:S(2)}) collective-permute-start(f32[2,192]{1,0:T(2,128)S(1)} %fusion.23), channel_id=1, source_target_pairs={{0,4},{1,5},{2,6},{3,7},{4,0},{5,1},{6,2},{7,3},{8,12},{9,13},{10,... | collective-permute-start | bytes 4616 | tf_op jit(solution)/shard_map/ppermute | solution.py:27
  25.6 4.5 %collective-permute-start.1 = (bf16[1,16,16,768]{3,2,1,0:T(8,128)(2,1)S(1)}, bf16[1,16,16,768]{3,2,1,0:T(8,128)(2,1)S(1)}, u32[]{:S(2)}, u32[]{:S(2)}) collective-permute-start(bf16[1,16,16,768]{3,2,1,0:T(8,128)(2,1)S(1)} %constant_dynamic-update-slice_fusion), channel_id=1, source_target_pairs={{96,0},{192,96},{288,192},{384,288},{480,384},{576,480},{672,576},... | collective-permute-start | bytes 1179656 | tf_op jit(solution)/shard_map/ppermute | solution.py:18
  30.2 15.1 %collective-permute-start.9 = (f32[2,192]{1,0:T(2,128)S(1)}, f32[2,192]{1,0:T(2,128)S(1)}, u32[]{:S(2)}, u32[]{:S(2)}) collective-permute-start(f32[2,192]{1,0:T(2,128)S(1)} %add.177), channel_id=1, source_target_pairs={{0,8},{1,9},{2,10},{3,11},{4,12},{5,13},{6,14},{7,15},{8,0},{9,1},... | collective-permute-start | bytes 4616 | tf_op jit(solution)/shard_map/ppermute | solution.py:27
  56.1 6.0 %collective-permute-start.12 = (f32[2,192]{1,0:T(2,128)S(1)}, f32[2,192]{1,0:T(2,128)S(1)}, u32[]{:S(2)}, u32[]{:S(2)}) collective-permute-start(f32[2,192]{1,0:T(2,128)S(1)} %add.179), channel_id=1, source_target_pairs={{0,64},{16,80},{32,0},{48,16},{64,32},{80,48},{1,65},{17,81},{33,1... | collective-permute-start | bytes 4616 | tf_op jit(solution)/shard_map/ppermute | solution.py:37
  70.8 4.4 %collective-permute-done.14 = f32[2,192]{1,0:T(2,128)S(1)} collective-permute-done((f32[2,192]{1,0:T(2,128)S(1)}, f32[2,192]{1,0:T(2,128)S(1)}, u32[]{:S(2)}, u32[]{:S(2)}) %collective-permute-start.14) | collective-permute-done | bytes 1568 | tf_op jit(solution)/shard_map/ppermute | solution.py:27
  77.3 7.4 %collective-permute-done.15 = f32[2,192]{1,0:T(2,128)S(1)} collective-permute-done((f32[2,192]{1,0:T(2,128)S(1)}, f32[2,192]{1,0:T(2,128)S(1)}, u32[]{:S(2)}, u32[]{:S(2)}) %collective-permute-start.15) | collective-permute-done | bytes 1568 | tf_op jit(solution)/shard_map/ppermute | solution.py:27
  90.5 5.2 %collective-permute-done.3 = bf16[3,1,16,768]{3,2,1,0:T(8,128)(2,1)S(1)} collective-permute-done((bf16[3,1,16,768]{3,2,1,0:T(8,128)(2,1)S(1)}, bf16[3,1,16,768]{3,2,1,0:T(8,128)(2,1)S(1)}, u32[]{:S(2)}, u32[]{:S(2)}) %collective-permute-start.3) | collective-permute-done | bytes 73760 | tf_op jit(solution)/shard_map/ppermute | solution.py:18
  101.4 4.3 %fusion.2 = bf16[2,36,18,192]{3,2,1,0:T(8,128)(2,1)S(1)} fusion(bf16[3,18,1,768]{3,2,1,0:T(2,128)(2,1)S(1)} %collective-permute-done.5, bf16[3,18,1,768]{3,2,1,0:T(2,128)(2,1)S(1)} %collective-permute-done.4, bf16[3,1,16,768]{3,2,1,0:T(8,128)(2,1)S(1)} %collective-permute-done.3, bf16[3,1,16,768]{3,2,1,0:T(8,128)(2,1)S(1)} %collective-permute-done.2, ...), kind=kLoop, calls=%fused_computation.24 | loop fusion | flops 6967296 | bytes 1990656 | tf_op jit(solution)/shard_map/concatenate
  111.3 9.7 %concatenate.29 = bf16[2,16,16,5184]{3,2,1,0:T(8,128)(2,1)} concatenate(bf16[2,16,16,192]{3,2,1,0:T(8,128)(2,1)} %get-tuple-element.73, bf16[2,16,16,192]{3,2,1,0:T(8,128)(2,1)} %get-tuple-element.72, bf16[2,16,16,192]{3,2,1,0:T(8,128)(2,1)} %get-tuple-element.71, bf16[2,16,16,192]{3,2,1,0:T(8,128)(2,1)} %get-tuple-element.70, bf16[2,16,16,192]{3,2,1,0:T(8,128)(2,1)} %get-tuple-element.69, ...), dimensions={3} | concatenate | bytes 10616832 | tf_op jit(solution)/shard_map/concatenate | solution.py:146
  121.0 8.1 %copy.46 = bf16[512,5184]{0,1:T(8,128)(2,1)} copy(bf16[512,5184]{1,0:T(8,128)(2,1)} %bitcast.59) | data formatting | bytes 10616832 | tf_op jit(solution)/shard_map/reshape | solution.py:146
  129.0 7.6 %dot_general.16 = bf16[6,2,2,2,2,54,512]{6,5,4,3,2,1,0:T(8,128)(2,1)} reshape(bf16[5184,512]{1,0:T(8,128)(2,1)} %bitcast.62) | data formatting | bytes 10616832 | tf_op jit(solution)/shard_map/dot_general | solution.py:153
  136.7 4.2 %fusion.15 = f32[6,2,2,2,2,54,192]{6,5,4,3,2,1,0:T(8,128)S(1)} fusion(bf16[6,2,2,2,2,54,512]{6,5,4,3,2,1,0:T(8,128)(2,1)} %dot_general.16, bf16[512,192,1,1,1,1,1]{1,0,6,5,4,3,2:T(8,128)(2,1)S(1)} %bitcast.66), kind=kOutput, calls=%fused_computation.88 | convolution fusion | flops 1019215872 | bytes 9486336 | tf_op jit(solution)/shard_map/dot_general | solution.py:153
  144.9 6.5 %collective-permute-start.26 = (f32[6,2,2,2,54,192]{5,3,4,2,1,0:T(2,128)S(1)}, f32[6,2,2,2,54,192]{5,3,4,2,1,0:T(2,128)}, u32[]{:S(2)}, u32[]{:S(2)}) collective-permute-start(f32[6,2,2,2,54,192]{5,3,4,2,1,0:T(2,128)S(1)} %copy.48), channel_id=1, source_target_pairs={{0,1},{1,0},{2,3},{3,2},{4,5},{5,4},{6,7},{7,6},{8,9},{9,8},{10,11... | collective-permute-start | bytes 5971976 | tf_op jit(solution)/shard_map/ppermute | solution.py:60
  151.4 4.5 %collective-permute-done.26 = f32[6,2,2,2,54,192]{5,3,4,2,1,0:T(2,128)} collective-permute-done((f32[6,2,2,2,54,192]{5,3,4,2,1,0:T(2,128)S(1)}, f32[6,2,2,2,54,192]{5,3,4,2,1,0:T(2,128)}, u32[]{:S(2)}, u32[]{:S(2)}) %collective-permute-start.26) | collective-permute-done | bytes 1990688 | tf_op jit(solution)/shard_map/ppermute | solution.py:60
  168.4 10.1 %concatenate.31 = bf16[2,16,16,5184]{3,2,1,0:T(8,128)(2,1)} concatenate(bf16[2,16,16,192]{3,2,1,0:T(8,128)(2,1)} %get-tuple-element.46, bf16[2,16,16,192]{3,2,1,0:T(8,128)(2,1)} %get-tuple-element.45, bf16[2,16,16,192]{3,2,1,0:T(8,128)(2,1)} %get-tuple-element.44, bf16[2,16,16,192]{3,2,1,0:T(8,128)(2,1)} %get-tuple-element.43, bf16[2,16,16,192]{3,2,1,0:T(8,128)(2,1)} %get-tuple-element.42, ...), dimensions={3} | concatenate | bytes 10616832 | tf_op jit(solution)/shard_map/concatenate | solution.py:147
  178.5 17.9 %collective-permute-done.27 = f32[6,2,2,54,192]{4,2,3,1,0:T(2,128)} collective-permute-done((f32[6,2,2,54,192]{4,2,3,1,0:T(2,128)}, f32[6,2,2,54,192]{4,2,3,1,0:T(2,128)}, u32[]{:S(2)}, u32[]{:S(2)}) %collective-permute-start.27) | collective-permute-done | bytes 995360 | tf_op jit(solution)/shard_map/ppermute | solution.py:60
  199.0 10.7 %all-gather.3.cloned.1.call-done = bf16[96,54,192]{2,1,0:T(8,128)(2,1)} async-done(((bf16[1,54,192]{2,1,0:T(8,128)(2,1)}), bf16[96,54,192]{2,1,0:T(8,128)(2,1)}) %all-gather.3.cloned.1.call-update) | async-done | bytes 1990672 | tf_op jit(solution)/shard_map/all_gather | solution.py:125
  209.7 5.3 %reshape.212 = bf16[27,192,192]{2,1,0:T(8,128)(2,1)} reshape(bf16[96,54,192]{2,1,0:T(8,128)(2,1)} %all-gather.3.cloned.1.call-done) | data formatting | bytes 3981312 | tf_op jit(solution)/shard_map/reshape | solution.py:157
  215.0 3.8 copy.44
  218.8 4.4 %convolution_convert_fusion = bf16[512,192]{0,1:T(8,128)(2,1)S(1)} fusion(bf16[512,5184]{1,0:T(8,128)(2,1)} %bitcast.61, bf16[5184,192]{1,0:T(8,128)(2,1)S(1)} %bitcast.63), kind=kOutput, calls=%fused_computation.9 | convolution fusion | flops 1019314176 | bytes 7495680 | tf_op jit(solution)/shard_map/dot_general | solution.py:159
  228.7 9.4 %collective-permute-start.28 = (f32[6,2,54,192]{3,1,2,0:T(2,128)}, f32[6,2,54,192]{3,1,2,0:T(2,128)}, u32[]{:S(2)}, u32[]{:S(2)}) collective-permute-start(f32[6,2,54,192]{3,1,2,0:T(2,128)} %copy.52), channel_id=1, source_target_pairs={{0,4},{1,5},{2,6},{3,7},{4,0},{5,1},{6,2},{7,3},{8,12},{9,13},{10,... | collective-permute-start | bytes 1493000 | tf_op jit(solution)/shard_map/ppermute | solution.py:60
  241.1 13.6 %collective-permute-done.17 = f32[3,192]{1,0:T(4,128)S(1)} collective-permute-done((f32[3,192]{1,0:T(4,128)S(1)}, f32[3,192]{1,0:T(4,128)S(1)}, u32[]{:S(2)}, u32[]{:S(2)}) %collective-permute-start.17) | collective-permute-done | bytes 2336 | tf_op jit(solution)/shard_map/ppermute | solution.py:27
  257.6 4.2 %collective-permute-done.18 = f32[3,192]{1,0:T(4,128)S(1)} collective-permute-done((f32[3,192]{1,0:T(4,128)S(1)}, f32[3,192]{1,0:T(4,128)S(1)}, u32[]{:S(2)}, u32[]{:S(2)}) %collective-permute-start.18) | collective-permute-done | bytes 2336 | tf_op jit(solution)/shard_map/ppermute | solution.py:27
  263.7 9.9 %collective-permute-done.19 = f32[3,192]{1,0:T(4,128)S(1)} collective-permute-done((f32[3,192]{1,0:T(4,128)S(1)}, f32[3,192]{1,0:T(4,128)S(1)}, u32[]{:S(2)}, u32[]{:S(2)}) %collective-permute-start.19) | collective-permute-done | bytes 2336 | tf_op jit(solution)/shard_map/ppermute | solution.py:27
  279.1 5.5 %collective-permute-start.21 = (f32[3,192]{1,0:T(4,128)S(1)}, f32[3,192]{1,0:T(4,128)S(1)}, u32[]{:S(2)}, u32[]{:S(2)}) collective-permute-start(f32[3,192]{1,0:T(4,128)S(1)} %add.199), channel_id=1, source_target_pairs={{0,32},{16,48},{32,64},{48,80},{64,0},{80,16},{1,33},{17,49},{33,6... | collective-permute-start | bytes 6920 | tf_op jit(solution)/shard_map/ppermute | solution.py:36
  284.6 6.1 %collective-permute-start.22 = (f32[3,192]{1,0:T(4,128)S(1)}, f32[3,192]{1,0:T(4,128)S(1)}, u32[]{:S(2)}, u32[]{:S(2)}) collective-permute-start(f32[3,192]{1,0:T(4,128)S(1)} %add.199), channel_id=1, source_target_pairs={{0,64},{16,80},{32,0},{48,16},{64,32},{80,48},{1,65},{17,81},{33,1... | collective-permute-start | bytes 6920 | tf_op jit(solution)/shard_map/ppermute | solution.py:37
  304.6 4.5 %convolution_add_fusion = f32[512,192]{0,1:T(8,128)S(1)} fusion(bf16[512,5184]{1,0:T(8,128)(2,1)} %bitcast.60, bf16[5184,192]{1,0:T(8,128)(2,1)S(1)} %copy-done.2, f32[192]{0:T(256)S(1)} %copy-done.14), kind=kOutput, calls=%fused_computation.8 | convolution fusion | flops 1019314176 | bytes 7693056 | tf_op jit(solution)/shard_map/dot_general | solution.py:148
  309.3 5.1 %collective-permute-start.25 = (f32[3,192]{1,0:T(4,128)S(1)}, f32[3,192]{1,0:T(4,128)S(1)}, u32[]{:S(2)}, u32[]{:S(2)}) collective-permute-start(f32[3,192]{1,0:T(4,128)S(1)} %add.203), channel_id=1, source_target_pairs={{0,384},{96,480},{192,576},{288,672},{384,0},{480,96},{576,192},{6... | collective-permute-start | bytes 6920 | tf_op jit(solution)/shard_map/ppermute | solution.py:27
  314.4 15.5 %collective-permute-done.29 = f32[6,54,192]{2,1,0:T(8,128)S(1)} collective-permute-done((f32[6,54,192]{2,1,0:T(8,128)}, f32[6,54,192]{2,1,0:T(8,128)S(1)}, u32[]{:S(2)}, u32[]{:S(2)}) %collective-permute-start.29) | collective-permute-done | bytes 248864 | tf_op jit(solution)/shard_map/ppermute | solution.py:60
  332.3 42.8 %reduce-scatter.2.cloned.1.call-done = f32[1,1,54,192]{3,2,1,0:T(8,128)} async-done(((f32[6,1,54,192]{3,2,1,0:T(8,128)}), f32[1,1,54,192]{3,2,1,0:T(8,128)}) %reduce-scatter.2.cloned.1.call-update) | async-done | bytes 41488 | tf_op jit(solution)/shard_map/reduce_scatter | solution.py:177
  385.1 5.2 %collective-permute-done.31 = f32[54,192]{1,0:T(8,128)S(1)} collective-permute-done((f32[54,192]{1,0:T(8,128)S(1)}, f32[54,192]{1,0:T(8,128)S(1)}, u32[]{:S(2)}, u32[]{:S(2)}) %collective-permute-start.31) | collective-permute-done | bytes 41504 | tf_op jit(solution)/shard_map/ppermute | solution.py:27
  394.3 6.4 %collective-permute-done.32 = f32[54,192]{1,0:T(8,128)S(1)} collective-permute-done((f32[54,192]{1,0:T(8,128)S(1)}, f32[54,192]{1,0:T(8,128)S(1)}, u32[]{:S(2)}, u32[]{:S(2)}) %collective-permute-start.32) | collective-permute-done | bytes 41504 | tf_op jit(solution)/shard_map/ppermute | solution.py:27
  (172 shorter events, 119.4 us)
Async XLA Ops:
  8.0 201.7 %all-gather.3.cloned.1.call-start = ((), (), s32[]{:S(2)}) async-start(), calls=%async_computation.2 | async-start | bytes 2781184 | tf_op jit(solution)/shard_map/all_gather | solution.py:125
  12.5 5.5 %collective-permute-start.7 = (f32[2,192]{1,0:T(2,128)S(1)}, f32[2,192]{1,0:T(2,128)S(1)}, u32[]{:S(2)}, u32[]{:S(2)}) collective-permute-start(f32[2,192]{1,0:T(2,128)S(1)} %fusion.7), channel_id=1, source_target_pairs={{0,2},{1,3},{2,0},{3,1},{4,6},{5,7},{6,4},{7,5},{8,10},{9,11},{10,... | collective-permute-start | bytes 4616 | tf_op jit(solution)/shard_map/ppermute | solution.py:27
  18.0 12.1 %collective-permute-start.8 = (f32[2,192]{1,0:T(2,128)S(1)}, f32[2,192]{1,0:T(2,128)S(1)}, u32[]{:S(2)}, u32[]{:S(2)}) collective-permute-start(f32[2,192]{1,0:T(2,128)S(1)} %fusion.23), channel_id=1, source_target_pairs={{0,4},{1,5},{2,6},{3,7},{4,0},{5,1},{6,2},{7,3},{8,12},{9,13},{10,... | collective-permute-start | bytes 4616 | tf_op jit(solution)/shard_map/ppermute | solution.py:27
  23.0 62.1 %collective-permute-start = (bf16[1,16,16,768]{3,2,1,0:T(8,128)(2,1)S(1)}, bf16[1,16,16,768]{3,2,1,0:T(8,128)(2,1)S(1)}, u32[]{:S(2)}, u32[]{:S(2)}) collective-permute-start(bf16[1,16,16,768]{3,2,1,0:T(8,128)(2,1)S(1)} %constant_dynamic-update-slice_fusion), channel_id=1, source_target_pairs={{0,96},{96,192},{192,288},{288,384},{384,480},{480,576},{576,672},... | collective-permute-start | bytes 1179656 | tf_op jit(solution)/shard_map/ppermute | solution.py:15
  25.6 59.5 %collective-permute-start.1 = (bf16[1,16,16,768]{3,2,1,0:T(8,128)(2,1)S(1)}, bf16[1,16,16,768]{3,2,1,0:T(8,128)(2,1)S(1)}, u32[]{:S(2)}, u32[]{:S(2)}) collective-permute-start(bf16[1,16,16,768]{3,2,1,0:T(8,128)(2,1)S(1)} %constant_dynamic-update-slice_fusion), channel_id=1, source_target_pairs={{96,0},{192,96},{288,192},{384,288},{480,384},{576,480},{672,576},... | collective-permute-start | bytes 1179656 | tf_op jit(solution)/shard_map/ppermute | solution.py:18
  30.1 344.9 %reduce-scatter.2.cloned.1.call-start = ((), (), s32[]{:S(2)}) async-start(), calls=%async_computation.1 | async-start | bytes 401408 | tf_op jit(solution)/shard_map/reduce_scatter | solution.py:177
  30.2 16.7 %collective-permute-start.9 = (f32[2,192]{1,0:T(2,128)S(1)}, f32[2,192]{1,0:T(2,128)S(1)}, u32[]{:S(2)}, u32[]{:S(2)}) collective-permute-start(f32[2,192]{1,0:T(2,128)S(1)} %add.177), channel_id=1, source_target_pairs={{0,8},{1,9},{2,10},{3,11},{4,12},{5,13},{6,14},{7,15},{8,0},{9,1},... | collective-permute-start | bytes 4616 | tf_op jit(solution)/shard_map/ppermute | solution.py:27
  46.9 5.5 %collective-permute-start.10 = (f32[2,192]{1,0:T(2,128)S(1)}, f32[2,192]{1,0:T(2,128)S(1)}, u32[]{:S(2)}, u32[]{:S(2)}) collective-permute-start(f32[2,192]{1,0:T(2,128)S(1)} %add.178), channel_id=1, source_target_pairs={{0,16},{16,0},{32,48},{48,32},{64,80},{80,64},{1,17},{17,1},{33,49... | collective-permute-start | bytes 4616 | tf_op jit(solution)/shard_map/ppermute | solution.py:34
  52.3 9.8 %collective-permute-start.11 = (f32[2,192]{1,0:T(2,128)S(1)}, f32[2,192]{1,0:T(2,128)S(1)}, u32[]{:S(2)}, u32[]{:S(2)}) collective-permute-start(f32[2,192]{1,0:T(2,128)S(1)} %add.179), channel_id=1, source_target_pairs={{0,32},{16,48},{32,64},{48,80},{64,0},{80,16},{1,33},{17,49},{33,6... | collective-permute-start | bytes 4616 | tf_op jit(solution)/shard_map/ppermute | solution.py:36
  56.1 7.3 %collective-permute-start.12 = (f32[2,192]{1,0:T(2,128)S(1)}, f32[2,192]{1,0:T(2,128)S(1)}, u32[]{:S(2)}, u32[]{:S(2)}) collective-permute-start(f32[2,192]{1,0:T(2,128)S(1)} %add.179), channel_id=1, source_target_pairs={{0,64},{16,80},{32,0},{48,16},{64,32},{80,48},{1,65},{17,81},{33,1... | collective-permute-start | bytes 4616 | tf_op jit(solution)/shard_map/ppermute | solution.py:37
  63.4 5.5 %collective-permute-start.13 = (f32[2,192]{1,0:T(2,128)S(1)}, f32[2,192]{1,0:T(2,128)S(1)}, u32[]{:S(2)}, u32[]{:S(2)}) collective-permute-start(f32[2,192]{1,0:T(2,128)S(1)} %select_add_fusion.1), channel_id=1, source_target_pairs={{0,96},{96,0},{192,288},{288,192},{384,480},{480,384},{576,672},{6... | collective-permute-start | bytes 4616 | tf_op jit(solution)/shard_map/ppermute | solution.py:27
  68.9 6.4 %collective-permute-start.14 = (f32[2,192]{1,0:T(2,128)S(1)}, f32[2,192]{1,0:T(2,128)S(1)}, u32[]{:S(2)}, u32[]{:S(2)}) collective-permute-start(f32[2,192]{1,0:T(2,128)S(1)} %add.182), channel_id=1, source_target_pairs={{0,192},{96,288},{192,0},{288,96},{384,576},{480,672},{576,384},{6... | collective-permute-start | bytes 4616 | tf_op jit(solution)/shard_map/ppermute | solution.py:27
  75.2 9.4 %collective-permute-start.15 = (f32[2,192]{1,0:T(2,128)S(1)}, f32[2,192]{1,0:T(2,128)S(1)}, u32[]{:S(2)}, u32[]{:S(2)}) collective-permute-start(f32[2,192]{1,0:T(2,128)S(1)} %add.183), channel_id=1, source_target_pairs={{0,384},{96,480},{192,576},{288,672},{384,0},{480,96},{576,192},{6... | collective-permute-start | bytes 4616 | tf_op jit(solution)/shard_map/ppermute | solution.py:27
  85.1 5.4 %collective-permute-start.2 = (bf16[3,1,16,768]{3,2,1,0:T(8,128)(2,1)S(1)}, bf16[3,1,16,768]{3,2,1,0:T(8,128)(2,1)S(1)}, u32[]{:S(2)}, u32[]{:S(2)}) collective-permute-start(bf16[3,1,16,768]{3,2,1,0:T(8,128)(2,1)S(1)} %get-tuple-element.15), channel_id=1, source_target_pairs={{0,16},{16,32},{32,48},{48,64},{64,80},{1,17},{17,33},{33,49},{49,... | collective-permute-start | bytes 221192 | tf_op jit(solution)/shard_map/ppermute | solution.py:15
  88.5 7.2 %collective-permute-start.3 = (bf16[3,1,16,768]{3,2,1,0:T(8,128)(2,1)S(1)}, bf16[3,1,16,768]{3,2,1,0:T(8,128)(2,1)S(1)}, u32[]{:S(2)}, u32[]{:S(2)}) collective-permute-start(bf16[3,1,16,768]{3,2,1,0:T(8,128)(2,1)S(1)} %get-tuple-element.16), channel_id=1, source_target_pairs={{16,0},{32,16},{48,32},{64,48},{80,64},{17,1},{33,17},{49,33},{65,... | collective-permute-start | bytes 221192 | tf_op jit(solution)/shard_map/ppermute | solution.py:18
  144.9 11.0 %collective-permute-start.26 = (f32[6,2,2,2,54,192]{5,3,4,2,1,0:T(2,128)S(1)}, f32[6,2,2,2,54,192]{5,3,4,2,1,0:T(2,128)}, u32[]{:S(2)}, u32[]{:S(2)}) collective-permute-start(f32[6,2,2,2,54,192]{5,3,4,2,1,0:T(2,128)S(1)} %copy.48), channel_id=1, source_target_pairs={{0,1},{1,0},{2,3},{3,2},{4,5},{5,4},{6,7},{7,6},{8,9},{9,8},{10,11... | collective-permute-start | bytes 5971976 | tf_op jit(solution)/shard_map/ppermute | solution.py:60
  160.9 35.5 %collective-permute-start.27 = (f32[6,2,2,54,192]{4,2,3,1,0:T(2,128)}, f32[6,2,2,54,192]{4,2,3,1,0:T(2,128)}, u32[]{:S(2)}, u32[]{:S(2)}) collective-permute-start(f32[6,2,2,54,192]{4,2,3,1,0:T(2,128)} %copy.50), channel_id=1, source_target_pairs={{0,2},{1,3},{2,0},{3,1},{4,6},{5,7},{6,4},{7,5},{8,10},{9,11},{10,... | collective-permute-start | bytes 2985992 | tf_op jit(solution)/shard_map/ppermute | solution.py:60
  225.3 12.8 %collective-permute-start.16 = (f32[3,192]{1,0:T(4,128)S(1)}, f32[3,192]{1,0:T(4,128)S(1)}, u32[]{:S(2)}, u32[]{:S(2)}) collective-permute-start(f32[3,192]{1,0:T(4,128)S(1)} %pad_maximum_fusion.32), channel_id=1, source_target_pairs={{0,1},{1,0},{2,3},{3,2},{4,5},{5,4},{6,7},{7,6},{8,9},{9,8},{10,11... | collective-permute-start | bytes 6920 | tf_op jit(solution)/shard_map/ppermute | solution.py:27
  228.7 71.8 %collective-permute-start.28 = (f32[6,2,54,192]{3,1,2,0:T(2,128)}, f32[6,2,54,192]{3,1,2,0:T(2,128)}, u32[]{:S(2)}, u32[]{:S(2)}) collective-permute-start(f32[6,2,54,192]{3,1,2,0:T(2,128)} %copy.52), channel_id=1, source_target_pairs={{0,4},{1,5},{2,6},{3,7},{4,0},{5,1},{6,2},{7,3},{8,12},{9,13},{10,... | collective-permute-start | bytes 1493000 | tf_op jit(solution)/shard_map/ppermute | solution.py:60
  238.1 16.6 %collective-permute-start.17 = (f32[3,192]{1,0:T(4,128)S(1)}, f32[3,192]{1,0:T(4,128)S(1)}, u32[]{:S(2)}, u32[]{:S(2)}) collective-permute-start(f32[3,192]{1,0:T(4,128)S(1)} %fusion.8), channel_id=1, source_target_pairs={{0,2},{1,3},{2,0},{3,1},{4,6},{5,7},{6,4},{7,5},{8,10},{9,11},{10,... | collective-permute-start | bytes 6920 | tf_op jit(solution)/shard_map/ppermute | solution.py:27
  254.7 7.0 %collective-permute-start.18 = (f32[3,192]{1,0:T(4,128)S(1)}, f32[3,192]{1,0:T(4,128)S(1)}, u32[]{:S(2)}, u32[]{:S(2)}) collective-permute-start(f32[3,192]{1,0:T(4,128)S(1)} %fusion.22), channel_id=1, source_target_pairs={{0,4},{1,5},{2,6},{3,7},{4,0},{5,1},{6,2},{7,3},{8,12},{9,13},{10,... | collective-permute-start | bytes 6920 | tf_op jit(solution)/shard_map/ppermute | solution.py:27
  261.8 11.8 %collective-permute-start.19 = (f32[3,192]{1,0:T(4,128)S(1)}, f32[3,192]{1,0:T(4,128)S(1)}, u32[]{:S(2)}, u32[]{:S(2)}) collective-permute-start(f32[3,192]{1,0:T(4,128)S(1)} %add.197), channel_id=1, source_target_pairs={{0,8},{1,9},{2,10},{3,11},{4,12},{5,13},{6,14},{7,15},{8,0},{9,1},... | collective-permute-start | bytes 6920 | tf_op jit(solution)/shard_map/ppermute | solution.py:27
  273.6 5.5 %collective-permute-start.20 = (f32[3,192]{1,0:T(4,128)S(1)}, f32[3,192]{1,0:T(4,128)S(1)}, u32[]{:S(2)}, u32[]{:S(2)}) collective-permute-start(f32[3,192]{1,0:T(4,128)S(1)} %add.198), channel_id=1, source_target_pairs={{0,16},{16,0},{32,48},{48,32},{64,80},{80,64},{1,17},{17,1},{33,49... | collective-permute-start | bytes 6920 | tf_op jit(solution)/shard_map/ppermute | solution.py:34
  279.1 11.7 %collective-permute-start.21 = (f32[3,192]{1,0:T(4,128)S(1)}, f32[3,192]{1,0:T(4,128)S(1)}, u32[]{:S(2)}, u32[]{:S(2)}) collective-permute-start(f32[3,192]{1,0:T(4,128)S(1)} %add.199), channel_id=1, source_target_pairs={{0,32},{16,48},{32,64},{48,80},{64,0},{80,16},{1,33},{17,49},{33,6... | collective-permute-start | bytes 6920 | tf_op jit(solution)/shard_map/ppermute | solution.py:36
  284.6 8.3 %collective-permute-start.22 = (f32[3,192]{1,0:T(4,128)S(1)}, f32[3,192]{1,0:T(4,128)S(1)}, u32[]{:S(2)}, u32[]{:S(2)}) collective-permute-start(f32[3,192]{1,0:T(4,128)S(1)} %add.199), channel_id=1, source_target_pairs={{0,64},{16,80},{32,0},{48,16},{64,32},{80,48},{1,65},{17,81},{33,1... | collective-permute-start | bytes 6920 | tf_op jit(solution)/shard_map/ppermute | solution.py:37
  292.9 5.5 %collective-permute-start.23 = (f32[3,192]{1,0:T(4,128)S(1)}, f32[3,192]{1,0:T(4,128)S(1)}, u32[]{:S(2)}, u32[]{:S(2)}) collective-permute-start(f32[3,192]{1,0:T(4,128)S(1)} %select_add_fusion), channel_id=1, source_target_pairs={{0,96},{96,0},{192,288},{288,192},{384,480},{480,384},{576,672},{6... | collective-permute-start | bytes 6920 | tf_op jit(solution)/shard_map/ppermute | solution.py:27
  298.4 10.9 %collective-permute-start.24 = (f32[3,192]{1,0:T(4,128)S(1)}, f32[3,192]{1,0:T(4,128)S(1)}, u32[]{:S(2)}, u32[]{:S(2)}) collective-permute-start(f32[3,192]{1,0:T(4,128)S(1)} %add.202), channel_id=1, source_target_pairs={{0,192},{96,288},{192,0},{288,96},{384,576},{480,672},{576,384},{6... | collective-permute-start | bytes 6920 | tf_op jit(solution)/shard_map/ppermute | solution.py:27
  302.6 27.2 %collective-permute-start.29 = (f32[6,54,192]{2,1,0:T(8,128)}, f32[6,54,192]{2,1,0:T(8,128)S(1)}, u32[]{:S(2)}, u32[]{:S(2)}) collective-permute-start(f32[6,54,192]{2,1,0:T(8,128)} %dynamic-slice_bitcast_fusion.3), channel_id=1, source_target_pairs={{0,8},{1,9},{2,10},{3,11},{4,12},{5,13},{6,14},{7,15},{8,0},{9,1},... | collective-permute-start | bytes 746504 | tf_op jit(solution)/shard_map/ppermute | solution.py:60
  309.3 22.2 %collective-permute-start.25 = (f32[3,192]{1,0:T(4,128)S(1)}, f32[3,192]{1,0:T(4,128)S(1)}, u32[]{:S(2)}, u32[]{:S(2)}) collective-permute-start(f32[3,192]{1,0:T(4,128)S(1)} %add.203), channel_id=1, source_target_pairs={{0,384},{96,480},{192,576},{288,672},{384,0},{480,96},{576,192},{6... | collective-permute-start | bytes 6920 | tf_op jit(solution)/shard_map/ppermute | solution.py:27
  375.0 6.3 %collective-permute-start.30 = (f32[54,192]{1,0:T(8,128)}, f32[54,192]{1,0:T(8,128)S(1)}, u32[]{:S(2)}, u32[]{:S(2)}) collective-permute-start(f32[54,192]{1,0:T(8,128)} %bitcast.70), channel_id=1, source_target_pairs={{0,96},{96,0},{192,288},{288,192},{384,480},{480,384},{576,672},{6... | collective-permute-start | bytes 124424 | tf_op jit(solution)/shard_map/ppermute | solution.py:27
  382.1 8.2 %collective-permute-start.31 = (f32[54,192]{1,0:T(8,128)S(1)}, f32[54,192]{1,0:T(8,128)S(1)}, u32[]{:S(2)}, u32[]{:S(2)}) collective-permute-start(f32[54,192]{1,0:T(8,128)S(1)} %bitcast_add_fusion.4), channel_id=1, source_target_pairs={{0,192},{96,288},{192,0},{288,96},{384,576},{480,672},{576,384},{6... | collective-permute-start | bytes 124424 | tf_op jit(solution)/shard_map/ppermute | solution.py:27
  390.3 10.4 %collective-permute-start.32 = (f32[54,192]{1,0:T(8,128)S(1)}, f32[54,192]{1,0:T(8,128)S(1)}, u32[]{:S(2)}, u32[]{:S(2)}) collective-permute-start(f32[54,192]{1,0:T(8,128)S(1)} %add.223), channel_id=1, source_target_pairs={{0,384},{96,480},{192,576},{288,672},{384,0},{480,96},{576,192},{6... | collective-permute-start | bytes 124424 | tf_op jit(solution)/shard_map/ppermute | solution.py:27
  (21 other events, 448.0 us)
Sparse Core Ops, SparseCore 0:
  30.2 179.4 all-gather.2
Sparse Core Ops, SparseCore 1:
  330.7 44.2 reduce-scatter.1

commit v2 on v1

--- a/solution.py
+++ b/solution.py
@@ -59,6 +59,49 @@
         send = lax.dynamic_index_in_dim(q, 1 - bit, axis=at, keepdims=False)
         q = keep + lax.ppermute(send, axis, [(i, i ^ step) for i in range(n)])
     return q.reshape(shape[:dim] + (1,) + shape[dim + 1 :])
+
+
+def xor_gather(x, axis):
+    n = lax.axis_size(axis)
+    here = lax.axis_index(axis)
+    step = 1
+    while step < n:
+        other = lax.ppermute(x, axis, [(i, i ^ step) for i in range(n)])
+        low = (here // step) % 2 == 0
+        x = jnp.where(low, jnp.concatenate([x, other]), jnp.concatenate([other, x]))
+        step *= 2
+    return x
+
+
+def six_gather(x, axis):
+    n = lax.axis_size(axis)
+    here = lax.axis_index(axis)
+    other = lax.ppermute(x, axis, [(i, i ^ 1) for i in range(n)])
+    x = jnp.where(here % 2 == 0, jnp.concatenate([x, other]), jnp.concatenate([other, x]))
+    pair = here // 2
+    ahead = lax.ppermute(x, axis, [(i, (i + 2) % n) for i in range(n)])
+    behind = lax.ppermute(x, axis, [(i, (i + 4) % n) for i in range(n)])
+    first = jnp.where(pair == 0, x, jnp.where(pair == 1, ahead, behind))
+    second = jnp.where(pair == 1, x, jnp.where(pair == 2, ahead, behind))
+    third = jnp.where(pair == 2, x, jnp.where(pair == 0, ahead, behind))
+    return jnp.concatenate([first, second, third])
+
+
+def six_scatter(q, axis):
+    n = lax.axis_size(axis)
+    here = lax.axis_index(axis)
+    bit = here % 2
+    pair = here // 2
+    q = q.reshape((3, 2) + q.shape[1:])
+    keep = lax.dynamic_index_in_dim(q, bit, axis=1, keepdims=False)
+    send = lax.dynamic_index_in_dim(q, 1 - bit, axis=1, keepdims=False)
+    q = keep + lax.ppermute(send, axis, [(i, i ^ 1) for i in range(n)])
+    own = lax.dynamic_index_in_dim(q, pair, axis=0, keepdims=False)
+    to_next = lax.dynamic_index_in_dim(q, (pair + 1) % 3, axis=0, keepdims=False)
+    to_after = lax.dynamic_index_in_dim(q, (pair + 2) % 3, axis=0, keepdims=False)
+    near = lax.ppermute(to_next, axis, [(i, (i + 2) % n) for i in range(n)])
+    far = lax.ppermute(to_after, axis, [(i, (i + 4) % n) for i in range(n)])
+    return own + near + far
 
 
 def per_group(values):
@@ -122,7 +165,7 @@
         & ((col_pos < local_cols + 1) | (col_index < lax.axis_size("cols") - 1))
     )
     padded = jnp.where(valid, jax.nn.silu(pre_ext), 0.0).astype(jnp.bfloat16)
-    whole = lax.all_gather(weight, ("rows", "cols"), axis=0, tiled=True)
+    whole = six_gather(xor_gather(weight, "cols"), "rows")
     cells = local_frames * local_rows * local_cols
     windows = []
     grad_windows = []
@@ -174,8 +217,8 @@
     col_count = lax.axis_size("cols")
     band = kernel_grad.reshape(row_count, col_count, -1, channels)
     band = halve_scatter(band, "cols", 1)
-    band = lax.psum_scatter(band, "rows", scatter_dimension=0, tiled=True)
-    grad_weight = xor_sum(band.reshape(-1, channels), "tm")
+    band = six_scatter(band.reshape(row_count, -1, channels), "rows")
+    grad_weight = xor_sum(band, "tm")
     term_a = per_group(gain * grad_shift) / count
     term_b = per_group(gain * grad_gain) / count
     grad_video = (grad_f + rstd_c * (grad_pre * gain - term_a - normed * term_b)).astype(

time: 412 us -> 452 us (1.097)
  the two profiles are of different devices: /device:TPU:32 before, /device:TPU:4 now
where the time goes in v2:
time: 452 us; the launch traced here: 448 us
  starting transfers between devices  184 us (41%)
  waiting for transfers between devices  149 us (33%)
  local copies, waits for them, and re-layouts  69.3 us (15%)
  other arithmetic  30 us (7%)
  matrix products  14.4 us (3%)
    ppermute x17, starting transfers between devices, xor_sum(): x = x + lax.ppermute(x, axis, [(i, i ^ step) for i in range(n)])  82.2 us
    ppermute x17, waiting for transfers between devices, xor_sum(): x = x + lax.ppermute(x, axis, [(i, i ^ step) for i in range(n)])  50.8 us
    ppermute x1, waiting for transfers between devices, six_gather(): ahead = lax.ppermute(x, axis, [(i, (i + 2) % n) for i in range(n)])  26.4 us
    ppermute x4, waiting for transfers between devices, halve_scatter(): q = keep + lax.ppermute(send, axis, [(i, i ^ step) for i in range(n)])  26.4 us
    ppermute x4, starting transfers between devices, xor_gather(): other = lax.ppermute(x, axis, [(i, i ^ step) for i in range(n)])  21.4 us
    ppermute x4, starting transfers between devices, halve_scatter(): q = keep + lax.ppermute(send, axis, [(i, i ^ step) for i in range(n)])  19.1 us
    ppermute x2, starting transfers between devices, six_sum(): behind = lax.ppermute(x, axis, [(i, (i + 4) % n) for i in range(n)])  15.3 us
    ppermute x1, waiting for transfers between devices, six_gather(): behind = lax.ppermute(x, axis, [(i, (i + 4) % n) for i in range(n)])  13.1 us
  transfers between devices with their start and end apart: 43, of which 29 were waited for; matrix products, arithmetic and copies ran while one was open for 22% of the time, Pallas kernels for 0%

profile of v2, /device:TPU:4, one launch (start us, length us, event | category | flops | bytes accessed | tf_op | source)
XLA Modules:
  0.0 448.4 jit_solution(1833076055854112040)
XLA Ops:
  4.9 4.6 %collective-permute-start = (bf16[1,16,16,768]{3,2,1,0:T(8,128)(2,1)S(1)}, bf16[1,16,16,768]{3,2,1,0:T(8,128)(2,1)S(1)}, u32[]{:S(2)}, u32[]{:S(2)}) collective-permute-start(bf16[1,16,16,768]{3,2,1,0:T(8,128)(2,1)S(1)} %constant_dynamic-update-slice_fusion), channel_id=1, source_target_pairs={{0,96},{96,192},{192,288},{288,384},{384,480},{480,576},{576,672},... | collective-permute-start | bytes 1179656 | tf_op jit(solution)/shard_map/ppermute | solution.py:15
  19.5 11.4 %collective-permute-start.8 = (f32[2,192]{1,0:T(2,128)S(1)}, f32[2,192]{1,0:T(2,128)S(1)}, u32[]{:S(2)}, u32[]{:S(2)}) collective-permute-start(f32[2,192]{1,0:T(2,128)S(1)} %fusion.22), channel_id=1, source_target_pairs={{0,4},{1,5},{2,6},{3,7},{4,0},{5,1},{6,2},{7,3},{8,12},{9,13},{10,... | collective-permute-start | bytes 4616 | tf_op jit(solution)/shard_map/ppermute | solution.py:27
  32.4 9.2 %collective-permute-start.9 = (f32[2,192]{1,0:T(2,128)S(1)}, f32[2,192]{1,0:T(2,128)S(1)}, u32[]{:S(2)}, u32[]{:S(2)}) collective-permute-start(f32[2,192]{1,0:T(2,128)S(1)} %add.222), channel_id=1, source_target_pairs={{0,8},{1,9},{2,10},{3,11},{4,12},{5,13},{6,14},{7,15},{8,0},{9,1},... | collective-permute-start | bytes 4616 | tf_op jit(solution)/shard_map/ppermute | solution.py:27
  52.4 7.1 %collective-permute-start.12 = (f32[2,192]{1,0:T(2,128)S(1)}, f32[2,192]{1,0:T(2,128)S(1)}, u32[]{:S(2)}, u32[]{:S(2)}) collective-permute-start(f32[2,192]{1,0:T(2,128)S(1)} %add.224), channel_id=1, source_target_pairs={{0,64},{16,80},{32,0},{48,16},{64,32},{80,48},{1,65},{17,81},{33,1... | collective-permute-start | bytes 4616 | tf_op jit(solution)/shard_map/ppermute | solution.py:37
  72.6 6.6 %collective-permute-start.15 = (f32[2,192]{1,0:T(2,128)S(1)}, f32[2,192]{1,0:T(2,128)S(1)}, u32[]{:S(2)}, u32[]{:S(2)}) collective-permute-start(f32[2,192]{1,0:T(2,128)S(1)} %add.228), channel_id=1, source_target_pairs={{0,384},{96,480},{192,576},{288,672},{384,0},{480,96},{576,192},{6... | collective-permute-start | bytes 4616 | tf_op jit(solution)/shard_map/ppermute | solution.py:27
  88.4 5.4 %collective-permute-start.18 = (bf16[216,192]{1,0:T(8,128)(2,1)S(1)}, bf16[216,192]{1,0:T(8,128)(2,1)S(1)}, u32[]{:S(2)}, u32[]{:S(2)}) collective-permute-start(bf16[216,192]{1,0:T(8,128)(2,1)S(1)} %maximum_select_fusion.3), channel_id=1, source_target_pairs={{0,4},{1,5},{2,6},{3,7},{4,0},{5,1},{6,2},{7,3},{8,12},{9,13},{10,... | collective-permute-start | bytes 248840 | tf_op jit(solution)/shard_map/ppermute | solution.py:69
  96.6 11.0 %collective-permute-start.19 = (bf16[432,192]{1,0:T(8,128)(2,1)S(1)}, bf16[432,192]{1,0:T(8,128)(2,1)S(1)}, u32[]{:S(2)}, u32[]{:S(2)}) collective-permute-start(bf16[432,192]{1,0:T(8,128)(2,1)S(1)} %maximum_select_fusion.2), channel_id=1, source_target_pairs={{0,8},{1,9},{2,10},{3,11},{4,12},{5,13},{6,14},{7,15},{8,0},{9,1},... | collective-permute-start | bytes 497672 | tf_op jit(solution)/shard_map/ppermute | solution.py:69
  109.0 4.5 %collective-permute-start.2 = (bf16[3,1,16,768]{3,2,1,0:T(8,128)(2,1)S(1)}, bf16[3,1,16,768]{3,2,1,0:T(8,128)(2,1)S(1)}, u32[]{:S(2)}, u32[]{:S(2)}) collective-permute-start(bf16[3,1,16,768]{3,2,1,0:T(8,128)(2,1)S(1)} %get-tuple-element.18), channel_id=1, source_target_pairs={{0,16},{16,32},{32,48},{48,64},{64,80},{1,17},{17,33},{33,49},{49,... | collective-permute-start | bytes 221192 | tf_op jit(solution)/shard_map/ppermute | solution.py:15
  113.6 4.4 collective-permute-done.3
  126.8 4.3 fusion.2
  136.8 10.0 %concatenate.62 = bf16[2,16,16,5184]{3,2,1,0:T(8,128)(2,1)} concatenate(bf16[2,16,16,192]{3,2,1,0:T(8,128)(2,1)} %get-tuple-element.76, bf16[2,16,16,192]{3,2,1,0:T(8,128)(2,1)} %get-tuple-element.75, bf16[2,16,16,192]{3,2,1,0:T(8,128)(2,1)} %get-tuple-element.74, bf16[2,16,16,192]{3,2,1,0:T(8,128)(2,1)S(1)} %get-tuple-element.73, ...), dimensions={3} | concatenate | bytes 10616832 | tf_op jit(solution)/shard_map/concatenate | solution.py:189
  146.8 8.1 %copy.64 = bf16[512,5184]{0,1:T(8,128)(2,1)} copy(bf16[512,5184]{1,0:T(8,128)(2,1)} %bitcast.66) | data formatting | bytes 10616832 | tf_op jit(solution)/shard_map/reshape | solution.py:189
  155.0 7.7 %dot_general.16 = bf16[6,2,2,2,2,54,512]{6,5,4,3,2,1,0:T(8,128)(2,1)} reshape(bf16[5184,512]{1,0:T(8,128)(2,1)} %bitcast.69) | data formatting | bytes 10616832 | tf_op jit(solution)/shard_map/dot_general | solution.py:196
  180.6 6.5 %collective-permute-start.22 = (bf16[1728,192]{0,1:T(8,128)(2,1)}, bf16[1728,192]{0,1:T(8,128)(2,1)}, u32[]{:S(2)}, u32[]{:S(2)}) collective-permute-start(bf16[1728,192]{0,1:T(8,128)(2,1)} %copy.53), channel_id=1, source_target_pairs={{0,64},{16,80},{32,0},{48,16},{64,32},{80,48},{1,65},{17,81},{33,1... | collective-permute-start | bytes 1990664 | tf_op jit(solution)/shard_map/ppermute | solution.py:83
  194.4 10.1 %concatenate.75 = bf16[2,16,16,5184]{3,2,1,0:T(8,128)(2,1)} concatenate(bf16[2,16,16,192]{3,2,1,0:T(8,128)(2,1)} %get-tuple-element.49, bf16[2,16,16,192]{3,2,1,0:T(8,128)(2,1)S(1)} %get-tuple-element.48, bf16[2,16,16,192]{3,2,1,0:T(8,128)(2,1)S(1)} %get-tuple-element.47, bf16[2,16,16,192]{3,2,1,0:T(8,128)(2,1)S(1)} %get-tuple-element.46, ...), dimensions={3} | concatenate | bytes 10616832 | tf_op jit(solution)/shard_map/concatenate | solution.py:190
  204.4 26.4 %collective-permute-done.21 = bf16[1728,192]{0,1:T(8,128)(2,1)} collective-permute-done((bf16[1728,192]{0,1:T(8,128)(2,1)}, bf16[1728,192]{0,1:T(8,128)(2,1)}, u32[]{:S(2)}, u32[]{:S(2)}) %collective-permute-start.21) | collective-permute-done | bytes 663584 | tf_op jit(solution)/shard_map/ppermute | solution.py:82
  232.2 13.1 %collective-permute-done.22 = bf16[1728,192]{0,1:T(8,128)(2,1)} collective-permute-done((bf16[1728,192]{0,1:T(8,128)(2,1)}, bf16[1728,192]{0,1:T(8,128)(2,1)}, u32[]{:S(2)}, u32[]{:S(2)}) %collective-permute-start.22) | collective-permute-done | bytes 663584 | tf_op jit(solution)/shard_map/ppermute | solution.py:83
  260.9 4.5 %copy.62 = bf16[27,192,192]{2,1,0:T(8,128)(2,1)} copy(bf16[27,192,192]{1,2,0:T(8,128)(2,1)} %bitcast.70) | data formatting | bytes 3981312 | tf_op jit(solution)/shard_map/transpose | solution.py:200
  265.4 5.3 %convolution_convert_fusion = bf16[512,192]{0,1:T(8,128)(2,1)S(1)} fusion(bf16[512,5184]{1,0:T(8,128)(2,1)} %bitcast.68, bf16[5184,192]{1,0:T(8,128)(2,1)} %bitcast.71), kind=kOutput, calls=%fused_computation.10 | convolution fusion | flops 1019314176 | bytes 7495680 | tf_op jit(solution)/shard_map/dot_general | solution.py:202
  276.2 12.4 %collective-permute-done.34 = f32[6,2,2,54,192]{4,2,3,1,0:T(2,128)} collective-permute-done((f32[6,2,2,54,192]{4,2,3,1,0:T(2,128)}, f32[6,2,2,54,192]{4,2,3,1,0:T(2,128)}, u32[]{:S(2)}, u32[]{:S(2)}) %collective-permute-start.34) | collective-permute-done | bytes 995360 | tf_op jit(solution)/shard_map/ppermute | solution.py:60
  298.8 12.3 %collective-permute-done.24 = f32[3,192]{1,0:T(4,128)S(1)} collective-permute-done((f32[3,192]{1,0:T(4,128)S(1)}, f32[3,192]{1,0:T(4,128)S(1)}, u32[]{:S(2)}, u32[]{:S(2)}) %collective-permute-start.24) | collective-permute-done | bytes 2336 | tf_op jit(solution)/shard_map/ppermute | solution.py:27
  318.2 12.6 %collective-permute-start.26 = (f32[3,192]{1,0:T(4,128)S(1)}, f32[3,192]{1,0:T(4,128)S(1)}, u32[]{:S(2)}, u32[]{:S(2)}) collective-permute-start(f32[3,192]{1,0:T(4,128)S(1)} %add.247), channel_id=1, source_target_pairs={{0,8},{1,9},{2,10},{3,11},{4,12},{5,13},{6,14},{7,15},{8,0},{9,1},... | collective-permute-start | bytes 6920 | tf_op jit(solution)/shard_map/ppermute | solution.py:27
  339.8 8.2 %collective-permute-start.29 = (f32[3,192]{1,0:T(4,128)S(1)}, f32[3,192]{1,0:T(4,128)S(1)}, u32[]{:S(2)}, u32[]{:S(2)}) collective-permute-start(f32[3,192]{1,0:T(4,128)S(1)} %add.249), channel_id=1, source_target_pairs={{0,64},{16,80},{32,0},{48,16},{64,32},{80,48},{1,65},{17,81},{33,1... | collective-permute-start | bytes 6920 | tf_op jit(solution)/shard_map/ppermute | solution.py:37
  362.0 6.4 %collective-permute-start.32 = (f32[3,192]{1,0:T(4,128)S(1)}, f32[3,192]{1,0:T(4,128)S(1)}, u32[]{:S(2)}, u32[]{:S(2)}) collective-permute-start(f32[3,192]{1,0:T(4,128)S(1)} %add.253), channel_id=1, source_target_pairs={{0,384},{96,480},{192,576},{288,672},{384,0},{480,96},{576,192},{6... | collective-permute-start | bytes 6920 | tf_op jit(solution)/shard_map/ppermute | solution.py:27
  371.3 11.1 %collective-permute-start.36 = (f32[6,54,192]{2,1,0:T(8,128)}, f32[6,54,192]{2,1,0:T(8,128)}, u32[]{:S(2)}, u32[]{:S(2)}) collective-permute-start(f32[6,54,192]{2,1,0:T(8,128)} %dynamic-slice_bitcast_fusion.3), channel_id=1, source_target_pairs={{0,8},{1,9},{2,10},{3,11},{4,12},{5,13},{6,14},{7,15},{8,0},{9,1},... | collective-permute-start | bytes 746504 | tf_op jit(solution)/shard_map/ppermute | solution.py:60
  382.4 4.9 %convolution_add_fusion = f32[512,192]{0,1:T(8,128)S(1)} fusion(bf16[512,5184]{1,0:T(8,128)(2,1)} %bitcast.67, f32[192]{0:T(256)S(1)} %copy-done.25, bf16[1728,192]{1,0:T(8,128)(2,1)} %copy-done.7, bf16[1728,192]{1,0:T(8,128)(2,1)} %copy-done.6, bf16[1728,192]{1,0:T(8,128)(2,1)S(1)} %copy-done.5), kind=kOutput, calls=%fused_computation.9 | convolution fusion | flops 1025286144 | bytes 7693056 | tf_op jit(solution)/shard_map/dot_general | solution.py:191
  387.6 14.0 %collective-permute-done.36 = f32[6,54,192]{2,1,0:T(8,128)} collective-permute-done((f32[6,54,192]{2,1,0:T(8,128)}, f32[6,54,192]{2,1,0:T(8,128)}, u32[]{:S(2)}, u32[]{:S(2)}) %collective-permute-start.36) | collective-permute-done | bytes 248864 | tf_op jit(solution)/shard_map/ppermute | solution.py:60
  405.1 4.8 %collective-permute-done.37 = f32[3,54,192]{2,1,0:T(8,128)S(1)} collective-permute-done((f32[3,54,192]{2,1,0:T(8,128)S(1)}, f32[3,54,192]{2,1,0:T(8,128)S(1)}, u32[]{:S(2)}, u32[]{:S(2)}) %collective-permute-start.37) | collective-permute-done | bytes 124448 | tf_op jit(solution)/shard_map/ppermute | solution.py:98
  412.1 4.6 %collective-permute-start.38 = (f32[54,192]{1,0:T(8,128)S(1)}, f32[54,192]{1,0:T(8,128)S(1)}, u32[]{:S(2)}, u32[]{:S(2)}) collective-permute-start(f32[54,192]{1,0:T(8,128)S(1)} %get-tuple-element.77), channel_id=1, source_target_pairs={{0,32},{16,48},{32,64},{48,80},{64,0},{80,16},{1,33},{17,49},{33,6... | collective-permute-start | bytes 124424 | tf_op jit(solution)/shard_map/ppermute | solution.py:102
  417.6 5.1 %collective-permute-done.38 = f32[54,192]{1,0:T(8,128)S(1)} collective-permute-done((f32[54,192]{1,0:T(8,128)S(1)}, f32[54,192]{1,0:T(8,128)S(1)}, u32[]{:S(2)}, u32[]{:S(2)}) %collective-permute-start.38) | collective-permute-done | bytes 41504 | tf_op jit(solution)/shard_map/ppermute | solution.py:102
  431.9 5.7 %collective-permute-done.41 = f32[54,192]{1,0:T(8,128)S(1)} collective-permute-done((f32[54,192]{1,0:T(8,128)S(1)}, f32[54,192]{1,0:T(8,128)S(1)}, u32[]{:S(2)}, u32[]{:S(2)}) %collective-permute-start.41) | collective-permute-done | bytes 41504 | tf_op jit(solution)/shard_map/ppermute | solution.py:27
  441.7 6.1 %collective-permute-done.42 = f32[54,192]{1,0:T(8,128)S(1)} collective-permute-done((f32[54,192]{1,0:T(8,128)S(1)}, f32[54,192]{1,0:T(8,128)S(1)}, u32[]{:S(2)}, u32[]{:S(2)}) %collective-permute-start.42) | collective-permute-done | bytes 41504 | tf_op jit(solution)/shard_map/ppermute | solution.py:27
  (214 shorter events, 178.0 us)
Async XLA Ops:
  3.6 104.1 %collective-permute-start.1 = (bf16[1,16,16,768]{3,2,1,0:T(8,128)(2,1)S(1)}, bf16[1,16,16,768]{3,2,1,0:T(8,128)(2,1)S(1)}, u32[]{:S(2)}, u32[]{:S(2)}) collective-permute-start(bf16[1,16,16,768]{3,2,1,0:T(8,128)(2,1)S(1)} %constant_dynamic-update-slice_fusion), channel_id=1, source_target_pairs={{96,0},{192,96},{288,192},{384,288},{480,384},{576,480},{672,576},... | collective-permute-start | bytes 1179656 | tf_op jit(solution)/shard_map/ppermute | solution.py:18
  4.9 102.8 %collective-permute-start = (bf16[1,16,16,768]{3,2,1,0:T(8,128)(2,1)S(1)}, bf16[1,16,16,768]{3,2,1,0:T(8,128)(2,1)S(1)}, u32[]{:S(2)}, u32[]{:S(2)}) collective-permute-start(bf16[1,16,16,768]{3,2,1,0:T(8,128)(2,1)S(1)} %constant_dynamic-update-slice_fusion), channel_id=1, source_target_pairs={{0,96},{96,192},{192,288},{288,384},{384,480},{480,576},{576,672},... | collective-permute-start | bytes 1179656 | tf_op jit(solution)/shard_map/ppermute | solution.py:15
  11.5 70.7 %collective-permute-start.16 = (bf16[54,192]{1,0:T(8,128)(2,1)S(1)}, bf16[54,192]{1,0:T(8,128)(2,1)S(1)}, u32[]{:S(2)}, u32[]{:S(2)}) collective-permute-start(bf16[54,192]{1,0:T(8,128)(2,1)S(1)} %copy-done.20), channel_id=1, source_target_pairs={{0,1},{1,0},{2,3},{3,2},{4,5},{5,4},{6,7},{7,6},{8,9},{9,8},{10,11... | collective-permute-start | bytes 62216 | tf_op jit(solution)/shard_map/ppermute | solution.py:69
  19.5 13.0 %collective-permute-start.8 = (f32[2,192]{1,0:T(2,128)S(1)}, f32[2,192]{1,0:T(2,128)S(1)}, u32[]{:S(2)}, u32[]{:S(2)}) collective-permute-start(f32[2,192]{1,0:T(2,128)S(1)} %fusion.22), channel_id=1, source_target_pairs={{0,4},{1,5},{2,6},{3,7},{4,0},{5,1},{6,2},{7,3},{8,12},{9,13},{10,... | collective-permute-start | bytes 4616 | tf_op jit(solution)/shard_map/ppermute | solution.py:27
  32.4 11.8 %collective-permute-start.9 = (f32[2,192]{1,0:T(2,128)S(1)}, f32[2,192]{1,0:T(2,128)S(1)}, u32[]{:S(2)}, u32[]{:S(2)}) collective-permute-start(f32[2,192]{1,0:T(2,128)S(1)} %add.222), channel_id=1, source_target_pairs={{0,8},{1,9},{2,10},{3,11},{4,12},{5,13},{6,14},{7,15},{8,0},{9,1},... | collective-permute-start | bytes 4616 | tf_op jit(solution)/shard_map/ppermute | solution.py:27
  49.7 9.8 %collective-permute-start.11 = (f32[2,192]{1,0:T(2,128)S(1)}, f32[2,192]{1,0:T(2,128)S(1)}, u32[]{:S(2)}, u32[]{:S(2)}) collective-permute-start(f32[2,192]{1,0:T(2,128)S(1)} %add.224), channel_id=1, source_target_pairs={{0,32},{16,48},{32,64},{48,80},{64,0},{80,16},{1,33},{17,49},{33,6... | collective-permute-start | bytes 4616 | tf_op jit(solution)/shard_map/ppermute | solution.py:36
  52.4 8.4 %collective-permute-start.12 = (f32[2,192]{1,0:T(2,128)S(1)}, f32[2,192]{1,0:T(2,128)S(1)}, u32[]{:S(2)}, u32[]{:S(2)}) collective-permute-start(f32[2,192]{1,0:T(2,128)S(1)} %add.224), channel_id=1, source_target_pairs={{0,64},{16,80},{32,0},{48,16},{64,32},{80,48},{1,65},{17,81},{33,1... | collective-permute-start | bytes 4616 | tf_op jit(solution)/shard_map/ppermute | solution.py:37
  72.6 9.4 %collective-permute-start.15 = (f32[2,192]{1,0:T(2,128)S(1)}, f32[2,192]{1,0:T(2,128)S(1)}, u32[]{:S(2)}, u32[]{:S(2)}) collective-permute-start(f32[2,192]{1,0:T(2,128)S(1)} %add.228), channel_id=1, source_target_pairs={{0,384},{96,480},{192,576},{288,672},{384,0},{480,96},{576,192},{6... | collective-permute-start | bytes 4616 | tf_op jit(solution)/shard_map/ppermute | solution.py:27
  88.4 8.1 %collective-permute-start.18 = (bf16[216,192]{1,0:T(8,128)(2,1)S(1)}, bf16[216,192]{1,0:T(8,128)(2,1)S(1)}, u32[]{:S(2)}, u32[]{:S(2)}) collective-permute-start(bf16[216,192]{1,0:T(8,128)(2,1)S(1)} %maximum_select_fusion.3), channel_id=1, source_target_pairs={{0,4},{1,5},{2,6},{3,7},{4,0},{5,1},{6,2},{7,3},{8,12},{9,13},{10,... | collective-permute-start | bytes 248840 | tf_op jit(solution)/shard_map/ppermute | solution.py:69
  96.6 26.0 %collective-permute-start.19 = (bf16[432,192]{1,0:T(8,128)(2,1)S(1)}, bf16[432,192]{1,0:T(8,128)(2,1)S(1)}, u32[]{:S(2)}, u32[]{:S(2)}) collective-permute-start(bf16[432,192]{1,0:T(8,128)(2,1)S(1)} %maximum_select_fusion.2), channel_id=1, source_target_pairs={{0,8},{1,9},{2,10},{3,11},{4,12},{5,13},{6,14},{7,15},{8,0},{9,1},... | collective-permute-start | bytes 497672 | tf_op jit(solution)/shard_map/ppermute | solution.py:69
  107.7 10.2 %collective-permute-start.3 = (bf16[3,1,16,768]{3,2,1,0:T(8,128)(2,1)S(1)}, bf16[3,1,16,768]{3,2,1,0:T(8,128)(2,1)S(1)}, u32[]{:S(2)}, u32[]{:S(2)}) collective-permute-start(bf16[3,1,16,768]{3,2,1,0:T(8,128)(2,1)S(1)} %get-tuple-element.19), channel_id=1, source_target_pairs={{16,0},{32,16},{48,32},{64,48},{80,64},{17,1},{33,17},{49,33},{65,... | collective-permute-start | bytes 221192 | tf_op jit(solution)/shard_map/ppermute | solution.py:18
  109.0 8.9 %collective-permute-start.2 = (bf16[3,1,16,768]{3,2,1,0:T(8,128)(2,1)S(1)}, bf16[3,1,16,768]{3,2,1,0:T(8,128)(2,1)S(1)}, u32[]{:S(2)}, u32[]{:S(2)}) collective-permute-start(bf16[3,1,16,768]{3,2,1,0:T(8,128)(2,1)S(1)} %get-tuple-element.18), channel_id=1, source_target_pairs={{0,16},{16,32},{32,48},{48,64},{64,80},{1,17},{17,33},{33,49},{49,... | collective-permute-start | bytes 221192 | tf_op jit(solution)/shard_map/ppermute | solution.py:15
  118.2 7.3 %collective-permute-start.5 = (bf16[3,18,1,768]{3,2,1,0:T(2,128)(2,1)S(1)}, bf16[3,18,1,768]{3,2,1,0:T(2,128)(2,1)S(1)}, u32[]{:S(2)}, u32[]{:S(2)}) collective-permute-start(bf16[3,18,1,768]{3,2,1,0:T(2,128)(2,1)S(1)} %get-tuple-element.17), channel_id=1, source_target_pairs={{1,0},{2,1},{3,2},{4,3},{5,4},{6,5},{7,6},{8,7},{9,8},{10,9},{11,1... | collective-permute-start | bytes 248840 | tf_op jit(solution)/shard_map/ppermute | solution.py:18
  122.7 51.7 %collective-permute-start.20 = (bf16[864,192]{1,0:T(8,128)(2,1)S(1)}, bf16[864,192]{1,0:T(8,128)(2,1)}, u32[]{:S(2)}, u32[]{:S(2)}) collective-permute-start(bf16[864,192]{1,0:T(8,128)(2,1)S(1)} %maximum_select_fusion.1), channel_id=1, source_target_pairs={{0,16},{16,0},{32,48},{48,32},{64,80},{80,64},{1,17},{17,1},{33,49... | collective-permute-start | bytes 995336 | tf_op jit(solution)/shard_map/ppermute | solution.py:79
  172.4 76.7 %collective-permute-start.33 = (f32[6,2,2,2,54,192]{5,3,4,2,1,0:T(2,128)}, f32[6,2,2,2,54,192]{5,3,4,2,1,0:T(2,128)}, u32[]{:S(2)}, u32[]{:S(2)}) collective-permute-start(f32[6,2,2,2,54,192]{5,3,4,2,1,0:T(2,128)} %copy.66), channel_id=1, source_target_pairs={{0,1},{1,0},{2,3},{3,2},{4,5},{5,4},{6,7},{7,6},{8,9},{9,8},{10,11... | collective-permute-start | bytes 5971976 | tf_op jit(solution)/shard_map/ppermute | solution.py:60
  177.1 53.7 %collective-permute-start.21 = (bf16[1728,192]{0,1:T(8,128)(2,1)}, bf16[1728,192]{0,1:T(8,128)(2,1)}, u32[]{:S(2)}, u32[]{:S(2)}) collective-permute-start(bf16[1728,192]{0,1:T(8,128)(2,1)} %copy.53), channel_id=1, source_target_pairs={{0,32},{16,48},{32,64},{48,80},{64,0},{80,16},{1,33},{17,49},{33,6... | collective-permute-start | bytes 1990664 | tf_op jit(solution)/shard_map/ppermute | solution.py:82
  180.6 64.7 %collective-permute-start.22 = (bf16[1728,192]{0,1:T(8,128)(2,1)}, bf16[1728,192]{0,1:T(8,128)(2,1)}, u32[]{:S(2)}, u32[]{:S(2)}) collective-permute-start(bf16[1728,192]{0,1:T(8,128)(2,1)} %copy.53), channel_id=1, source_target_pairs={{0,64},{16,80},{32,0},{48,16},{64,32},{80,48},{1,65},{17,81},{33,1... | collective-permute-start | bytes 1990664 | tf_op jit(solution)/shard_map/ppermute | solution.py:83
  254.9 33.6 %collective-permute-start.34 = (f32[6,2,2,54,192]{4,2,3,1,0:T(2,128)}, f32[6,2,2,54,192]{4,2,3,1,0:T(2,128)}, u32[]{:S(2)}, u32[]{:S(2)}) collective-permute-start(f32[6,2,2,54,192]{4,2,3,1,0:T(2,128)} %copy.68), channel_id=1, source_target_pairs={{0,2},{1,3},{2,0},{3,1},{4,6},{5,7},{6,4},{7,5},{8,10},{9,11},{10,... | collective-permute-start | bytes 2985992 | tf_op jit(solution)/shard_map/ppermute | solution.py:60
  274.2 20.3 %collective-permute-start.23 = (f32[3,192]{1,0:T(4,128)S(1)}, f32[3,192]{1,0:T(4,128)S(1)}, u32[]{:S(2)}, u32[]{:S(2)}) collective-permute-start(f32[3,192]{1,0:T(4,128)S(1)} %pad_maximum_fusion.33), channel_id=1, source_target_pairs={{0,1},{1,0},{2,3},{3,2},{4,5},{5,4},{6,7},{7,6},{8,9},{9,8},{10,11... | collective-permute-start | bytes 6920 | tf_op jit(solution)/shard_map/ppermute | solution.py:27
  292.5 75.9 %collective-permute-start.35 = (f32[6,2,54,192]{3,1,2,0:T(2,128)}, f32[6,2,54,192]{3,1,2,0:T(2,128)}, u32[]{:S(2)}, u32[]{:S(2)}) collective-permute-start(f32[6,2,54,192]{3,1,2,0:T(2,128)} %copy.70), channel_id=1, source_target_pairs={{0,4},{1,5},{2,6},{3,7},{4,0},{5,1},{6,2},{7,3},{8,12},{9,13},{10,... | collective-permute-start | bytes 1493000 | tf_op jit(solution)/shard_map/ppermute | solution.py:60
  294.6 16.6 %collective-permute-start.24 = (f32[3,192]{1,0:T(4,128)S(1)}, f32[3,192]{1,0:T(4,128)S(1)}, u32[]{:S(2)}, u32[]{:S(2)}) collective-permute-start(f32[3,192]{1,0:T(4,128)S(1)} %fusion.8), channel_id=1, source_target_pairs={{0,2},{1,3},{2,0},{3,1},{4,6},{5,7},{6,4},{7,5},{8,10},{9,11},{10,... | collective-permute-start | bytes 6920 | tf_op jit(solution)/shard_map/ppermute | solution.py:27
  311.1 7.0 %collective-permute-start.25 = (f32[3,192]{1,0:T(4,128)S(1)}, f32[3,192]{1,0:T(4,128)S(1)}, u32[]{:S(2)}, u32[]{:S(2)}) collective-permute-start(f32[3,192]{1,0:T(4,128)S(1)} %fusion.21), channel_id=1, source_target_pairs={{0,4},{1,5},{2,6},{3,7},{4,0},{5,1},{6,2},{7,3},{8,12},{9,13},{10,... | collective-permute-start | bytes 6920 | tf_op jit(solution)/shard_map/ppermute | solution.py:27
  318.2 14.2 %collective-permute-start.26 = (f32[3,192]{1,0:T(4,128)S(1)}, f32[3,192]{1,0:T(4,128)S(1)}, u32[]{:S(2)}, u32[]{:S(2)}) collective-permute-start(f32[3,192]{1,0:T(4,128)S(1)} %add.247), channel_id=1, source_target_pairs={{0,8},{1,9},{2,10},{3,11},{4,12},{5,13},{6,14},{7,15},{8,0},{9,1},... | collective-permute-start | bytes 6920 | tf_op jit(solution)/shard_map/ppermute | solution.py:27
  337.9 10.1 %collective-permute-start.28 = (f32[3,192]{1,0:T(4,128)S(1)}, f32[3,192]{1,0:T(4,128)S(1)}, u32[]{:S(2)}, u32[]{:S(2)}) collective-permute-start(f32[3,192]{1,0:T(4,128)S(1)} %add.249), channel_id=1, source_target_pairs={{0,32},{16,48},{32,64},{48,80},{64,0},{80,16},{1,33},{17,49},{33,6... | collective-permute-start | bytes 6920 | tf_op jit(solution)/shard_map/ppermute | solution.py:36
  339.8 10.3 %collective-permute-start.29 = (f32[3,192]{1,0:T(4,128)S(1)}, f32[3,192]{1,0:T(4,128)S(1)}, u32[]{:S(2)}, u32[]{:S(2)}) collective-permute-start(f32[3,192]{1,0:T(4,128)S(1)} %add.249), channel_id=1, source_target_pairs={{0,64},{16,80},{32,0},{48,16},{64,32},{80,48},{1,65},{17,81},{33,1... | collective-permute-start | bytes 6920 | tf_op jit(solution)/shard_map/ppermute | solution.py:37
  362.0 25.5 %collective-permute-start.32 = (f32[3,192]{1,0:T(4,128)S(1)}, f32[3,192]{1,0:T(4,128)S(1)}, u32[]{:S(2)}, u32[]{:S(2)}) collective-permute-start(f32[3,192]{1,0:T(4,128)S(1)} %add.253), channel_id=1, source_target_pairs={{0,384},{96,480},{192,576},{288,672},{384,0},{480,96},{576,192},{6... | collective-permute-start | bytes 6920 | tf_op jit(solution)/shard_map/ppermute | solution.py:27
  371.3 30.3 %collective-permute-start.36 = (f32[6,54,192]{2,1,0:T(8,128)}, f32[6,54,192]{2,1,0:T(8,128)}, u32[]{:S(2)}, u32[]{:S(2)}) collective-permute-start(f32[6,54,192]{2,1,0:T(8,128)} %dynamic-slice_bitcast_fusion.3), channel_id=1, source_target_pairs={{0,8},{1,9},{2,10},{3,11},{4,12},{5,13},{6,14},{7,15},{8,0},{9,1},... | collective-permute-start | bytes 746504 | tf_op jit(solution)/shard_map/ppermute | solution.py:60
  402.6 7.3 %collective-permute-start.37 = (f32[3,54,192]{2,1,0:T(8,128)S(1)}, f32[3,54,192]{2,1,0:T(8,128)S(1)}, u32[]{:S(2)}, u32[]{:S(2)}) collective-permute-start(f32[3,54,192]{2,1,0:T(8,128)S(1)} %dynamic-slice_bitcast_fusion.4), channel_id=1, source_target_pairs={{0,16},{16,0},{32,48},{48,32},{64,80},{80,64},{1,17},{17,1},{33,49... | collective-permute-start | bytes 373256 | tf_op jit(solution)/shard_map/ppermute | solution.py:98
  410.0 7.6 %collective-permute-start.39 = (f32[54,192]{1,0:T(8,128)S(1)}, f32[54,192]{1,0:T(8,128)S(1)}, u32[]{:S(2)}, u32[]{:S(2)}) collective-permute-start(f32[54,192]{1,0:T(8,128)S(1)} %get-tuple-element.78), channel_id=1, source_target_pairs={{0,64},{16,80},{32,0},{48,16},{64,32},{80,48},{1,65},{17,81},{33,1... | collective-permute-start | bytes 124424 | tf_op jit(solution)/shard_map/ppermute | solution.py:103
  412.1 10.5 %collective-permute-start.38 = (f32[54,192]{1,0:T(8,128)S(1)}, f32[54,192]{1,0:T(8,128)S(1)}, u32[]{:S(2)}, u32[]{:S(2)}) collective-permute-start(f32[54,192]{1,0:T(8,128)S(1)} %get-tuple-element.77), channel_id=1, source_target_pairs={{0,32},{16,48},{32,64},{48,80},{64,0},{80,16},{1,33},{17,49},{33,6... | collective-permute-start | bytes 124424 | tf_op jit(solution)/shard_map/ppermute | solution.py:102
  428.8 8.8 %collective-permute-start.41 = (f32[54,192]{1,0:T(8,128)S(1)}, f32[54,192]{1,0:T(8,128)S(1)}, u32[]{:S(2)}, u32[]{:S(2)}) collective-permute-start(f32[54,192]{1,0:T(8,128)S(1)} %add.280), channel_id=1, source_target_pairs={{0,192},{96,288},{192,0},{288,96},{384,576},{480,672},{576,384},{6... | collective-permute-start | bytes 124424 | tf_op jit(solution)/shard_map/ppermute | solution.py:27
  437.6 10.2 %collective-permute-start.42 = (f32[54,192]{1,0:T(8,128)S(1)}, f32[54,192]{1,0:T(8,128)S(1)}, u32[]{:S(2)}, u32[]{:S(2)}) collective-permute-start(f32[54,192]{1,0:T(8,128)S(1)} %add.281), channel_id=1, source_target_pairs={{0,384},{96,480},{192,576},{288,672},{384,0},{480,96},{576,192},{6... | collective-permute-start | bytes 124424 | tf_op jit(solution)/shard_map/ppermute | solution.py:27
  (37 other events, 655.4 us)

commit v3 on v2

--- a/solution.py
+++ b/solution.py
@@ -104,6 +104,103 @@
     return own + near + far
 
 
+def three_way(here, mine, ahead, behind):
+    first = jnp.where(here == 0, mine, jnp.where(here == 1, ahead, behind))
+    second = jnp.where(here == 1, mine, jnp.where(here == 2, ahead, behind))
+    third = jnp.where(here == 2, mine, jnp.where(here == 0, ahead, behind))
+    return first, second, third
+
+
+def stats_and_weight(stats, weight):
+    count = lax.axis_size("cols")
+    here = lax.axis_index("cols")
+    step = 1
+    while step < count:
+        pairs = [(i, i ^ step) for i in range(count)]
+        other_stats = lax.ppermute(stats, "cols", pairs)
+        other_weight = lax.ppermute(weight, "cols", pairs)
+        stats = stats + other_stats
+        low = (here // step) % 2 == 0
+        weight = jnp.where(
+            low,
+            jnp.concatenate([weight, other_weight]),
+            jnp.concatenate([other_weight, weight]),
+        )
+        step *= 2
+    count = lax.axis_size("rows")
+    here = lax.axis_index("rows")
+    pairs = [(i, i ^ 1) for i in range(count)]
+    other_stats = lax.ppermute(stats, "rows", pairs)
+    other_weight = lax.ppermute(weight, "rows", pairs)
+    stats = stats + other_stats
+    weight = jnp.where(
+        here % 2 == 0,
+        jnp.concatenate([weight, other_weight]),
+        jnp.concatenate([other_weight, weight]),
+    )
+    ahead_pairs = [(i, (i + 2) % count) for i in range(count)]
+    behind_pairs = [(i, (i + 4) % count) for i in range(count)]
+    ahead_stats = lax.ppermute(stats, "rows", ahead_pairs)
+    ahead_weight = lax.ppermute(weight, "rows", ahead_pairs)
+    behind_stats = lax.ppermute(stats, "rows", behind_pairs)
+    behind_weight = lax.ppermute(weight, "rows", behind_pairs)
+    first, second, third = three_way(here // 2, stats, ahead_stats, behind_stats)
+    stats = (first + second) + third
+    weight = jnp.concatenate(three_way(here // 2, weight, ahead_weight, behind_weight))
+    return xor_sum(stats, "tm"), weight
+
+
+def reduce_grads(small, band):
+    channels = small.shape[-1]
+    extra = small.shape[0]
+    count = lax.axis_size("cols")
+    here = lax.axis_index("cols")
+    bits = count.bit_length() - 1
+    rows = band.shape[0]
+    q = band.reshape((rows,) + (2,) * bits + band.shape[2:])
+    for level in range(bits):
+        step = 1 << level
+        at = bits - level
+        bit = (here // step) % 2
+        keep = lax.dynamic_index_in_dim(q, bit, axis=at, keepdims=False)
+        send = lax.dynamic_index_in_dim(q, 1 - bit, axis=at, keepdims=False)
+        got = lax.ppermute(
+            jnp.concatenate([send.reshape(-1, channels), small]),
+            "cols",
+            [(i, i ^ step) for i in range(count)],
+        )
+        q = keep + got[:-extra].reshape(keep.shape)
+        small = small + got[-extra:]
+    count = lax.axis_size("rows")
+    here = lax.axis_index("rows")
+    bit = here % 2
+    pair = here // 2
+    q = q.reshape((3, 2) + q.shape[1:])
+    keep = lax.dynamic_index_in_dim(q, bit, axis=1, keepdims=False)
+    send = lax.dynamic_index_in_dim(q, 1 - bit, axis=1, keepdims=False)
+    got = lax.ppermute(
+        jnp.concatenate([send.reshape(-1, channels), small]),
+        "rows",
+        [(i, i ^ 1) for i in range(count)],
+    )
+    q = keep + got[:-extra].reshape(keep.shape)
+    small = small + got[-extra:]
+    own = lax.dynamic_index_in_dim(q, pair, axis=0, keepdims=False)
+    to_next = lax.dynamic_index_in_dim(q, (pair + 1) % 3, axis=0, keepdims=False)
+    to_after = lax.dynamic_index_in_dim(q, (pair + 2) % 3, axis=0, keepdims=False)
+    near = lax.ppermute(
+        jnp.concatenate([to_next, small]), "rows", [(i, (i + 2) % count) for i in range(count)]
+    )
+    far = lax.ppermute(
+        jnp.concatenate([to_after, small]), "rows", [(i, (i + 4) % count) for i in range(count)]
+    )
+    band = own + near[:-extra] + far[:-extra]
+    first, second, third = three_way(pair, small, near[-extra:], far[-extra:])
+    small = (first + second) + third
+    both = xor_sum(jnp.concatenate([band, small]), "tm")
+    return both[-extra:], both[:-extra]
+
+
 def per_group(values):
     return jnp.repeat(values.reshape(GROUPS, -1).sum(axis=1), CH // GROUPS)
 
@@ -137,8 +234,9 @@
     )
     grad_ext = from_pairs(framed[1:, :, :, 2 * channels :], local_rows, local_cols, channels)
     video_f = video.astype(jnp.float32)
-    sums, squares = all_sum(
-        jnp.stack([jnp.sum(video_f, axis=(0, 1, 2)), jnp.sum(video_f * video_f, axis=(0, 1, 2))])
+    (sums, squares), whole = stats_and_weight(
+        jnp.stack([jnp.sum(video_f, axis=(0, 1, 2)), jnp.sum(video_f * video_f, axis=(0, 1, 2))]),
+        weight,
     )
     devices_all = lax.axis_size("tm") * lax.axis_size("rows") * lax.axis_size("cols")
     count = float(local_frames * local_rows * local_cols * devices_all * (channels // GROUPS))
@@ -165,7 +263,6 @@
         & ((col_pos < local_cols + 1) | (col_index < lax.axis_size("cols") - 1))
     )
     padded = jnp.where(valid, jax.nn.silu(pre_ext), 0.0).astype(jnp.bfloat16)
-    whole = six_gather(xor_gather(weight, "cols"), "rows")
     cells = local_frames * local_rows * local_cols
     windows = []
     grad_windows = []
@@ -212,13 +309,12 @@
     gain_part = jnp.sum(grad_pre * normed, axis=(0, 1, 2))
     shift_part = jnp.sum(grad_pre, axis=(0, 1, 2))
     bias_part = jnp.sum(grad_f, axis=(0, 1, 2))
-    grad_gain, grad_shift, grad_conv_bias = all_sum(jnp.stack([gain_part, shift_part, bias_part]))
     row_count = lax.axis_size("rows")
     col_count = lax.axis_size("cols")
-    band = kernel_grad.reshape(row_count, col_count, -1, channels)
-    band = halve_scatter(band, "cols", 1)
-    band = six_scatter(band.reshape(row_count, -1, channels), "rows")
-    grad_weight = xor_sum(band, "tm")
+    (grad_gain, grad_shift, grad_conv_bias), grad_weight = reduce_grads(
+        jnp.stack([gain_part, shift_part, bias_part]),
+        kernel_grad.reshape(row_count, col_count, -1, channels),
+    )
     term_a = per_group(gain * grad_shift) / count
     term_b = per_group(gain * grad_gain) / count
     grad_video = (grad_f + rstd_c * (grad_pre * gain - term_a - normed * term_b)).astype(

time: 452 us -> 451 us (level)
  the two profiles are of different devices: /device:TPU:4 before, /device:TPU:1 now
where the time goes in v3:
time: 451 us; the launch traced here: 445 us
  starting transfers between devices  154 us (34%)
  waiting for transfers between devices  137 us (30%)
  local copies, waits for them, and re-layouts  102 us (23%)
  other arithmetic  32.1 us (7%)
  matrix products  17.2 us (4%)
    ppermute x4, waiting for transfers between devices, reduce_grads(): lax.ppermute(jnp.concatenate([send.reshape(-1, channels), small]), 'cols'...  56.1 us
    ppermute x4, starting transfers between devices, stats_and_weight(): other_weight = lax.ppermute(weight, 'cols', pairs)  28 us
    ppermute x6, starting transfers between devices, xor_sum(): x = x + lax.ppermute(x, axis, [(i, i ^ step) for i in range(n)])  27.4 us
    ppermute x3, starting transfers between devices, padded_2(): lax.ppermute(lax.slice_in_dim(block, block.shape[dim] - width, None, axis...  22 us
    ppermute x1, waiting for transfers between devices, stats_and_weight(): ahead_weight = lax.ppermute(weight, 'rows', ahead_pairs)  19.6 us
    ppermute x4, starting transfers between devices, reduce_grads(): lax.ppermute(jnp.concatenate([send.reshape(-1, channels), small]), 'cols'...  15.5 us
    ppermute x4, starting transfers between devices, stats_and_weight(): other_stats = lax.ppermute(stats, 'cols', pairs)  14.1 us
    ppermute x1, starting transfers between devices, reduce_grads(): lax.ppermute(jnp.concatenate([to_after, small]), 'rows', [(i, (i + 4) % c...  13.9 us
  transfers between devices with their start and end apart: 33, of which 25 were waited for; matrix products, arithmetic and copies ran while one was open for 17% of the time, Pallas kernels for 0%

profile of v3, /device:TPU:1, one launch (start us, length us, event | category | flops | bytes accessed | tf_op | source)
XLA Modules:
  0.0 444.8 jit_solution(11835646332236496348)
XLA Ops:
  3.6 4.0 collective-permute-start
  8.9 9.7 %collective-permute-start.16 = (bf16[54,192]{1,0:T(8,128)(2,1)S(1)}, bf16[54,192]{1,0:T(8,128)(2,1)S(1)}, u32[]{:S(2)}, u32[]{:S(2)}) collective-permute-start(bf16[54,192]{1,0:T(8,128)(2,1)S(1)} %copy-done.25), channel_id=1, source_target_pairs={{0,1},{1,0},{2,3},{3,2},{4,5},{5,4},{6,7},{7,6},{8,9},{9,8},{10,11... | collective-permute-start | bytes 62216 | tf_op jit(solution)/shard_map/ppermute | solution.py:121
  32.0 8.3 %collective-permute-start.9 = (f32[2,192]{1,0:T(2,128)S(1)}, f32[2,192]{1,0:T(2,128)S(1)}, u32[]{:S(2)}, u32[]{:S(2)}) collective-permute-start(f32[2,192]{1,0:T(2,128)S(1)} %add.214), channel_id=1, source_target_pairs={{0,8},{1,9},{2,10},{3,11},{4,12},{5,13},{6,14},{7,15},{8,0},{9,1},... | collective-permute-start | bytes 4616 | tf_op jit(solution)/shard_map/ppermute | solution.py:120
  49.4 6.8 %collective-permute-start.12 = (f32[2,192]{1,0:T(2,128)S(1)}, f32[2,192]{1,0:T(2,128)S(1)}, u32[]{:S(2)}, u32[]{:S(2)}) collective-permute-start(f32[2,192]{1,0:T(2,128)S(1)} %add.216), channel_id=1, source_target_pairs={{0,64},{16,80},{32,0},{48,16},{64,32},{80,48},{1,65},{17,81},{33,1... | collective-permute-start | bytes 4616 | tf_op jit(solution)/shard_map/ppermute | solution.py:145
  56.9 4.3 collective-permute-start.13
  67.3 7.5 %collective-permute-start.15 = (f32[2,192]{1,0:T(2,128)S(1)}, f32[2,192]{1,0:T(2,128)S(1)}, u32[]{:S(2)}, u32[]{:S(2)}) collective-permute-start(f32[2,192]{1,0:T(2,128)S(1)} %add.220), channel_id=1, source_target_pairs={{0,384},{96,480},{192,576},{288,672},{384,0},{480,96},{576,192},{6... | collective-permute-start | bytes 4616 | tf_op jit(solution)/shard_map/ppermute | solution.py:27
  81.0 4.7 %collective-permute-start.18 = (bf16[216,192]{1,0:T(8,128)(2,1)S(1)}, bf16[216,192]{1,0:T(8,128)(2,1)S(1)}, u32[]{:S(2)}, u32[]{:S(2)}) collective-permute-start(bf16[216,192]{1,0:T(8,128)(2,1)S(1)} %maximum_select_fusion.3), channel_id=1, source_target_pairs={{0,4},{1,5},{2,6},{3,7},{4,0},{5,1},{6,2},{7,3},{8,12},{9,13},{10,... | collective-permute-start | bytes 248840 | tf_op jit(solution)/shard_map/ppermute | solution.py:121
  88.1 10.5 %collective-permute-start.19 = (bf16[432,192]{1,0:T(8,128)(2,1)S(1)}, bf16[432,192]{1,0:T(8,128)(2,1)S(1)}, u32[]{:S(2)}, u32[]{:S(2)}) collective-permute-start(bf16[432,192]{1,0:T(8,128)(2,1)S(1)} %maximum_select_fusion.2), channel_id=1, source_target_pairs={{0,8},{1,9},{2,10},{3,11},{4,12},{5,13},{6,14},{7,15},{8,0},{9,1},... | collective-permute-start | bytes 497672 | tf_op jit(solution)/shard_map/ppermute | solution.py:121
  102.5 4.5 %collective-permute-done.2 = bf16[3,1,16,768]{3,2,1,0:T(8,128)(2,1)S(1)} collective-permute-done((bf16[3,1,16,768]{3,2,1,0:T(8,128)(2,1)S(1)}, bf16[3,1,16,768]{3,2,1,0:T(8,128)(2,1)S(1)}, u32[]{:S(2)}, u32[]{:S(2)}) %collective-permute-start.2) | collective-permute-done | bytes 73760 | tf_op jit(solution)/shard_map/ppermute | solution.py:15
  108.8 15.5 %collective-permute-start.4 = (bf16[3,18,1,768]{3,2,1,0:T(2,128)(2,1)S(1)}, bf16[3,18,1,768]{3,2,1,0:T(2,128)(2,1)S(1)}, u32[]{:S(2)}, u32[]{:S(2)}) collective-permute-start(bf16[3,18,1,768]{3,2,1,0:T(2,128)(2,1)S(1)} %get-tuple-element.16), channel_id=1, source_target_pairs={{0,1},{1,2},{2,3},{3,4},{4,5},{5,6},{6,7},{7,8},{8,9},{9,10},{10,1... | collective-permute-start | bytes 248840 | tf_op jit(solution)/shard_map/ppermute | solution.py:15
  131.3 4.3 fusion.2
  141.6 9.9 %concatenate.87 = bf16[2,16,16,5184]{3,2,1,0:T(8,128)(2,1)} concatenate(bf16[2,16,16,192]{3,2,1,0:T(8,128)(2,1)} %get-tuple-element.76, bf16[2,16,16,192]{3,2,1,0:T(8,128)(2,1)} %get-tuple-element.75, bf16[2,16,16,192]{3,2,1,0:T(8,128)(2,1)} %get-tuple-element.74, bf16[2,16,16,192]{3,2,1,0:T(8,128)(2,1)} %get-tuple-element.73, bf16[2,16,16,192]{3,2,1,0:T(8,128)(2,1)} %get-tuple-element.72, ...), dimensions={3} | concatenate | bytes 10616832 | tf_op jit(solution)/shard_map/concatenate | solution.py:286
  151.5 8.1 %copy.55 = bf16[512,5184]{0,1:T(8,128)(2,1)} copy(bf16[512,5184]{1,0:T(8,128)(2,1)} %bitcast.59) | data formatting | bytes 10616832 | tf_op jit(solution)/shard_map/reshape | solution.py:286
  159.6 7.7 %dot_general.16 = bf16[6,2,2,2,2,54,512]{6,5,4,3,2,1,0:T(8,128)(2,1)} reshape(bf16[5184,512]{1,0:T(8,128)(2,1)} %bitcast.62) | data formatting | bytes 10616832 | tf_op jit(solution)/shard_map/dot_general | solution.py:293
  167.3 6.7 %fusion.15 = f32[6,2,2,2,2,54,192]{6,5,4,3,2,1,0:T(8,128)} fusion(bf16[6,2,2,2,2,54,512]{6,5,4,3,2,1,0:T(8,128)(2,1)} %dot_general.16, bf16[512,192,1,1,1,1,1]{1,0,6,5,4,3,2:T(8,128)(2,1)S(1)} %bitcast.66), kind=kOutput, calls=%fused_computation.112 | convolution fusion | flops 1019215872 | bytes 9486336 | tf_op jit(solution)/shard_map/dot_general | solution.py:293
  174.0 3.9 fusion.1
  184.1 5.9 %collective-permute-start.22 = (bf16[1728,192]{0,1:T(8,128)(2,1)}, bf16[1728,192]{0,1:T(8,128)(2,1)}, u32[]{:S(2)}, u32[]{:S(2)}) collective-permute-start(bf16[1728,192]{0,1:T(8,128)(2,1)} %copy.44), channel_id=1, source_target_pairs={{0,64},{16,80},{32,0},{48,16},{64,32},{80,48},{1,65},{17,81},{33,1... | collective-permute-start | bytes 1990664 | tf_op jit(solution)/shard_map/ppermute | solution.py:146
  200.6 10.1 %concatenate.100 = bf16[2,16,16,5184]{3,2,1,0:T(8,128)(2,1)} concatenate(bf16[2,16,16,192]{3,2,1,0:T(8,128)(2,1)} %get-tuple-element.49, bf16[2,16,16,192]{3,2,1,0:T(8,128)(2,1)} %get-tuple-element.48, bf16[2,16,16,192]{3,2,1,0:T(8,128)(2,1)} %get-tuple-element.47, bf16[2,16,16,192]{3,2,1,0:T(8,128)(2,1)} %get-tuple-element.46, bf16[2,16,16,192]{3,2,1,0:T(8,128)(2,1)S(1)} %get-tuple-element.45, ...), dimensions={3} | concatenate | bytes 10616832 | tf_op jit(solution)/shard_map/concatenate | solution.py:287
  210.7 19.6 %collective-permute-done.21 = bf16[1728,192]{0,1:T(8,128)(2,1)} collective-permute-done((bf16[1728,192]{0,1:T(8,128)(2,1)}, bf16[1728,192]{0,1:T(8,128)(2,1)}, u32[]{:S(2)}, u32[]{:S(2)}) %collective-permute-start.21) | collective-permute-done | bytes 663584 | tf_op jit(solution)/shard_map/ppermute | solution.py:144
  231.7 13.3 %collective-permute-done.22 = bf16[1728,192]{0,1:T(8,128)(2,1)} collective-permute-done((bf16[1728,192]{0,1:T(8,128)(2,1)}, bf16[1728,192]{0,1:T(8,128)(2,1)}, u32[]{:S(2)}, u32[]{:S(2)}) %collective-permute-start.22) | collective-permute-done | bytes 663584 | tf_op jit(solution)/shard_map/ppermute | solution.py:146
  251.5 5.3 %convolution_convert_fusion = bf16[512,192]{0,1:T(8,128)(2,1)S(1)} fusion(bf16[512,5184]{1,0:T(8,128)(2,1)} %bitcast.61, bf16[5184,192]{1,0:T(8,128)(2,1)} %bitcast.64), kind=kOutput, calls=%fused_computation.9 | convolution fusion | flops 1019314176 | bytes 7495680 | tf_op jit(solution)/shard_map/dot_general | solution.py:299
  259.4 6.2 %concatenate.101 = f32[2595,192]{1,0:T(8,128)S(1)} concatenate(f32[2592,192]{1,0:T(8,128)} %reshape.249, f32[1,192]{1,0:T(1,128)S(1)} %bitcast.84, f32[1,192]{1,0:T(1,128)S(1)} %bitcast.81, f32[1,192]{1,0:T(1,128)S(1)} %bitcast.87), dimensions={0} | concatenate | bytes 3985920 | tf_op jit(solution)/shard_map/concatenate | solution.py:168
  292.7 5.3 %collective-permute-start.24 = (f32[1299,192]{0,1:T(8,128)}, f32[1299,192]{0,1:T(8,128)}, u32[]{:S(2)}, u32[]{:S(2)}) collective-permute-start(f32[1299,192]{0,1:T(8,128)} %copy.60), channel_id=1, source_target_pairs={{0,2},{1,3},{2,0},{3,1},{4,6},{5,7},{6,4},{7,5},{8,10},{9,11},{10,... | collective-permute-start | bytes 2992904 | tf_op jit(solution)/shard_map/ppermute | solution.py:167
  298.1 24.2 %collective-permute-done.24 = f32[1299,192]{0,1:T(8,128)} collective-permute-done((f32[1299,192]{0,1:T(8,128)}, f32[1299,192]{0,1:T(8,128)}, u32[]{:S(2)}, u32[]{:S(2)}) %collective-permute-start.24) | collective-permute-done | bytes 997664 | tf_op jit(solution)/shard_map/ppermute | solution.py:167
  332.5 4.6 %collective-permute-start.25 = (f32[651,192]{0,1:T(8,128)}, f32[651,192]{0,1:T(8,128)S(1)}, u32[]{:S(2)}, u32[]{:S(2)}) collective-permute-start(f32[651,192]{0,1:T(8,128)} %copy.63), channel_id=1, source_target_pairs={{0,4},{1,5},{2,6},{3,7},{4,0},{5,1},{6,2},{7,3},{8,12},{9,13},{10,... | collective-permute-start | bytes 1499912 | tf_op jit(solution)/shard_map/ppermute | solution.py:167
  337.1 12.9 %collective-permute-done.25 = f32[651,192]{0,1:T(8,128)S(1)} collective-permute-done((f32[651,192]{0,1:T(8,128)}, f32[651,192]{0,1:T(8,128)S(1)}, u32[]{:S(2)}, u32[]{:S(2)}) %collective-permute-start.25) | collective-permute-done | bytes 500000 | tf_op jit(solution)/shard_map/ppermute | solution.py:167
  355.8 15.1 %collective-permute-done.26 = f32[327,192]{1,0:T(8,128)S(1)} collective-permute-done((f32[327,192]{1,0:T(8,128)S(1)}, f32[327,192]{1,0:T(8,128)S(1)}, u32[]{:S(2)}, u32[]{:S(2)}) %collective-permute-start.26) | collective-permute-done | bytes 251168 | tf_op jit(solution)/shard_map/ppermute | solution.py:167
  377.6 10.2 %collective-permute-done.27 = f32[165,192]{1,0:T(8,128)S(1)} collective-permute-done((f32[165,192]{1,0:T(8,128)}, f32[165,192]{1,0:T(8,128)S(1)}, u32[]{:S(2)}, u32[]{:S(2)}) %collective-permute-start.27) | collective-permute-done | bytes 126752 | tf_op jit(solution)/shard_map/ppermute | solution.py:181
  391.6 4.3 collective-permute-start.28
  395.9 13.9 %collective-permute-start.29 = (f32[57,192]{1,0:T(8,128)S(1)}, f32[57,192]{1,0:T(8,128)}, u32[]{:S(2)}, u32[]{:S(2)}) collective-permute-start(f32[57,192]{1,0:T(8,128)S(1)} %get-tuple-element.85), channel_id=1, source_target_pairs={{0,64},{16,80},{32,0},{48,16},{64,32},{80,48},{1,65},{17,81},{33,1... | collective-permute-start | bytes 131336 | tf_op jit(solution)/shard_map/ppermute | solution.py:194
  425.3 5.2 %convolution_add_fusion = f32[512,192]{0,1:T(8,128)} fusion(bf16[512,5184]{1,0:T(8,128)(2,1)} %bitcast.60, f32[192]{0:T(256)S(1)} %copy-done.30, bf16[1728,192]{1,0:T(8,128)(2,1)S(1)} %copy-done.8, bf16[1728,192]{1,0:T(8,128)(2,1)S(1)} %copy-done.6, bf16[1728,192]{1,0:T(8,128)(2,1)S(1)} %copy-done.4), kind=kOutput, calls=%fused_computation.8 | convolution fusion | flops 1025286144 | bytes 7693056 | tf_op jit(solution)/shard_map/dot_general | solution.py:288
  431.8 5.7 %collective-permute-start.32 = (f32[57,192]{1,0:T(8,128)S(1)}, f32[57,192]{1,0:T(8,128)S(1)}, u32[]{:S(2)}, u32[]{:S(2)}) collective-permute-start(f32[57,192]{1,0:T(8,128)S(1)} %add.269), channel_id=1, source_target_pairs={{0,384},{96,480},{192,576},{288,672},{384,0},{480,96},{576,192},{6... | collective-permute-start | bytes 131336 | tf_op jit(solution)/shard_map/ppermute | solution.py:27
  (228 shorter events, 164.9 us)
Async XLA Ops:
  3.6 95.1 %collective-permute-start = (bf16[1,16,16,768]{3,2,1,0:T(8,128)(2,1)S(1)}, bf16[1,16,16,768]{3,2,1,0:T(8,128)(2,1)S(1)}, u32[]{:S(2)}, u32[]{:S(2)}) collective-permute-start(bf16[1,16,16,768]{3,2,1,0:T(8,128)(2,1)S(1)} %constant_dynamic-update-slice_fusion), channel_id=1, source_target_pairs={{0,96},{96,192},{192,288},{288,384},{384,480},{480,576},{576,672},... | collective-permute-start | bytes 1179656 | tf_op jit(solution)/shard_map/ppermute | solution.py:15
  7.6 91.0 %collective-permute-start.1 = (bf16[1,16,16,768]{3,2,1,0:T(8,128)(2,1)S(1)}, bf16[1,16,16,768]{3,2,1,0:T(8,128)(2,1)S(1)}, u32[]{:S(2)}, u32[]{:S(2)}) collective-permute-start(bf16[1,16,16,768]{3,2,1,0:T(8,128)(2,1)S(1)} %constant_dynamic-update-slice_fusion), channel_id=1, source_target_pairs={{96,0},{192,96},{288,192},{384,288},{480,384},{576,480},{672,576},... | collective-permute-start | bytes 1179656 | tf_op jit(solution)/shard_map/ppermute | solution.py:18
  8.9 67.1 %collective-permute-start.16 = (bf16[54,192]{1,0:T(8,128)(2,1)S(1)}, bf16[54,192]{1,0:T(8,128)(2,1)S(1)}, u32[]{:S(2)}, u32[]{:S(2)}) collective-permute-start(bf16[54,192]{1,0:T(8,128)(2,1)S(1)} %copy-done.25), channel_id=1, source_target_pairs={{0,1},{1,0},{2,3},{3,2},{4,5},{5,4},{6,7},{7,6},{8,9},{9,8},{10,11... | collective-permute-start | bytes 62216 | tf_op jit(solution)/shard_map/ppermute | solution.py:121
  21.8 4.3 collective-permute-start.7
  26.2 5.8 %collective-permute-start.8 = (f32[2,192]{1,0:T(2,128)S(1)}, f32[2,192]{1,0:T(2,128)S(1)}, u32[]{:S(2)}, u32[]{:S(2)}) collective-permute-start(f32[2,192]{1,0:T(2,128)S(1)} %fusion.22), channel_id=1, source_target_pairs={{0,4},{1,5},{2,6},{3,7},{4,0},{5,1},{6,2},{7,3},{8,12},{9,13},{10,... | collective-permute-start | bytes 4616 | tf_op jit(solution)/shard_map/ppermute | solution.py:120
  32.0 10.6 %collective-permute-start.9 = (f32[2,192]{1,0:T(2,128)S(1)}, f32[2,192]{1,0:T(2,128)S(1)}, u32[]{:S(2)}, u32[]{:S(2)}) collective-permute-start(f32[2,192]{1,0:T(2,128)S(1)} %add.214), channel_id=1, source_target_pairs={{0,8},{1,9},{2,10},{3,11},{4,12},{5,13},{6,14},{7,15},{8,0},{9,1},... | collective-permute-start | bytes 4616 | tf_op jit(solution)/shard_map/ppermute | solution.py:120
  42.6 4.3 collective-permute-start.10
  47.0 9.3 %collective-permute-start.11 = (f32[2,192]{1,0:T(2,128)S(1)}, f32[2,192]{1,0:T(2,128)S(1)}, u32[]{:S(2)}, u32[]{:S(2)}) collective-permute-start(f32[2,192]{1,0:T(2,128)S(1)} %add.216), channel_id=1, source_target_pairs={{0,32},{16,48},{32,64},{48,80},{64,0},{80,16},{1,33},{17,49},{33,6... | collective-permute-start | bytes 4616 | tf_op jit(solution)/shard_map/ppermute | solution.py:143
  49.4 7.5 %collective-permute-start.12 = (f32[2,192]{1,0:T(2,128)S(1)}, f32[2,192]{1,0:T(2,128)S(1)}, u32[]{:S(2)}, u32[]{:S(2)}) collective-permute-start(f32[2,192]{1,0:T(2,128)S(1)} %add.216), channel_id=1, source_target_pairs={{0,64},{16,80},{32,0},{48,16},{64,32},{80,48},{1,65},{17,81},{33,1... | collective-permute-start | bytes 4616 | tf_op jit(solution)/shard_map/ppermute | solution.py:145
  56.9 5.2 %collective-permute-start.13 = (f32[2,192]{1,0:T(2,128)S(1)}, f32[2,192]{1,0:T(2,128)S(1)}, u32[]{:S(2)}, u32[]{:S(2)}) collective-permute-start(f32[2,192]{1,0:T(2,128)S(1)} %select_add_fusion.1), channel_id=1, source_target_pairs={{0,96},{96,0},{192,288},{288,192},{384,480},{480,384},{576,672},{6... | collective-permute-start | bytes 4616 | tf_op jit(solution)/shard_map/ppermute | solution.py:27
  62.1 5.2 %collective-permute-start.14 = (f32[2,192]{1,0:T(2,128)S(1)}, f32[2,192]{1,0:T(2,128)S(1)}, u32[]{:S(2)}, u32[]{:S(2)}) collective-permute-start(f32[2,192]{1,0:T(2,128)S(1)} %add.219), channel_id=1, source_target_pairs={{0,192},{96,288},{192,0},{288,96},{384,576},{480,672},{576,384},{6... | collective-permute-start | bytes 4616 | tf_op jit(solution)/shard_map/ppermute | solution.py:27
  67.3 8.4 %collective-permute-start.15 = (f32[2,192]{1,0:T(2,128)S(1)}, f32[2,192]{1,0:T(2,128)S(1)}, u32[]{:S(2)}, u32[]{:S(2)}) collective-permute-start(f32[2,192]{1,0:T(2,128)S(1)} %add.220), channel_id=1, source_target_pairs={{0,384},{96,480},{192,576},{288,672},{384,0},{480,96},{576,192},{6... | collective-permute-start | bytes 4616 | tf_op jit(solution)/shard_map/ppermute | solution.py:27
  76.1 4.9 %collective-permute-start.17 = (bf16[108,192]{1,0:T(8,128)(2,1)S(1)}, bf16[108,192]{1,0:T(8,128)(2,1)S(1)}, u32[]{:S(2)}, u32[]{:S(2)}) collective-permute-start(bf16[108,192]{1,0:T(8,128)(2,1)S(1)} %maximum_select_fusion.4), channel_id=1, source_target_pairs={{0,2},{1,3},{2,0},{3,1},{4,6},{5,7},{6,4},{7,5},{8,10},{9,11},{10,... | collective-permute-start | bytes 124424 | tf_op jit(solution)/shard_map/ppermute | solution.py:121
  81.0 7.0 %collective-permute-start.18 = (bf16[216,192]{1,0:T(8,128)(2,1)S(1)}, bf16[216,192]{1,0:T(8,128)(2,1)S(1)}, u32[]{:S(2)}, u32[]{:S(2)}) collective-permute-start(bf16[216,192]{1,0:T(8,128)(2,1)S(1)} %maximum_select_fusion.3), channel_id=1, source_target_pairs={{0,4},{1,5},{2,6},{3,7},{4,0},{5,1},{6,2},{7,3},{8,12},{9,13},{10,... | collective-permute-start | bytes 248840 | tf_op jit(solution)/shard_map/ppermute | solution.py:121
  88.1 38.1 %collective-permute-start.19 = (bf16[432,192]{1,0:T(8,128)(2,1)S(1)}, bf16[432,192]{1,0:T(8,128)(2,1)S(1)}, u32[]{:S(2)}, u32[]{:S(2)}) collective-permute-start(bf16[432,192]{1,0:T(8,128)(2,1)S(1)} %maximum_select_fusion.2), channel_id=1, source_target_pairs={{0,8},{1,9},{2,10},{3,11},{4,12},{5,13},{6,14},{7,15},{8,0},{9,1},... | collective-permute-start | bytes 497672 | tf_op jit(solution)/shard_map/ppermute | solution.py:121
  98.7 8.4 %collective-permute-start.2 = (bf16[3,1,16,768]{3,2,1,0:T(8,128)(2,1)S(1)}, bf16[3,1,16,768]{3,2,1,0:T(8,128)(2,1)S(1)}, u32[]{:S(2)}, u32[]{:S(2)}) collective-permute-start(bf16[3,1,16,768]{3,2,1,0:T(8,128)(2,1)S(1)} %get-tuple-element.18), channel_id=1, source_target_pairs={{0,16},{16,32},{32,48},{48,64},{64,80},{1,17},{17,33},{33,49},{49,... | collective-permute-start | bytes 221192 | tf_op jit(solution)/shard_map/ppermute | solution.py:15
  101.2 7.3 %collective-permute-start.3 = (bf16[3,1,16,768]{3,2,1,0:T(8,128)(2,1)S(1)}, bf16[3,1,16,768]{3,2,1,0:T(8,128)(2,1)S(1)}, u32[]{:S(2)}, u32[]{:S(2)}) collective-permute-start(bf16[3,1,16,768]{3,2,1,0:T(8,128)(2,1)S(1)} %get-tuple-element.19), channel_id=1, source_target_pairs={{16,0},{32,16},{48,32},{64,48},{80,64},{17,1},{33,17},{49,33},{65,... | collective-permute-start | bytes 221192 | tf_op jit(solution)/shard_map/ppermute | solution.py:18
  108.8 19.9 %collective-permute-start.4 = (bf16[3,18,1,768]{3,2,1,0:T(2,128)(2,1)S(1)}, bf16[3,18,1,768]{3,2,1,0:T(2,128)(2,1)S(1)}, u32[]{:S(2)}, u32[]{:S(2)}) collective-permute-start(bf16[3,18,1,768]{3,2,1,0:T(2,128)(2,1)S(1)} %get-tuple-element.16), channel_id=1, source_target_pairs={{0,1},{1,2},{2,3},{3,4},{4,5},{5,6},{6,7},{7,8},{8,9},{9,10},{10,1... | collective-permute-start | bytes 248840 | tf_op jit(solution)/shard_map/ppermute | solution.py:15
  124.3 7.1 %collective-permute-start.5 = (bf16[3,18,1,768]{3,2,1,0:T(2,128)(2,1)S(1)}, bf16[3,18,1,768]{3,2,1,0:T(2,128)(2,1)S(1)}, u32[]{:S(2)}, u32[]{:S(2)}) collective-permute-start(bf16[3,18,1,768]{3,2,1,0:T(2,128)(2,1)S(1)} %get-tuple-element.17), channel_id=1, source_target_pairs={{1,0},{2,1},{3,2},{4,3},{5,4},{6,5},{7,6},{8,7},{9,8},{10,9},{11,1... | collective-permute-start | bytes 248840 | tf_op jit(solution)/shard_map/ppermute | solution.py:18
  126.4 51.5 %collective-permute-start.20 = (bf16[864,192]{1,0:T(8,128)(2,1)S(1)}, bf16[864,192]{1,0:T(8,128)(2,1)}, u32[]{:S(2)}, u32[]{:S(2)}) collective-permute-start(bf16[864,192]{1,0:T(8,128)(2,1)S(1)} %maximum_select_fusion.1), channel_id=1, source_target_pairs={{0,16},{16,0},{32,48},{48,32},{64,80},{80,64},{1,17},{17,1},{33,49... | collective-permute-start | bytes 995336 | tf_op jit(solution)/shard_map/ppermute | solution.py:134
  180.5 49.7 %collective-permute-start.21 = (bf16[1728,192]{0,1:T(8,128)(2,1)}, bf16[1728,192]{0,1:T(8,128)(2,1)}, u32[]{:S(2)}, u32[]{:S(2)}) collective-permute-start(bf16[1728,192]{0,1:T(8,128)(2,1)} %copy.44), channel_id=1, source_target_pairs={{0,32},{16,48},{32,64},{48,80},{64,0},{80,16},{1,33},{17,49},{33,6... | collective-permute-start | bytes 1990664 | tf_op jit(solution)/shard_map/ppermute | solution.py:144
  184.1 60.9 %collective-permute-start.22 = (bf16[1728,192]{0,1:T(8,128)(2,1)}, bf16[1728,192]{0,1:T(8,128)(2,1)}, u32[]{:S(2)}, u32[]{:S(2)}) collective-permute-start(bf16[1728,192]{0,1:T(8,128)(2,1)} %copy.44), channel_id=1, source_target_pairs={{0,64},{16,80},{32,0},{48,16},{64,32},{80,48},{1,65},{17,81},{33,1... | collective-permute-start | bytes 1990664 | tf_op jit(solution)/shard_map/ppermute | solution.py:146
  267.8 6.2 %collective-permute-start.23 = (f32[2595,192]{0,1:T(8,128)}, f32[2595,192]{0,1:T(8,128)S(1)}, u32[]{:S(2)}, u32[]{:S(2)}) collective-permute-start(f32[2595,192]{0,1:T(8,128)} %copy.57), channel_id=1, source_target_pairs={{0,1},{1,0},{2,3},{3,2},{4,5},{5,4},{6,7},{7,6},{8,9},{9,8},{10,11... | collective-permute-start | bytes 5978888 | tf_op jit(solution)/shard_map/ppermute | solution.py:167
  292.7 29.5 %collective-permute-start.24 = (f32[1299,192]{0,1:T(8,128)}, f32[1299,192]{0,1:T(8,128)}, u32[]{:S(2)}, u32[]{:S(2)}) collective-permute-start(f32[1299,192]{0,1:T(8,128)} %copy.60), channel_id=1, source_target_pairs={{0,2},{1,3},{2,0},{3,1},{4,6},{5,7},{6,4},{7,5},{8,10},{9,11},{10,... | collective-permute-start | bytes 2992904 | tf_op jit(solution)/shard_map/ppermute | solution.py:167
  332.5 17.5 %collective-permute-start.25 = (f32[651,192]{0,1:T(8,128)}, f32[651,192]{0,1:T(8,128)S(1)}, u32[]{:S(2)}, u32[]{:S(2)}) collective-permute-start(f32[651,192]{0,1:T(8,128)} %copy.63), channel_id=1, source_target_pairs={{0,4},{1,5},{2,6},{3,7},{4,0},{5,1},{6,2},{7,3},{8,12},{9,13},{10,... | collective-permute-start | bytes 1499912 | tf_op jit(solution)/shard_map/ppermute | solution.py:167
  352.5 18.4 %collective-permute-start.26 = (f32[327,192]{1,0:T(8,128)S(1)}, f32[327,192]{1,0:T(8,128)S(1)}, u32[]{:S(2)}, u32[]{:S(2)}) collective-permute-start(f32[327,192]{1,0:T(8,128)S(1)} %pad_maximum_fusion.27), channel_id=1, source_target_pairs={{0,8},{1,9},{2,10},{3,11},{4,12},{5,13},{6,14},{7,15},{8,0},{9,1},... | collective-permute-start | bytes 753416 | tf_op jit(solution)/shard_map/ppermute | solution.py:167
  375.7 12.1 %collective-permute-start.27 = (f32[165,192]{1,0:T(8,128)}, f32[165,192]{1,0:T(8,128)S(1)}, u32[]{:S(2)}, u32[]{:S(2)}) collective-permute-start(f32[165,192]{1,0:T(8,128)} %pad_maximum_fusion.28), channel_id=1, source_target_pairs={{0,16},{16,0},{32,48},{48,32},{64,80},{80,64},{1,17},{17,1},{33,49... | collective-permute-start | bytes 380168 | tf_op jit(solution)/shard_map/ppermute | solution.py:181
  391.6 19.9 %collective-permute-start.28 = (f32[57,192]{1,0:T(8,128)}, f32[57,192]{1,0:T(8,128)S(1)}, u32[]{:S(2)}, u32[]{:S(2)}) collective-permute-start(f32[57,192]{1,0:T(8,128)} %get-tuple-element.84), channel_id=1, source_target_pairs={{0,32},{16,48},{32,64},{48,80},{64,0},{80,16},{1,33},{17,49},{33,6... | collective-permute-start | bytes 131336 | tf_op jit(solution)/shard_map/ppermute | solution.py:191
  395.9 19.0 %collective-permute-start.29 = (f32[57,192]{1,0:T(8,128)S(1)}, f32[57,192]{1,0:T(8,128)}, u32[]{:S(2)}, u32[]{:S(2)}) collective-permute-start(f32[57,192]{1,0:T(8,128)S(1)} %get-tuple-element.85), channel_id=1, source_target_pairs={{0,64},{16,80},{32,0},{48,16},{64,32},{80,48},{1,65},{17,81},{33,1... | collective-permute-start | bytes 131336 | tf_op jit(solution)/shard_map/ppermute | solution.py:194
  416.5 5.0 %collective-permute-start.30 = (f32[57,192]{1,0:T(8,128)S(1)}, f32[57,192]{1,0:T(8,128)S(1)}, u32[]{:S(2)}, u32[]{:S(2)}) collective-permute-start(f32[57,192]{1,0:T(8,128)S(1)} %pad_maximum_fusion.39), channel_id=1, source_target_pairs={{0,96},{96,0},{192,288},{288,192},{384,480},{480,384},{576,672},{6... | collective-permute-start | bytes 131336 | tf_op jit(solution)/shard_map/ppermute | solution.py:27
  421.5 10.2 %collective-permute-start.31 = (f32[57,192]{1,0:T(8,128)S(1)}, f32[57,192]{1,0:T(8,128)S(1)}, u32[]{:S(2)}, u32[]{:S(2)}) collective-permute-start(f32[57,192]{1,0:T(8,128)S(1)} %fusion.7), channel_id=1, source_target_pairs={{0,192},{96,288},{192,0},{288,96},{384,576},{480,672},{576,384},{6... | collective-permute-start | bytes 131336 | tf_op jit(solution)/shard_map/ppermute | solution.py:27
  431.8 8.9 %collective-permute-start.32 = (f32[57,192]{1,0:T(8,128)S(1)}, f32[57,192]{1,0:T(8,128)S(1)}, u32[]{:S(2)}, u32[]{:S(2)}) collective-permute-start(f32[57,192]{1,0:T(8,128)S(1)} %add.269), channel_id=1, source_target_pairs={{0,384},{96,480},{192,576},{288,672},{384,0},{480,96},{576,192},{6... | collective-permute-start | bytes 131336 | tf_op jit(solution)/shard_map/ppermute | solution.py:27
  (32 other events, 504.9 us)

commit v4 on v3

--- a/solution.py
+++ b/solution.py
@@ -111,14 +111,35 @@
     return first, second, third
 
 
+def split_high(x):
+    scaled = x * 65537.0
+    return scaled - (scaled - x)
+
+
+def to_pieces(x):
+    high = split_high(x)
+    rest = x - high
+    middle = split_high(rest)
+    return jnp.concatenate([high, middle, rest - middle]).astype(jnp.bfloat16)
+
+
+def from_pieces(pieces):
+    high, middle, low = jnp.split(pieces.astype(jnp.float32), 3)
+    return (high + middle) + low
+
+
 def stats_and_weight(stats, weight):
+    extra = 3 * stats.shape[0]
+
+    def swap(weight, stats, axis, pairs):
+        got = lax.ppermute(jnp.concatenate([weight, to_pieces(stats)]), axis, pairs)
+        return got[:-extra], from_pieces(got[-extra:])
+
     count = lax.axis_size("cols")
     here = lax.axis_index("cols")
     step = 1
     while step < count:
-        pairs = [(i, i ^ step) for i in range(count)]
-        other_stats = lax.ppermute(stats, "cols", pairs)
-        other_weight = lax.ppermute(weight, "cols", pairs)
+        other_weight, other_stats = swap(weight, stats, "cols", [(i, i ^ step) for i in range(count)])
         stats = stats + other_stats
         low = (here // step) % 2 == 0
         weight = jnp.where(
@@ -129,21 +150,19 @@
         step *= 2
     count = lax.axis_size("rows")
     here = lax.axis_index("rows")
-    pairs = [(i, i ^ 1) for i in range(count)]
-    other_stats = lax.ppermute(stats, "rows", pairs)
-    other_weight = lax.ppermute(weight, "rows", pairs)
+    other_weight, other_stats = swap(weight, stats, "rows", [(i, i ^ 1) for i in range(count)])
     stats = stats + other_stats
     weight = jnp.where(
         here % 2 == 0,
         jnp.concatenate([weight, other_weight]),
         jnp.concatenate([other_weight, weight]),
     )
-    ahead_pairs = [(i, (i + 2) % count) for i in range(count)]
-    behind_pairs = [(i, (i + 4) % count) for i in range(count)]
-    ahead_stats = lax.ppermute(stats, "rows", ahead_pairs)
-    ahead_weight = lax.ppermute(weight, "rows", ahead_pairs)
-    behind_stats = lax.ppermute(stats, "rows", behind_pairs)
-    behind_weight = lax.ppermute(weight, "rows", behind_pairs)
+    ahead_weight, ahead_stats = swap(
+        weight, stats, "rows", [(i, (i + 2) % count) for i in range(count)]
+    )
+    behind_weight, behind_stats = swap(
+        weight, stats, "rows", [(i, (i + 4) % count) for i in range(count)]
+    )
     first, second, third = three_way(here // 2, stats, ahead_stats, behind_stats)
     stats = (first + second) + third
     weight = jnp.concatenate(three_way(here // 2, weight, ahead_weight, behind_weight))

time: 451 us -> 425 us (0.942)
  starting transfers between devices: 154 us -> 126 us
  waiting for transfers between devices: 137 us -> 129 us
  local copies, waits for them, and re-layouts: 102 us -> 108 us
  other arithmetic: 32.1 us -> 37.7 us
    ppermute x14 -> x7, starting transfers between devices: 64.9 us -> 35 us  [swap(): got = lax.ppermute(jnp.concatenate([weight, to_pieces(stats)]), axis, pairs)]
    ppermute x4, starting transfers between devices: 15.5 us -> 24.8 us  [reduce_grads(): lax.ppermute(jnp.concatenate([send.reshape(-1, channels), small]), 'cols'...]
    concatenate x0 -> x2, local copies, waits for them, and re-layouts: none -> 6.19 us  [swap(): got = lax.ppermute(jnp.concatenate([weight, to_pieces(stats)]), axis, pairs)]
    ppermute x1, waiting for transfers between devices: 10.2 us -> 4.38 us  [reduce_grads(): lax.ppermute(jnp.concatenate([send.reshape(-1, channels), small]), 'rows'...]
    ppermute x1, starting transfers between devices: 13.9 us -> 8.69 us  [reduce_grads(): lax.ppermute(jnp.concatenate([to_after, small]), 'rows', [(i, (i + 4) % c...]
    unnamed x66 -> x72, local copies, waits for them, and re-layouts: 6.8 us -> 12 us
    ppermute x4, waiting for transfers between devices: 56.1 us -> 60.9 us  [reduce_grads(): lax.ppermute(jnp.concatenate([send.reshape(-1, channels), small]), 'cols'...]
    another operation x3 -> x13, other arithmetic: 8.27 us -> 10.3 us
  transfers between devices with their start and end apart: 33 -> 26, of which waited for: 25 -> 17; matrix products, arithmetic and copies ran while one was open for 17% -> 11% of each run, Pallas kernels for 0% -> 0%
where the time goes in v4:
time: 425 us; the launch traced here: 417 us
  waiting for transfers between devices  129 us (30%)
  starting transfers between devices  126 us (30%)
  local copies, waits for them, and re-layouts  108 us (25%)
  other arithmetic  37.7 us (9%)
  matrix products  14.7 us (3%)
    ppermute x4, waiting for transfers between devices, reduce_grads(): lax.ppermute(jnp.concatenate([send.reshape(-1, channels), small]), 'cols'...  60.9 us
    ppermute x7, waiting for transfers between devices, swap(): got = lax.ppermute(jnp.concatenate([weight, to_pieces(stats)]), axis, pairs)  48.5 us
    ppermute x7, starting transfers between devices, swap(): got = lax.ppermute(jnp.concatenate([weight, to_pieces(stats)]), axis, pairs)  35 us
    ppermute x6, starting transfers between devices, xor_sum(): x = x + lax.ppermute(x, axis, [(i, i ^ step) for i in range(n)])  27.1 us
    ppermute x4, starting transfers between devices, reduce_grads(): lax.ppermute(jnp.concatenate([send.reshape(-1, channels), small]), 'cols'...  24.8 us
    ppermute x3, starting transfers between devices, padded_2(): lax.ppermute(lax.slice_in_dim(block, block.shape[dim] - width, None, axis...  22 us
    concatenate x4, local copies, waits for them, and re-layouts, reduce_grads(): jnp.concatenate([send.reshape(-1, channels), small])  12.3 us
    unnamed x72, local copies, waits for them, and re-layouts  12 us
  transfers between devices with their start and end apart: 26, of which 17 were waited for; matrix products, arithmetic and copies ran while one was open for 11% of the time, Pallas kernels for 0%

profile of v4, /device:TPU:1, one launch (start us, length us, event | category | flops | bytes accessed | tf_op | source)
XLA Modules:
  0.0 417.4 jit_solution(7573527103762327774)
XLA Ops:
  9.1 9.7 %collective-permute-start.6 = (bf16[60,192]{1,0:T(8,128)(2,1)S(1)}, bf16[60,192]{1,0:T(8,128)(2,1)S(1)}, u32[]{:S(2)}, u32[]{:S(2)}) collective-permute-start(bf16[60,192]{1,0:T(8,128)(2,1)S(1)} %pad_maximum_fusion.44), channel_id=1, source_target_pairs={{0,1},{1,0},{2,3},{3,2},{4,5},{5,4},{6,7},{7,6},{8,9},{9,8},{10,11... | collective-permute-start | bytes 69128 | tf_op jit(solution)/shard_map/ppermute | solution.py:135
  26.7 5.1 %collective-permute-done.8 = bf16[222,192]{1,0:T(8,128)(2,1)S(1)} collective-permute-done((bf16[222,192]{1,0:T(8,128)(2,1)S(1)}, bf16[222,192]{1,0:T(8,128)(2,1)S(1)}, u32[]{:S(2)}, u32[]{:S(2)}) %collective-permute-start.8) | collective-permute-done | bytes 85280 | tf_op jit(solution)/shard_map/ppermute | solution.py:135
  32.0 8.4 %collective-permute-start.9 = (bf16[438,192]{1,0:T(8,128)(2,1)S(1)}, bf16[438,192]{1,0:T(8,128)(2,1)S(1)}, u32[]{:S(2)}, u32[]{:S(2)}) collective-permute-start(bf16[438,192]{1,0:T(8,128)(2,1)S(1)} %pad_maximum_fusion.29), channel_id=1, source_target_pairs={{0,8},{1,9},{2,10},{3,11},{4,12},{5,13},{6,14},{7,15},{8,0},{9,1},... | collective-permute-start | bytes 504584 | tf_op jit(solution)/shard_map/ppermute | solution.py:135
  41.1 4.8 %collective-permute-done.9 = bf16[438,192]{1,0:T(8,128)(2,1)S(1)} collective-permute-done((bf16[438,192]{1,0:T(8,128)(2,1)S(1)}, bf16[438,192]{1,0:T(8,128)(2,1)S(1)}, u32[]{:S(2)}, u32[]{:S(2)}) %collective-permute-start.9) | collective-permute-done | bytes 168224 | tf_op jit(solution)/shard_map/ppermute | solution.py:135
  46.2 7.6 %collective-permute-start.2 = (bf16[3,1,16,768]{3,2,1,0:T(8,128)(2,1)S(1)}, bf16[3,1,16,768]{3,2,1,0:T(8,128)(2,1)S(1)}, u32[]{:S(2)}, u32[]{:S(2)}) collective-permute-start(bf16[3,1,16,768]{3,2,1,0:T(8,128)(2,1)S(1)} %get-tuple-element.28), channel_id=1, source_target_pairs={{0,16},{16,32},{32,48},{48,64},{64,80},{1,17},{17,33},{33,49},{49,... | collective-permute-start | bytes 221192 | tf_op jit(solution)/shard_map/ppermute | solution.py:15
  60.3 10.4 %collective-permute-start.4 = (bf16[3,18,1,768]{3,2,1,0:T(2,128)(2,1)S(1)}, bf16[3,18,1,768]{3,2,1,0:T(2,128)(2,1)S(1)}, u32[]{:S(2)}, u32[]{:S(2)}) collective-permute-start(bf16[3,18,1,768]{3,2,1,0:T(2,128)(2,1)S(1)} %get-tuple-element.26), channel_id=1, source_target_pairs={{0,1},{1,2},{2,3},{3,4},{4,5},{5,6},{6,7},{7,8},{8,9},{9,10},{10,1... | collective-permute-start | bytes 248840 | tf_op jit(solution)/shard_map/ppermute | solution.py:15
  72.9 4.4 %collective-permute-done.5 = bf16[3,18,1,768]{3,2,1,0:T(2,128)(2,1)S(1)} collective-permute-done((bf16[3,18,1,768]{3,2,1,0:T(2,128)(2,1)S(1)}, bf16[3,18,1,768]{3,2,1,0:T(2,128)(2,1)S(1)}, u32[]{:S(2)}, u32[]{:S(2)}) %collective-permute-start.5) | collective-permute-done | bytes 82976 | tf_op jit(solution)/shard_map/ppermute | solution.py:18
  95.7 5.3 %collective-permute-start.12 = (bf16[1734,192]{0,1:T(8,128)(2,1)}, bf16[1734,192]{0,1:T(8,128)(2,1)}, u32[]{:S(2)}, u32[]{:S(2)}) collective-permute-start(bf16[1734,192]{0,1:T(8,128)(2,1)} %copy.44), channel_id=1, source_target_pairs={{0,64},{16,80},{32,0},{48,16},{64,32},{80,48},{1,65},{17,81},{33,1... | collective-permute-start | bytes 1997576 | tf_op jit(solution)/shard_map/ppermute | solution.py:135
  104.8 10.3 %concatenate.144 = bf16[2,16,16,5184]{3,2,1,0:T(8,128)(2,1)} concatenate(bf16[2,16,16,192]{3,2,1,0:T(8,128)(2,1)} %get-tuple-element.59, bf16[2,16,16,192]{3,2,1,0:T(8,128)(2,1)} %get-tuple-element.58, bf16[2,16,16,192]{3,2,1,0:T(8,128)(2,1)} %get-tuple-element.57, bf16[2,16,16,192]{3,2,1,0:T(8,128)(2,1)} %get-tuple-element.56, bf16[2,16,16,192]{3,2,1,0:T(8,128)(2,1)} %get-tuple-element.55, ...), dimensions={3} | concatenate | bytes 10616832 | tf_op jit(solution)/shard_map/concatenate | solution.py:306
  115.1 5.1 %fusion.2 = bf16[2,36,18,192]{3,2,1,0:T(8,128)(2,1)} fusion(bf16[3,18,1,768]{3,2,1,0:T(2,128)(2,1)S(1)} %copy-done.20, bf16[3,18,1,768]{3,2,1,0:T(2,128)(2,1)S(1)} %copy-done.18, bf16[3,1,16,768]{3,2,1,0:T(8,128)(2,1)S(1)} %copy-done.22, bf16[3,1,16,768]{3,2,1,0:T(8,128)(2,1)S(1)} %collective-permute-done.2, ...), kind=kLoop, calls=%fused_computation.24 | loop fusion | flops 6967296 | bytes 1990656 | tf_op jit(solution)/shard_map/concatenate.1
  120.2 21.6 %collective-permute-done.11 = bf16[1734,192]{0,1:T(8,128)(2,1)} collective-permute-done((bf16[1734,192]{0,1:T(8,128)(2,1)}, bf16[1734,192]{0,1:T(8,128)(2,1)}, u32[]{:S(2)}, u32[]{:S(2)}) %collective-permute-start.11) | collective-permute-done | bytes 665888 | tf_op jit(solution)/shard_map/ppermute | solution.py:135
  143.3 13.3 %collective-permute-done.12 = bf16[1734,192]{0,1:T(8,128)(2,1)} collective-permute-done((bf16[1734,192]{0,1:T(8,128)(2,1)}, bf16[1734,192]{0,1:T(8,128)(2,1)}, u32[]{:S(2)}, u32[]{:S(2)}) %collective-permute-start.12) | collective-permute-done | bytes 665888 | tf_op jit(solution)/shard_map/ppermute | solution.py:135
  160.8 4.3 %collective-permute-start.13 = (f32[2,192]{1,0:T(2,128)S(1)}, f32[2,192]{1,0:T(2,128)S(1)}, u32[]{:S(2)}, u32[]{:S(2)}) collective-permute-start(f32[2,192]{1,0:T(2,128)S(1)} %select_add_fusion.1), channel_id=1, source_target_pairs={{0,96},{96,0},{192,288},{288,192},{384,480},{480,384},{576,672},{6... | collective-permute-start | bytes 4616 | tf_op jit(solution)/shard_map/ppermute | solution.py:27
  166.5 5.2 %collective-permute-start.14 = (f32[2,192]{1,0:T(2,128)S(1)}, f32[2,192]{1,0:T(2,128)S(1)}, u32[]{:S(2)}, u32[]{:S(2)}) collective-permute-start(f32[2,192]{1,0:T(2,128)S(1)} %add.280), channel_id=1, source_target_pairs={{0,192},{96,288},{192,0},{288,96},{384,576},{480,672},{576,384},{6... | collective-permute-start | bytes 4616 | tf_op jit(solution)/shard_map/ppermute | solution.py:27
  175.7 5.0 %collective-permute-start.15 = (f32[2,192]{1,0:T(2,128)S(1)}, f32[2,192]{1,0:T(2,128)S(1)}, u32[]{:S(2)}, u32[]{:S(2)}) collective-permute-start(f32[2,192]{1,0:T(2,128)S(1)} %add.281), channel_id=1, source_target_pairs={{0,384},{96,480},{192,576},{288,672},{384,0},{480,96},{576,192},{6... | collective-permute-start | bytes 4616 | tf_op jit(solution)/shard_map/ppermute | solution.py:27
  180.7 5.3 %convolution_convert_fusion = bf16[512,192]{0,1:T(8,128)(2,1)S(1)} fusion(bf16[512,5184]{1,0:T(8,128)(2,1)} %bitcast.63, bf16[5184,192]{1,0:T(8,128)(2,1)} %bitcast.66), kind=kOutput, calls=%fused_computation.9 | convolution fusion | flops 1019314176 | bytes 7495680 | tf_op jit(solution)/shard_map/dot_general | solution.py:318
  193.2 9.5 %concatenate.141 = bf16[2,16,16,5184]{3,2,1,0:T(8,128)(2,1)} concatenate(bf16[2,16,16,192]{3,2,1,0:T(8,128)(2,1)} %get-tuple-element.86, bf16[2,16,16,192]{3,2,1,0:T(8,128)(2,1)} %get-tuple-element.85, bf16[2,16,16,192]{3,2,1,0:T(8,128)(2,1)} %get-tuple-element.84, bf16[2,16,16,192]{3,2,1,0:T(8,128)(2,1)} %get-tuple-element.83, bf16[2,16,16,192]{3,2,1,0:T(8,128)(2,1)} %get-tuple-element.82, ...), dimensions={3} | concatenate | bytes 10616832 | tf_op jit(solution)/shard_map/concatenate | solution.py:305
  202.8 8.1 %copy.53 = bf16[512,5184]{0,1:T(8,128)(2,1)} copy(bf16[512,5184]{1,0:T(8,128)(2,1)} %bitcast.61) | data formatting | bytes 10616832 | tf_op jit(solution)/shard_map/reshape | solution.py:305
  210.9 7.6 %dot_general.16 = bf16[6,2,2,2,2,54,512]{6,5,4,3,2,1,0:T(8,128)(2,1)} reshape(bf16[5184,512]{1,0:T(8,128)(2,1)} %bitcast.64) | data formatting | bytes 10616832 | tf_op jit(solution)/shard_map/dot_general | solution.py:312
  229.7 6.2 %concatenate.145 = f32[2595,192]{1,0:T(8,128)S(1)} concatenate(f32[2592,192]{1,0:T(8,128)} %reshape.249, f32[1,192]{1,0:T(1,128)S(1)} %bitcast.80, f32[1,192]{1,0:T(1,128)S(1)} %bitcast.77, f32[1,192]{1,0:T(1,128)S(1)} %bitcast.83), dimensions={0} | concatenate | bytes 3985920 | tf_op jit(solution)/shard_map/concatenate | solution.py:187
  264.9 5.2 %collective-permute-start.17 = (f32[1299,192]{0,1:T(8,128)}, f32[1299,192]{0,1:T(8,128)}, u32[]{:S(2)}, u32[]{:S(2)}) collective-permute-start(f32[1299,192]{0,1:T(8,128)} %copy.58), channel_id=1, source_target_pairs={{0,2},{1,3},{2,0},{3,1},{4,6},{5,7},{6,4},{7,5},{8,10},{9,11},{10,... | collective-permute-start | bytes 2992904 | tf_op jit(solution)/shard_map/ppermute | solution.py:186
  270.2 24.2 %collective-permute-done.17 = f32[1299,192]{0,1:T(8,128)} collective-permute-done((f32[1299,192]{0,1:T(8,128)}, f32[1299,192]{0,1:T(8,128)}, u32[]{:S(2)}, u32[]{:S(2)}) %collective-permute-start.17) | collective-permute-done | bytes 997664 | tf_op jit(solution)/shard_map/ppermute | solution.py:186
  304.6 7.9 %collective-permute-start.18 = (f32[651,192]{0,1:T(8,128)}, f32[651,192]{0,1:T(8,128)S(1)}, u32[]{:S(2)}, u32[]{:S(2)}) collective-permute-start(f32[651,192]{0,1:T(8,128)} %copy.61), channel_id=1, source_target_pairs={{0,4},{1,5},{2,6},{3,7},{4,0},{5,1},{6,2},{7,3},{8,12},{9,13},{10,... | collective-permute-start | bytes 1499912 | tf_op jit(solution)/shard_map/ppermute | solution.py:186
  312.6 12.9 %collective-permute-done.18 = f32[651,192]{0,1:T(8,128)S(1)} collective-permute-done((f32[651,192]{0,1:T(8,128)}, f32[651,192]{0,1:T(8,128)S(1)}, u32[]{:S(2)}, u32[]{:S(2)}) %collective-permute-start.18) | collective-permute-done | bytes 500000 | tf_op jit(solution)/shard_map/ppermute | solution.py:186
  328.0 7.6 %collective-permute-start.19 = (f32[327,192]{1,0:T(8,128)S(1)}, f32[327,192]{1,0:T(8,128)S(1)}, u32[]{:S(2)}, u32[]{:S(2)}) collective-permute-start(f32[327,192]{1,0:T(8,128)S(1)} %pad_maximum_fusion.28), channel_id=1, source_target_pairs={{0,8},{1,9},{2,10},{3,11},{4,12},{5,13},{6,14},{7,15},{8,0},{9,1},... | collective-permute-start | bytes 753416 | tf_op jit(solution)/shard_map/ppermute | solution.py:186
  335.6 19.9 %collective-permute-done.19 = f32[327,192]{1,0:T(8,128)S(1)} collective-permute-done((f32[327,192]{1,0:T(8,128)S(1)}, f32[327,192]{1,0:T(8,128)S(1)}, u32[]{:S(2)}, u32[]{:S(2)}) %collective-permute-start.19) | collective-permute-done | bytes 251168 | tf_op jit(solution)/shard_map/ppermute | solution.py:186
  362.2 4.4 %collective-permute-done.20 = f32[165,192]{1,0:T(8,128)S(1)} collective-permute-done((f32[165,192]{1,0:T(8,128)}, f32[165,192]{1,0:T(8,128)S(1)}, u32[]{:S(2)}, u32[]{:S(2)}) %collective-permute-start.20) | collective-permute-done | bytes 126752 | tf_op jit(solution)/shard_map/ppermute | solution.py:200
  372.3 8.7 %collective-permute-start.22 = (f32[57,192]{1,0:T(8,128)S(1)}, f32[57,192]{1,0:T(8,128)}, u32[]{:S(2)}, u32[]{:S(2)}) collective-permute-start(f32[57,192]{1,0:T(8,128)S(1)} %get-tuple-element.95), channel_id=1, source_target_pairs={{0,64},{16,80},{32,0},{48,16},{64,32},{80,48},{1,65},{17,81},{33,1... | collective-permute-start | bytes 131336 | tf_op jit(solution)/shard_map/ppermute | solution.py:213
  386.4 5.4 %collective-permute-start.23 = (f32[57,192]{1,0:T(8,128)S(1)}, f32[57,192]{1,0:T(8,128)S(1)}, u32[]{:S(2)}, u32[]{:S(2)}) collective-permute-start(f32[57,192]{1,0:T(8,128)S(1)} %pad_maximum_fusion.42), channel_id=1, source_target_pairs={{0,96},{96,0},{192,288},{288,192},{384,480},{480,384},{576,672},{6... | collective-permute-start | bytes 131336 | tf_op jit(solution)/shard_map/ppermute | solution.py:27
  393.5 4.3 %collective-permute-start.24 = (f32[57,192]{1,0:T(8,128)S(1)}, f32[57,192]{1,0:T(8,128)S(1)}, u32[]{:S(2)}, u32[]{:S(2)}) collective-permute-start(f32[57,192]{1,0:T(8,128)S(1)} %fusion.29), channel_id=1, source_target_pairs={{0,192},{96,288},{192,0},{288,96},{384,576},{480,672},{576,384},{6... | collective-permute-start | bytes 131336 | tf_op jit(solution)/shard_map/ppermute | solution.py:27
  397.9 5.2 %convolution_add_fusion = f32[512,192]{0,1:T(8,128)} fusion(bf16[512,5184]{1,0:T(8,128)(2,1)} %bitcast.62, f32[192]{0:T(256)S(1)} %copy-done.31, bf16[1728,192]{1,0:T(8,128)(2,1)S(1)} %copy-done.9, bf16[1728,192]{1,0:T(8,128)(2,1)S(1)} %copy-done.11, bf16[1728,192]{1,0:T(8,128)(2,1)S(1)} %copy-done.7), kind=kOutput, calls=%fused_computation.8 | convolution fusion | flops 1025286144 | bytes 7693056 | tf_op jit(solution)/shard_map/dot_general | solution.py:307
  408.1 5.2 %collective-permute-done.25 = f32[57,192]{1,0:T(8,128)S(1)} collective-permute-done((f32[57,192]{1,0:T(8,128)S(1)}, f32[57,192]{1,0:T(8,128)S(1)}, u32[]{:S(2)}, u32[]{:S(2)}) %collective-permute-start.25) | collective-permute-done | bytes 43808 | tf_op jit(solution)/shard_map/ppermute | solution.py:27
  (243 shorter events, 147.2 us)
Async XLA Ops:
  3.6 42.6 %collective-permute-start = (bf16[1,16,16,768]{3,2,1,0:T(8,128)(2,1)S(1)}, bf16[1,16,16,768]{3,2,1,0:T(8,128)(2,1)S(1)}, u32[]{:S(2)}, u32[]{:S(2)}) collective-permute-start(bf16[1,16,16,768]{3,2,1,0:T(8,128)(2,1)S(1)} %constant_dynamic-update-slice_fusion), channel_id=1, source_target_pairs={{0,96},{96,192},{192,288},{288,384},{384,480},{480,576},{576,672},... | collective-permute-start | bytes 1179656 | tf_op jit(solution)/shard_map/ppermute | solution.py:15
  7.6 38.6 %collective-permute-start.1 = (bf16[1,16,16,768]{3,2,1,0:T(8,128)(2,1)S(1)}, bf16[1,16,16,768]{3,2,1,0:T(8,128)(2,1)S(1)}, u32[]{:S(2)}, u32[]{:S(2)}) collective-permute-start(bf16[1,16,16,768]{3,2,1,0:T(8,128)(2,1)S(1)} %constant_dynamic-update-slice_fusion), channel_id=1, source_target_pairs={{96,0},{192,96},{288,192},{384,288},{480,384},{576,480},{672,576},... | collective-permute-start | bytes 1179656 | tf_op jit(solution)/shard_map/ppermute | solution.py:18
  9.1 10.5 %collective-permute-start.6 = (bf16[60,192]{1,0:T(8,128)(2,1)S(1)}, bf16[60,192]{1,0:T(8,128)(2,1)S(1)}, u32[]{:S(2)}, u32[]{:S(2)}) collective-permute-start(bf16[60,192]{1,0:T(8,128)(2,1)S(1)} %pad_maximum_fusion.44), channel_id=1, source_target_pairs={{0,1},{1,0},{2,3},{3,2},{4,5},{5,4},{6,7},{7,6},{8,9},{9,8},{10,11... | collective-permute-start | bytes 69128 | tf_op jit(solution)/shard_map/ppermute | solution.py:135
  19.7 5.0 %collective-permute-start.7 = (bf16[114,192]{1,0:T(8,128)(2,1)S(1)}, bf16[114,192]{1,0:T(8,128)(2,1)S(1)}, u32[]{:S(2)}, u32[]{:S(2)}) collective-permute-start(bf16[114,192]{1,0:T(8,128)(2,1)S(1)} %pad_maximum_fusion.43), channel_id=1, source_target_pairs={{0,2},{1,3},{2,0},{3,1},{4,6},{5,7},{6,4},{7,5},{8,10},{9,11},{10,... | collective-permute-start | bytes 131336 | tf_op jit(solution)/shard_map/ppermute | solution.py:135
  24.8 7.0 %collective-permute-start.8 = (bf16[222,192]{1,0:T(8,128)(2,1)S(1)}, bf16[222,192]{1,0:T(8,128)(2,1)S(1)}, u32[]{:S(2)}, u32[]{:S(2)}) collective-permute-start(bf16[222,192]{1,0:T(8,128)(2,1)S(1)} %pad_maximum_fusion.36), channel_id=1, source_target_pairs={{0,4},{1,5},{2,6},{3,7},{4,0},{5,1},{6,2},{7,3},{8,12},{9,13},{10,... | collective-permute-start | bytes 255752 | tf_op jit(solution)/shard_map/ppermute | solution.py:135
  32.0 13.9 %collective-permute-start.9 = (bf16[438,192]{1,0:T(8,128)(2,1)S(1)}, bf16[438,192]{1,0:T(8,128)(2,1)S(1)}, u32[]{:S(2)}, u32[]{:S(2)}) collective-permute-start(bf16[438,192]{1,0:T(8,128)(2,1)S(1)} %pad_maximum_fusion.29), channel_id=1, source_target_pairs={{0,8},{1,9},{2,10},{3,11},{4,12},{5,13},{6,14},{7,15},{8,0},{9,1},... | collective-permute-start | bytes 504584 | tf_op jit(solution)/shard_map/ppermute | solution.py:135
  46.1 26.5 %copy-start.3 = (bf16[2,16,16,192]{3,2,1,0:T(8,128)(2,1)S(1)}, bf16[2,16,16,192]{3,2,1,0:T(8,128)(2,1)}, u32[]{:S(2)}) copy-start(bf16[2,16,16,192]{3,2,1,0:T(8,128)(2,1)} %param.7) | copy-start | bytes 589828
  46.2 13.8 %collective-permute-start.2 = (bf16[3,1,16,768]{3,2,1,0:T(8,128)(2,1)S(1)}, bf16[3,1,16,768]{3,2,1,0:T(8,128)(2,1)S(1)}, u32[]{:S(2)}, u32[]{:S(2)}) collective-permute-start(bf16[3,1,16,768]{3,2,1,0:T(8,128)(2,1)S(1)} %get-tuple-element.28), channel_id=1, source_target_pairs={{0,16},{16,32},{32,48},{48,64},{64,80},{1,17},{17,33},{33,49},{49,... | collective-permute-start | bytes 221192 | tf_op jit(solution)/shard_map/ppermute | solution.py:15
  53.8 6.2 %collective-permute-start.3 = (bf16[3,1,16,768]{3,2,1,0:T(8,128)(2,1)S(1)}, bf16[3,1,16,768]{3,2,1,0:T(8,128)(2,1)S(1)}, u32[]{:S(2)}, u32[]{:S(2)}) collective-permute-start(bf16[3,1,16,768]{3,2,1,0:T(8,128)(2,1)S(1)} %get-tuple-element.29), channel_id=1, source_target_pairs={{16,0},{32,16},{48,32},{64,48},{80,64},{17,1},{33,17},{49,33},{65,... | collective-permute-start | bytes 221192 | tf_op jit(solution)/shard_map/ppermute | solution.py:18
  56.0 25.3 %collective-permute-start.10 = (bf16[870,192]{1,0:T(8,128)(2,1)}, bf16[870,192]{1,0:T(8,128)(2,1)}, u32[]{:S(2)}, u32[]{:S(2)}) collective-permute-start(bf16[870,192]{1,0:T(8,128)(2,1)} %pad_maximum_fusion.27), channel_id=1, source_target_pairs={{0,16},{16,0},{32,48},{48,32},{64,80},{80,64},{1,17},{17,1},{33,49... | collective-permute-start | bytes 1002248 | tf_op jit(solution)/shard_map/ppermute | solution.py:135
  60.3 12.7 %collective-permute-start.4 = (bf16[3,18,1,768]{3,2,1,0:T(2,128)(2,1)S(1)}, bf16[3,18,1,768]{3,2,1,0:T(2,128)(2,1)S(1)}, u32[]{:S(2)}, u32[]{:S(2)}) collective-permute-start(bf16[3,18,1,768]{3,2,1,0:T(2,128)(2,1)S(1)} %get-tuple-element.26), channel_id=1, source_target_pairs={{0,1},{1,2},{2,3},{3,4},{4,5},{5,6},{6,7},{7,8},{8,9},{9,10},{10,1... | collective-permute-start | bytes 248840 | tf_op jit(solution)/shard_map/ppermute | solution.py:15
  70.7 6.7 %collective-permute-start.5 = (bf16[3,18,1,768]{3,2,1,0:T(2,128)(2,1)S(1)}, bf16[3,18,1,768]{3,2,1,0:T(2,128)(2,1)S(1)}, u32[]{:S(2)}, u32[]{:S(2)}) collective-permute-start(bf16[3,18,1,768]{3,2,1,0:T(2,128)(2,1)S(1)} %get-tuple-element.27), channel_id=1, source_target_pairs={{1,0},{2,1},{3,2},{4,3},{5,4},{6,5},{7,6},{8,7},{9,8},{10,9},{11,1... | collective-permute-start | bytes 248840 | tf_op jit(solution)/shard_map/ppermute | solution.py:18
  91.8 50.1 %collective-permute-start.11 = (bf16[1734,192]{0,1:T(8,128)(2,1)}, bf16[1734,192]{0,1:T(8,128)(2,1)}, u32[]{:S(2)}, u32[]{:S(2)}) collective-permute-start(bf16[1734,192]{0,1:T(8,128)(2,1)} %copy.44), channel_id=1, source_target_pairs={{0,32},{16,48},{32,64},{48,80},{64,0},{80,16},{1,33},{17,49},{33,6... | collective-permute-start | bytes 1997576 | tf_op jit(solution)/shard_map/ppermute | solution.py:135
  95.7 60.9 %collective-permute-start.12 = (bf16[1734,192]{0,1:T(8,128)(2,1)}, bf16[1734,192]{0,1:T(8,128)(2,1)}, u32[]{:S(2)}, u32[]{:S(2)}) collective-permute-start(bf16[1734,192]{0,1:T(8,128)(2,1)} %copy.44), channel_id=1, source_target_pairs={{0,64},{16,80},{32,0},{48,16},{64,32},{80,48},{1,65},{17,81},{33,1... | collective-permute-start | bytes 1997576 | tf_op jit(solution)/shard_map/ppermute | solution.py:135
  160.8 5.7 %collective-permute-start.13 = (f32[2,192]{1,0:T(2,128)S(1)}, f32[2,192]{1,0:T(2,128)S(1)}, u32[]{:S(2)}, u32[]{:S(2)}) collective-permute-start(f32[2,192]{1,0:T(2,128)S(1)} %select_add_fusion.1), channel_id=1, source_target_pairs={{0,96},{96,0},{192,288},{288,192},{384,480},{480,384},{576,672},{6... | collective-permute-start | bytes 4616 | tf_op jit(solution)/shard_map/ppermute | solution.py:27
  166.5 9.1 %collective-permute-start.14 = (f32[2,192]{1,0:T(2,128)S(1)}, f32[2,192]{1,0:T(2,128)S(1)}, u32[]{:S(2)}, u32[]{:S(2)}) collective-permute-start(f32[2,192]{1,0:T(2,128)S(1)} %add.280), channel_id=1, source_target_pairs={{0,192},{96,288},{192,0},{288,96},{384,576},{480,672},{576,384},{6... | collective-permute-start | bytes 4616 | tf_op jit(solution)/shard_map/ppermute | solution.py:27
  175.7 11.3 %collective-permute-start.15 = (f32[2,192]{1,0:T(2,128)S(1)}, f32[2,192]{1,0:T(2,128)S(1)}, u32[]{:S(2)}, u32[]{:S(2)}) collective-permute-start(f32[2,192]{1,0:T(2,128)S(1)} %add.281), channel_id=1, source_target_pairs={{0,384},{96,480},{192,576},{288,672},{384,0},{480,96},{576,192},{6... | collective-permute-start | bytes 4616 | tf_op jit(solution)/shard_map/ppermute | solution.py:27
  238.1 8.0 %collective-permute-start.16 = (f32[2595,192]{0,1:T(8,128)}, f32[2595,192]{0,1:T(8,128)S(1)}, u32[]{:S(2)}, u32[]{:S(2)}) collective-permute-start(f32[2595,192]{0,1:T(8,128)} %copy.55), channel_id=1, source_target_pairs={{0,1},{1,0},{2,3},{3,2},{4,5},{5,4},{6,7},{7,6},{8,9},{9,8},{10,11... | collective-permute-start | bytes 5978888 | tf_op jit(solution)/shard_map/ppermute | solution.py:186
  264.9 29.4 %collective-permute-start.17 = (f32[1299,192]{0,1:T(8,128)}, f32[1299,192]{0,1:T(8,128)}, u32[]{:S(2)}, u32[]{:S(2)}) collective-permute-start(f32[1299,192]{0,1:T(8,128)} %copy.58), channel_id=1, source_target_pairs={{0,2},{1,3},{2,0},{3,1},{4,6},{5,7},{6,4},{7,5},{8,10},{9,11},{10,... | collective-permute-start | bytes 2992904 | tf_op jit(solution)/shard_map/ppermute | solution.py:186
  303.5 23.1 %copy-start.2 = (f32[6,2,2,54,192]{4,3,2,1,0:T(8,128)S(1)}, f32[6,2,2,54,192]{4,3,2,1,0:T(8,128)}, u32[]{:S(2)}) copy-start(f32[6,2,2,54,192]{4,3,2,1,0:T(8,128)} %copy-done.1) | copy-start | bytes 2985988
  304.6 20.9 %collective-permute-start.18 = (f32[651,192]{0,1:T(8,128)}, f32[651,192]{0,1:T(8,128)S(1)}, u32[]{:S(2)}, u32[]{:S(2)}) collective-permute-start(f32[651,192]{0,1:T(8,128)} %copy.61), channel_id=1, source_target_pairs={{0,4},{1,5},{2,6},{3,7},{4,0},{5,1},{6,2},{7,3},{8,12},{9,13},{10,... | collective-permute-start | bytes 1499912 | tf_op jit(solution)/shard_map/ppermute | solution.py:186
  328.0 27.5 %collective-permute-start.19 = (f32[327,192]{1,0:T(8,128)S(1)}, f32[327,192]{1,0:T(8,128)S(1)}, u32[]{:S(2)}, u32[]{:S(2)}) collective-permute-start(f32[327,192]{1,0:T(8,128)S(1)} %pad_maximum_fusion.28), channel_id=1, source_target_pairs={{0,8},{1,9},{2,10},{3,11},{4,12},{5,13},{6,14},{7,15},{8,0},{9,1},... | collective-permute-start | bytes 753416 | tf_op jit(solution)/shard_map/ppermute | solution.py:186
  357.1 40.8 %copy-start.7 = (bf16[1728,192]{1,0:T(8,128)(2,1)S(1)}, bf16[1728,192]{1,0:T(8,128)(2,1)}, u32[]{:S(2)}) copy-start(bf16[1728,192]{1,0:T(8,128)(2,1)} %copy-done.6) | copy-start | bytes 1990660
  357.1 40.8 %copy-start.9 = (bf16[1728,192]{1,0:T(8,128)(2,1)S(1)}, bf16[1728,192]{1,0:T(8,128)(2,1)}, u32[]{:S(2)}) copy-start(bf16[1728,192]{1,0:T(8,128)(2,1)} %copy-done.8) | copy-start | bytes 1990660
  357.1 40.8 %copy-start.11 = (bf16[1728,192]{1,0:T(8,128)(2,1)S(1)}, bf16[1728,192]{1,0:T(8,128)(2,1)}, u32[]{:S(2)}) copy-start(bf16[1728,192]{1,0:T(8,128)(2,1)} %copy-done.10) | copy-start | bytes 1990660
  357.1 40.8 %copy-start.31 = (f32[192]{0:T(256)S(1)}, f32[192]{0:T(256)}, u32[]{:S(2)}) copy-start(f32[192]{0:T(256)} %param.11) | copy-start | bytes 2308
  360.3 6.3 %collective-permute-start.20 = (f32[165,192]{1,0:T(8,128)}, f32[165,192]{1,0:T(8,128)S(1)}, u32[]{:S(2)}, u32[]{:S(2)}) collective-permute-start(f32[165,192]{1,0:T(8,128)} %pad_maximum_fusion.30), channel_id=1, source_target_pairs={{0,16},{16,0},{32,48},{48,32},{64,80},{80,64},{1,17},{17,1},{33,49... | collective-permute-start | bytes 380168 | tf_op jit(solution)/shard_map/ppermute | solution.py:200
  370.4 11.0 %collective-permute-start.21 = (f32[57,192]{1,0:T(8,128)}, f32[57,192]{1,0:T(8,128)S(1)}, u32[]{:S(2)}, u32[]{:S(2)}) collective-permute-start(f32[57,192]{1,0:T(8,128)} %get-tuple-element.94), channel_id=1, source_target_pairs={{0,32},{16,48},{32,64},{48,80},{64,0},{80,16},{1,33},{17,49},{33,6... | collective-permute-start | bytes 131336 | tf_op jit(solution)/shard_map/ppermute | solution.py:210
  372.3 12.5 %collective-permute-start.22 = (f32[57,192]{1,0:T(8,128)S(1)}, f32[57,192]{1,0:T(8,128)}, u32[]{:S(2)}, u32[]{:S(2)}) collective-permute-start(f32[57,192]{1,0:T(8,128)S(1)} %get-tuple-element.95), channel_id=1, source_target_pairs={{0,64},{16,80},{32,0},{48,16},{64,32},{80,48},{1,65},{17,81},{33,1... | collective-permute-start | bytes 131336 | tf_op jit(solution)/shard_map/ppermute | solution.py:213
  386.4 7.1 %collective-permute-start.23 = (f32[57,192]{1,0:T(8,128)S(1)}, f32[57,192]{1,0:T(8,128)S(1)}, u32[]{:S(2)}, u32[]{:S(2)}) collective-permute-start(f32[57,192]{1,0:T(8,128)S(1)} %pad_maximum_fusion.42), channel_id=1, source_target_pairs={{0,96},{96,0},{192,288},{288,192},{384,480},{480,384},{576,672},{6... | collective-permute-start | bytes 131336 | tf_op jit(solution)/shard_map/ppermute | solution.py:27
  393.5 10.8 %collective-permute-start.24 = (f32[57,192]{1,0:T(8,128)S(1)}, f32[57,192]{1,0:T(8,128)S(1)}, u32[]{:S(2)}, u32[]{:S(2)}) collective-permute-start(f32[57,192]{1,0:T(8,128)S(1)} %fusion.29), channel_id=1, source_target_pairs={{0,192},{96,288},{192,0},{288,96},{384,576},{480,672},{576,384},{6... | collective-permute-start | bytes 131336 | tf_op jit(solution)/shard_map/ppermute | solution.py:27
  404.4 9.0 %collective-permute-start.25 = (f32[57,192]{1,0:T(8,128)S(1)}, f32[57,192]{1,0:T(8,128)S(1)}, u32[]{:S(2)}, u32[]{:S(2)}) collective-permute-start(f32[57,192]{1,0:T(8,128)S(1)} %add.325), channel_id=1, source_target_pairs={{0,384},{96,480},{192,576},{288,672},{384,0},{480,96},{576,192},{6... | collective-permute-start | bytes 131336 | tf_op jit(solution)/shard_map/ppermute | solution.py:27
  (26 other events, 171.9 us)

commit v5 on v1

--- a/solution.py
+++ b/solution.py
@@ -59,6 +59,23 @@
         send = lax.dynamic_index_in_dim(q, 1 - bit, axis=at, keepdims=False)
         q = keep + lax.ppermute(send, axis, [(i, i ^ step) for i in range(n)])
     return q.reshape(shape[:dim] + (1,) + shape[dim + 1 :])
+
+
+def six_scatter(q, axis):
+    n = lax.axis_size(axis)
+    here = lax.axis_index(axis)
+    bit = here % 2
+    pair = here // 2
+    q = q.reshape((3, 2) + q.shape[1:])
+    keep = lax.dynamic_index_in_dim(q, bit, axis=1, keepdims=False)
+    send = lax.dynamic_index_in_dim(q, 1 - bit, axis=1, keepdims=False)
+    q = keep + lax.ppermute(send, axis, [(i, i ^ 1) for i in range(n)])
+    own = lax.dynamic_index_in_dim(q, pair, axis=0, keepdims=False)
+    to_next = lax.dynamic_index_in_dim(q, (pair + 1) % 3, axis=0, keepdims=False)
+    to_after = lax.dynamic_index_in_dim(q, (pair + 2) % 3, axis=0, keepdims=False)
+    near = lax.ppermute(to_next, axis, [(i, (i + 2) % n) for i in range(n)])
+    far = lax.ppermute(to_after, axis, [(i, (i + 4) % n) for i in range(n)])
+    return own + near + far
 
 
 def per_group(values):
@@ -174,8 +191,8 @@
     col_count = lax.axis_size("cols")
     band = kernel_grad.reshape(row_count, col_count, -1, channels)
     band = halve_scatter(band, "cols", 1)
-    band = lax.psum_scatter(band, "rows", scatter_dimension=0, tiled=True)
-    grad_weight = xor_sum(band.reshape(-1, channels), "tm")
+    band = six_scatter(band.reshape(row_count, -1, channels), "rows")
+    grad_weight = xor_sum(band, "tm")
     term_a = per_group(gain * grad_shift) / count
     term_b = per_group(gain * grad_gain) / count
     grad_video = (grad_f + rstd_c * (grad_pre * gain - term_a - normed * term_b)).astype(

time: 412 us -> 383 us (0.930)
  the two profiles are of different devices: /device:TPU:32 before, /device:TPU:2 now
where the time goes in v5:
time: 383 us; the launch traced here: 379 us
  starting transfers between devices  152 us (40%)
  waiting for transfers between devices  105 us (27%)
  local copies, waits for them, and re-layouts  69.2 us (18%)
  other arithmetic  24.1 us (6%)
  between operations  15.2 us (4%)
  matrix products  14.7 us (4%)
    ppermute x17, starting transfers between devices, xor_sum(): x = x + lax.ppermute(x, axis, [(i, i ^ step) for i in range(n)])  82.1 us
    ppermute x17, waiting for transfers between devices, xor_sum(): x = x + lax.ppermute(x, axis, [(i, i ^ step) for i in range(n)])  32.3 us
    all_gather x1, waiting for transfers between devices, per_device(): whole = lax.all_gather(weight, ('rows', 'cols'), axis=0, tiled=True)  31.9 us
    ppermute x4, starting transfers between devices, halve_scatter(): q = keep + lax.ppermute(send, axis, [(i, i ^ step) for i in range(n)])  18.1 us
    ppermute x4, waiting for transfers between devices, halve_scatter(): q = keep + lax.ppermute(send, axis, [(i, i ^ step) for i in range(n)])  14.9 us
    ppermute x2, starting transfers between devices, six_sum(): behind = lax.ppermute(x, axis, [(i, (i + 4) % n) for i in range(n)])  13.2 us
    ppermute x1, starting transfers between devices, six_scatter(): near = lax.ppermute(to_next, axis, [(i, (i + 2) % n) for i in range(n)])  10.7 us
    concatenate x1, local copies, waits for them, and re-layouts, per_device(): patches = jnp.concatenate(windows, axis=-1).reshape(cells, 27 * channels)  10.2 us
  transfers between devices with their start and end apart: 37, of which 24 were waited for; matrix products, arithmetic and copies ran while one was open for 27% of the time, Pallas kernels for 0%

profile of v5, /device:TPU:2, one launch (start us, length us, event | category | flops | bytes accessed | tf_op | source)
XLA Modules:
  0.0 379.5 jit_solution(8195266165263645458)
XLA Ops:
  11.7 11.4 %collective-permute-start.7 = (f32[2,192]{1,0:T(2,128)S(1)}, f32[2,192]{1,0:T(2,128)S(1)}, u32[]{:S(2)}, u32[]{:S(2)}) collective-permute-start(f32[2,192]{1,0:T(2,128)S(1)} %fusion.7), channel_id=1, source_target_pairs={{0,2},{1,3},{2,0},{3,1},{4,6},{5,7},{6,4},{7,5},{8,10},{9,11},{10,... | collective-permute-start | bytes 4616 | tf_op jit(solution)/shard_map/ppermute | solution.py:27
  31.7 9.6 %collective-permute-start.9 = (f32[2,192]{1,0:T(2,128)S(1)}, f32[2,192]{1,0:T(2,128)S(1)}, u32[]{:S(2)}, u32[]{:S(2)}) collective-permute-start(f32[2,192]{1,0:T(2,128)S(1)} %add.217), channel_id=1, source_target_pairs={{0,8},{1,9},{2,10},{3,11},{4,12},{5,13},{6,14},{7,15},{8,0},{9,1},... | collective-permute-start | bytes 4616 | tf_op jit(solution)/shard_map/ppermute | solution.py:27
  52.0 6.6 %collective-permute-start.12 = (f32[2,192]{1,0:T(2,128)S(1)}, f32[2,192]{1,0:T(2,128)S(1)}, u32[]{:S(2)}, u32[]{:S(2)}) collective-permute-start(f32[2,192]{1,0:T(2,128)S(1)} %add.219), channel_id=1, source_target_pairs={{0,64},{16,80},{32,0},{48,16},{64,32},{80,48},{1,65},{17,81},{33,1... | collective-permute-start | bytes 4616 | tf_op jit(solution)/shard_map/ppermute | solution.py:37
  65.4 5.2 %collective-permute-start.14 = (f32[2,192]{1,0:T(2,128)S(1)}, f32[2,192]{1,0:T(2,128)S(1)}, u32[]{:S(2)}, u32[]{:S(2)}) collective-permute-start(f32[2,192]{1,0:T(2,128)S(1)} %add.222), channel_id=1, source_target_pairs={{0,192},{96,288},{192,0},{288,96},{384,576},{480,672},{576,384},{6... | collective-permute-start | bytes 4616 | tf_op jit(solution)/shard_map/ppermute | solution.py:27
  72.2 8.9 %collective-permute-start.15 = (f32[2,192]{1,0:T(2,128)S(1)}, f32[2,192]{1,0:T(2,128)S(1)}, u32[]{:S(2)}, u32[]{:S(2)}) collective-permute-start(f32[2,192]{1,0:T(2,128)S(1)} %add.223), channel_id=1, source_target_pairs={{0,384},{96,480},{192,576},{288,672},{384,0},{480,96},{576,192},{6... | collective-permute-start | bytes 4616 | tf_op jit(solution)/shard_map/ppermute | solution.py:27
  88.6 5.2 %collective-permute-done.3 = bf16[3,1,16,768]{3,2,1,0:T(8,128)(2,1)S(1)} collective-permute-done((bf16[3,1,16,768]{3,2,1,0:T(8,128)(2,1)S(1)}, bf16[3,1,16,768]{3,2,1,0:T(8,128)(2,1)S(1)}, u32[]{:S(2)}, u32[]{:S(2)}) %collective-permute-start.3) | collective-permute-done | bytes 73760 | tf_op jit(solution)/shard_map/ppermute | solution.py:18
  102.7 4.3 %fusion.2 = bf16[2,36,18,192]{3,2,1,0:T(8,128)(2,1)S(1)} fusion(bf16[3,18,1,768]{3,2,1,0:T(2,128)(2,1)S(1)} %collective-permute-done.5, bf16[3,18,1,768]{3,2,1,0:T(2,128)(2,1)S(1)} %collective-permute-done.4, bf16[3,1,16,768]{3,2,1,0:T(8,128)(2,1)S(1)} %collective-permute-done.3, bf16[3,1,16,768]{3,2,1,0:T(8,128)(2,1)S(1)} %collective-permute-done.2, ...), kind=kLoop, calls=%fused_computation.24 | loop fusion | flops 6967296 | bytes 1990656 | tf_op jit(solution)/shard_map/concatenate
  112.0 10.2 %concatenate.29 = bf16[2,16,16,5184]{3,2,1,0:T(8,128)(2,1)} concatenate(bf16[2,16,16,192]{3,2,1,0:T(8,128)(2,1)S(1)} %get-tuple-element.73, bf16[2,16,16,192]{3,2,1,0:T(8,128)(2,1)S(1)} %get-tuple-element.72, bf16[2,16,16,192]{3,2,1,0:T(8,128)(2,1)S(1)} %get-tuple-element.71, bf16[2,16,16,192]{3,2,1,0:T(8,128)(2,1)S(1)} %get-tuple-element.70, ...), dimensions={3} | concatenate | bytes 10616832 | tf_op jit(solution)/shard_map/concatenate | solution.py:163
  122.1 8.1 %copy.53 = bf16[512,5184]{0,1:T(8,128)(2,1)} copy(bf16[512,5184]{1,0:T(8,128)(2,1)} %bitcast.66) | data formatting | bytes 10616832 | tf_op jit(solution)/shard_map/reshape | solution.py:163
  130.3 7.6 %dot_general.16 = bf16[6,2,2,2,2,54,512]{6,5,4,3,2,1,0:T(8,128)(2,1)} reshape(bf16[5184,512]{1,0:T(8,128)(2,1)} %bitcast.69) | data formatting | bytes 10616832 | tf_op jit(solution)/shard_map/dot_general | solution.py:170
  137.9 4.2 %fusion.15 = f32[6,2,2,2,2,54,192]{6,5,4,3,2,1,0:T(8,128)S(1)} fusion(bf16[6,2,2,2,2,54,512]{6,5,4,3,2,1,0:T(8,128)(2,1)} %dot_general.16, bf16[512,192,1,1,1,1,1]{1,0,6,5,4,3,2:T(8,128)(2,1)S(1)} %bitcast.73), kind=kOutput, calls=%fused_computation.92 | convolution fusion | flops 1019215872 | bytes 9486336 | tf_op jit(solution)/shard_map/dot_general | solution.py:170
  150.2 3.9 %fusion.1 = bf16[2,36,18,192]{3,2,1,0:T(8,128)(2,1)S(1)} fusion(bf16[3,18,1,768]{3,2,1,0:T(2,128)(2,1)S(1)} %copy-done.7, bf16[3,18,1,768]{3,2,1,0:T(2,128)(2,1)S(1)} %copy-done.5, bf16[3,1,16,768]{3,2,1,0:T(8,128)(2,1)S(1)} %copy-done.11, bf16[3,1,16,768]{3,2,1,0:T(8,128)(2,1)S(1)} %copy-done.9, bf16[1,16,16,768]{3,2,1,0:T(8,128)(2,1)S(1)} %collective-permute-done.1, ...), kind=kLoop, calls=%fused_computation.11 | loop fusion | flops 6967296 | bytes 1990656 | tf_op jit(solution)/shard_map/concatenate.1
  156.4 10.0 %concatenate.31 = bf16[2,16,16,5184]{3,2,1,0:T(8,128)(2,1)} concatenate(bf16[2,16,16,192]{3,2,1,0:T(8,128)(2,1)S(1)} %get-tuple-element.46, bf16[2,16,16,192]{3,2,1,0:T(8,128)(2,1)S(1)} %get-tuple-element.45, bf16[2,16,16,192]{3,2,1,0:T(8,128)(2,1)S(1)} %get-tuple-element.44, bf16[2,16,16,192]{3,2,1,0:T(8,128)(2,1)S(1)} %get-tuple-element.43, ...), dimensions={3} | concatenate | bytes 10616832 | tf_op jit(solution)/shard_map/concatenate | solution.py:164
  171.3 4.4 %collective-permute-start.27 = (f32[6,2,2,54,192]{4,2,3,1,0:T(2,128)}, f32[6,2,2,54,192]{4,2,3,1,0:T(2,128)}, u32[]{:S(2)}, u32[]{:S(2)}) collective-permute-start(f32[6,2,2,54,192]{4,2,3,1,0:T(2,128)} %copy.57), channel_id=1, source_target_pairs={{0,2},{1,3},{2,0},{3,1},{4,6},{5,7},{6,4},{7,5},{8,10},{9,11},{10,... | collective-permute-start | bytes 2985992 | tf_op jit(solution)/shard_map/ppermute | solution.py:60
  175.8 31.9 %all-gather.3.cloned.1.call-done = bf16[96,54,192]{2,1,0:T(8,128)(2,1)} async-done(((bf16[1,54,192]{2,1,0:T(8,128)(2,1)}), bf16[96,54,192]{2,1,0:T(8,128)(2,1)}) %all-gather.3.cloned.1.call-update) | async-done | bytes 1990672 | tf_op jit(solution)/shard_map/all_gather | solution.py:142
  207.6 5.4 %reshape.206 = bf16[27,192,192]{2,1,0:T(8,128)(2,1)} reshape(bf16[96,54,192]{2,1,0:T(8,128)(2,1)} %all-gather.3.cloned.1.call-done) | data formatting | bytes 3981312 | tf_op jit(solution)/shard_map/reshape | solution.py:174
  213.0 4.5 %copy.51 = bf16[27,192,192]{2,1,0:T(8,128)(2,1)} copy(bf16[27,192,192]{1,2,0:T(8,128)(2,1)} %bitcast.71) | data formatting | bytes 3981312 | tf_op jit(solution)/shard_map/transpose | solution.py:174
  217.5 5.3 %convolution_convert_fusion = bf16[512,192]{0,1:T(8,128)(2,1)S(1)} fusion(bf16[512,5184]{1,0:T(8,128)(2,1)} %bitcast.68, bf16[5184,192]{1,0:T(8,128)(2,1)} %bitcast.70), kind=kOutput, calls=%fused_computation.9 | convolution fusion | flops 1019314176 | bytes 7495680 | tf_op jit(solution)/shard_map/dot_general | solution.py:176
  237.3 3.9 %collective-permute-done.18 = f32[3,192]{1,0:T(4,128)S(1)} collective-permute-done((f32[3,192]{1,0:T(4,128)S(1)}, f32[3,192]{1,0:T(4,128)S(1)}, u32[]{:S(2)}, u32[]{:S(2)}) %collective-permute-start.18) | collective-permute-done | bytes 2336 | tf_op jit(solution)/shard_map/ppermute | solution.py:27
  241.2 6.6 %collective-permute-start.19 = (f32[3,192]{1,0:T(4,128)S(1)}, f32[3,192]{1,0:T(4,128)S(1)}, u32[]{:S(2)}, u32[]{:S(2)}) collective-permute-start(f32[3,192]{1,0:T(4,128)S(1)} %add.237), channel_id=1, source_target_pairs={{0,8},{1,9},{2,10},{3,11},{4,12},{5,13},{6,14},{7,15},{8,0},{9,1},... | collective-permute-start | bytes 6920 | tf_op jit(solution)/shard_map/ppermute | solution.py:27
  247.9 5.1 %collective-permute-done.19 = f32[3,192]{1,0:T(4,128)S(1)} collective-permute-done((f32[3,192]{1,0:T(4,128)S(1)}, f32[3,192]{1,0:T(4,128)S(1)}, u32[]{:S(2)}, u32[]{:S(2)}) %collective-permute-start.19) | collective-permute-done | bytes 2336 | tf_op jit(solution)/shard_map/ppermute | solution.py:27
  261.7 6.6 %collective-permute-start.22 = (f32[3,192]{1,0:T(4,128)S(1)}, f32[3,192]{1,0:T(4,128)S(1)}, u32[]{:S(2)}, u32[]{:S(2)}) collective-permute-start(f32[3,192]{1,0:T(4,128)S(1)} %add.239), channel_id=1, source_target_pairs={{0,64},{16,80},{32,0},{48,16},{64,32},{80,48},{1,65},{17,81},{33,1... | collective-permute-start | bytes 6920 | tf_op jit(solution)/shard_map/ppermute | solution.py:37
  277.6 3.9 %reshape.217 = bf16[5184,192]{1,0:T(8,128)(2,1)S(1)} reshape(bf16[96,54,192]{2,1,0:T(8,128)(2,1)} %all-gather.3.cloned.1.call-done) | data formatting | bytes 3981312
  281.5 3.9 %collective-permute-start.24 = (f32[3,192]{1,0:T(4,128)S(1)}, f32[3,192]{1,0:T(4,128)S(1)}, u32[]{:S(2)}, u32[]{:S(2)}) collective-permute-start(f32[3,192]{1,0:T(4,128)S(1)} %add.242), channel_id=1, source_target_pairs={{0,192},{96,288},{192,0},{288,96},{384,576},{480,672},{576,384},{6... | collective-permute-start | bytes 6920 | tf_op jit(solution)/shard_map/ppermute | solution.py:27
  285.5 5.2 %convolution_add_fusion = f32[512,192]{0,1:T(8,128)} fusion(bf16[512,5184]{1,0:T(8,128)(2,1)} %bitcast.67, bf16[5184,192]{1,0:T(8,128)(2,1)S(1)} %reshape.217, f32[192]{0:T(256)S(1)} %copy-done.15), kind=kOutput, calls=%fused_computation.8 | convolution fusion | flops 1019314176 | bytes 7693056 | tf_op jit(solution)/shard_map/dot_general | solution.py:165
  292.0 5.1 %collective-permute-start.25 = (f32[3,192]{1,0:T(4,128)S(1)}, f32[3,192]{1,0:T(4,128)S(1)}, u32[]{:S(2)}, u32[]{:S(2)}) collective-permute-start(f32[3,192]{1,0:T(4,128)S(1)} %add.243), channel_id=1, source_target_pairs={{0,384},{96,480},{192,576},{288,672},{384,0},{480,96},{576,192},{6... | collective-permute-start | bytes 6920 | tf_op jit(solution)/shard_map/ppermute | solution.py:27
  298.6 8.1 %collective-permute-start.29 = (f32[6,54,192]{2,1,0:T(8,128)S(1)}, f32[6,54,192]{2,1,0:T(8,128)S(1)}, u32[]{:S(2)}, u32[]{:S(2)}) collective-permute-start(f32[6,54,192]{2,1,0:T(8,128)S(1)} %dynamic-slice_bitcast_fusion.3), channel_id=1, source_target_pairs={{0,8},{1,9},{2,10},{3,11},{4,12},{5,13},{6,14},{7,15},{8,0},{9,1},... | collective-permute-start | bytes 746504 | tf_op jit(solution)/shard_map/ppermute | solution.py:60
  307.4 14.9 %collective-permute-done.29 = f32[6,54,192]{2,1,0:T(8,128)S(1)} collective-permute-done((f32[6,54,192]{2,1,0:T(8,128)S(1)}, f32[6,54,192]{2,1,0:T(8,128)S(1)}, u32[]{:S(2)}, u32[]{:S(2)}) %collective-permute-start.29) | collective-permute-done | bytes 248864 | tf_op jit(solution)/shard_map/ppermute | solution.py:60
  325.0 4.8 %collective-permute-done.30 = f32[3,54,192]{2,1,0:T(8,128)S(1)} collective-permute-done((f32[3,54,192]{2,1,0:T(8,128)S(1)}, f32[3,54,192]{2,1,0:T(8,128)S(1)}, u32[]{:S(2)}, u32[]{:S(2)}) %collective-permute-start.30) | collective-permute-done | bytes 124448 | tf_op jit(solution)/shard_map/ppermute | solution.py:72
  329.8 10.7 %collective-permute-start.31 = (f32[54,192]{1,0:T(8,128)S(1)}, f32[54,192]{1,0:T(8,128)S(1)}, u32[]{:S(2)}, u32[]{:S(2)}) collective-permute-start(f32[54,192]{1,0:T(8,128)S(1)} %get-tuple-element.74), channel_id=1, source_target_pairs={{0,32},{16,48},{32,64},{48,80},{64,0},{80,16},{1,33},{17,49},{33,6... | collective-permute-start | bytes 124424 | tf_op jit(solution)/shard_map/ppermute | solution.py:76
  342.7 4.8 %collective-permute-done.32 = f32[54,192]{1,0:T(8,128)S(1)} collective-permute-done((f32[54,192]{1,0:T(8,128)S(1)}, f32[54,192]{1,0:T(8,128)S(1)}, u32[]{:S(2)}, u32[]{:S(2)}) %collective-permute-start.32) | collective-permute-done | bytes 41504 | tf_op jit(solution)/shard_map/ppermute | solution.py:77
  361.9 4.8 %collective-permute-start.35 = (f32[54,192]{1,0:T(8,128)S(1)}, f32[54,192]{1,0:T(8,128)S(1)}, u32[]{:S(2)}, u32[]{:S(2)}) collective-permute-start(f32[54,192]{1,0:T(8,128)S(1)} %add.276), channel_id=1, source_target_pairs={{0,384},{96,480},{192,576},{288,672},{384,0},{480,96},{576,192},{6... | collective-permute-start | bytes 124424 | tf_op jit(solution)/shard_map/ppermute | solution.py:27
  (181 shorter events, 128.8 us)
Async XLA Ops:
  7.2 200.5 %all-gather.3.cloned.1.call-start = ((), (), s32[]{:S(2)}) async-start(), calls=%async_computation | async-start | bytes 2781184 | tf_op jit(solution)/shard_map/all_gather | solution.py:142
  11.7 13.0 %collective-permute-start.7 = (f32[2,192]{1,0:T(2,128)S(1)}, f32[2,192]{1,0:T(2,128)S(1)}, u32[]{:S(2)}, u32[]{:S(2)}) collective-permute-start(f32[2,192]{1,0:T(2,128)S(1)} %fusion.7), channel_id=1, source_target_pairs={{0,2},{1,3},{2,0},{3,1},{4,6},{5,7},{6,4},{7,5},{8,10},{9,11},{10,... | collective-permute-start | bytes 4616 | tf_op jit(solution)/shard_map/ppermute | solution.py:27
  24.7 7.0 %collective-permute-start.8 = (f32[2,192]{1,0:T(2,128)S(1)}, f32[2,192]{1,0:T(2,128)S(1)}, u32[]{:S(2)}, u32[]{:S(2)}) collective-permute-start(f32[2,192]{1,0:T(2,128)S(1)} %fusion.23), channel_id=1, source_target_pairs={{0,4},{1,5},{2,6},{3,7},{4,0},{5,1},{6,2},{7,3},{8,12},{9,13},{10,... | collective-permute-start | bytes 4616 | tf_op jit(solution)/shard_map/ppermute | solution.py:27
  26.6 56.6 %collective-permute-start = (bf16[1,16,16,768]{3,2,1,0:T(8,128)(2,1)S(1)}, bf16[1,16,16,768]{3,2,1,0:T(8,128)(2,1)S(1)}, u32[]{:S(2)}, u32[]{:S(2)}) collective-permute-start(bf16[1,16,16,768]{3,2,1,0:T(8,128)(2,1)S(1)} %constant_dynamic-update-slice_fusion), channel_id=1, source_target_pairs={{0,96},{96,192},{192,288},{288,384},{384,480},{480,576},{576,672},... | collective-permute-start | bytes 1179656 | tf_op jit(solution)/shard_map/ppermute | solution.py:15
  28.0 55.3 %collective-permute-start.1 = (bf16[1,16,16,768]{3,2,1,0:T(8,128)(2,1)S(1)}, bf16[1,16,16,768]{3,2,1,0:T(8,128)(2,1)S(1)}, u32[]{:S(2)}, u32[]{:S(2)}) collective-permute-start(bf16[1,16,16,768]{3,2,1,0:T(8,128)(2,1)S(1)} %constant_dynamic-update-slice_fusion), channel_id=1, source_target_pairs={{96,0},{192,96},{288,192},{384,288},{480,384},{576,480},{672,576},... | collective-permute-start | bytes 1179656 | tf_op jit(solution)/shard_map/ppermute | solution.py:18
  31.7 11.8 %collective-permute-start.9 = (f32[2,192]{1,0:T(2,128)S(1)}, f32[2,192]{1,0:T(2,128)S(1)}, u32[]{:S(2)}, u32[]{:S(2)}) collective-permute-start(f32[2,192]{1,0:T(2,128)S(1)} %add.217), channel_id=1, source_target_pairs={{0,8},{1,9},{2,10},{3,11},{4,12},{5,13},{6,14},{7,15},{8,0},{9,1},... | collective-permute-start | bytes 4616 | tf_op jit(solution)/shard_map/ppermute | solution.py:27
  48.9 9.8 %collective-permute-start.11 = (f32[2,192]{1,0:T(2,128)S(1)}, f32[2,192]{1,0:T(2,128)S(1)}, u32[]{:S(2)}, u32[]{:S(2)}) collective-permute-start(f32[2,192]{1,0:T(2,128)S(1)} %add.219), channel_id=1, source_target_pairs={{0,32},{16,48},{32,64},{48,80},{64,0},{80,16},{1,33},{17,49},{33,6... | collective-permute-start | bytes 4616 | tf_op jit(solution)/shard_map/ppermute | solution.py:36
  52.0 7.9 %collective-permute-start.12 = (f32[2,192]{1,0:T(2,128)S(1)}, f32[2,192]{1,0:T(2,128)S(1)}, u32[]{:S(2)}, u32[]{:S(2)}) collective-permute-start(f32[2,192]{1,0:T(2,128)S(1)} %add.219), channel_id=1, source_target_pairs={{0,64},{16,80},{32,0},{48,16},{64,32},{80,48},{1,65},{17,81},{33,1... | collective-permute-start | bytes 4616 | tf_op jit(solution)/shard_map/ppermute | solution.py:37
  65.4 6.8 %collective-permute-start.14 = (f32[2,192]{1,0:T(2,128)S(1)}, f32[2,192]{1,0:T(2,128)S(1)}, u32[]{:S(2)}, u32[]{:S(2)}) collective-permute-start(f32[2,192]{1,0:T(2,128)S(1)} %add.222), channel_id=1, source_target_pairs={{0,192},{96,288},{192,0},{288,96},{384,576},{480,672},{576,384},{6... | collective-permute-start | bytes 4616 | tf_op jit(solution)/shard_map/ppermute | solution.py:27
  72.2 10.5 %collective-permute-start.15 = (f32[2,192]{1,0:T(2,128)S(1)}, f32[2,192]{1,0:T(2,128)S(1)}, u32[]{:S(2)}, u32[]{:S(2)}) collective-permute-start(f32[2,192]{1,0:T(2,128)S(1)} %add.223), channel_id=1, source_target_pairs={{0,384},{96,480},{192,576},{288,672},{384,0},{480,96},{576,192},{6... | collective-permute-start | bytes 4616 | tf_op jit(solution)/shard_map/ppermute | solution.py:27
  86.6 7.1 %collective-permute-start.3 = (bf16[3,1,16,768]{3,2,1,0:T(8,128)(2,1)S(1)}, bf16[3,1,16,768]{3,2,1,0:T(8,128)(2,1)S(1)}, u32[]{:S(2)}, u32[]{:S(2)}) collective-permute-start(bf16[3,1,16,768]{3,2,1,0:T(8,128)(2,1)S(1)} %get-tuple-element.16), channel_id=1, source_target_pairs={{16,0},{32,16},{48,32},{64,48},{80,64},{17,1},{33,17},{49,33},{65,... | collective-permute-start | bytes 221192 | tf_op jit(solution)/shard_map/ppermute | solution.py:18
  94.1 6.9 %collective-permute-start.4 = (bf16[3,18,1,768]{3,2,1,0:T(2,128)(2,1)S(1)}, bf16[3,18,1,768]{3,2,1,0:T(2,128)(2,1)S(1)}, u32[]{:S(2)}, u32[]{:S(2)}) collective-permute-start(bf16[3,18,1,768]{3,2,1,0:T(2,128)(2,1)S(1)} %get-tuple-element.13), channel_id=1, source_target_pairs={{0,1},{1,2},{2,3},{3,4},{4,5},{5,6},{6,7},{7,8},{8,9},{9,10},{10,1... | collective-permute-start | bytes 248840 | tf_op jit(solution)/shard_map/ppermute | solution.py:15
  96.0 6.7 %collective-permute-start.5 = (bf16[3,18,1,768]{3,2,1,0:T(2,128)(2,1)S(1)}, bf16[3,18,1,768]{3,2,1,0:T(2,128)(2,1)S(1)}, u32[]{:S(2)}, u32[]{:S(2)}) collective-permute-start(bf16[3,18,1,768]{3,2,1,0:T(2,128)(2,1)S(1)} %get-tuple-element.14), channel_id=1, source_target_pairs={{1,0},{2,1},{3,2},{4,3},{5,4},{6,5},{7,6},{8,7},{9,8},{10,9},{11,1... | collective-permute-start | bytes 248840 | tf_op jit(solution)/shard_map/ppermute | solution.py:18
  147.6 18.8 %collective-permute-start.26 = (f32[6,2,2,2,54,192]{5,3,4,2,1,0:T(2,128)}, f32[6,2,2,2,54,192]{5,3,4,2,1,0:T(2,128)}, u32[]{:S(2)}, u32[]{:S(2)}) collective-permute-start(f32[6,2,2,2,54,192]{5,3,4,2,1,0:T(2,128)} %copy.55), channel_id=1, source_target_pairs={{0,1},{1,0},{2,3},{3,2},{4,5},{5,4},{6,7},{7,6},{8,9},{9,8},{10,11... | collective-permute-start | bytes 5971976 | tf_op jit(solution)/shard_map/ppermute | solution.py:60
  171.3 97.0 %collective-permute-start.27 = (f32[6,2,2,54,192]{4,2,3,1,0:T(2,128)}, f32[6,2,2,54,192]{4,2,3,1,0:T(2,128)}, u32[]{:S(2)}, u32[]{:S(2)}) collective-permute-start(f32[6,2,2,54,192]{4,2,3,1,0:T(2,128)} %copy.57), channel_id=1, source_target_pairs={{0,2},{1,3},{2,0},{3,1},{4,6},{5,7},{6,4},{7,5},{8,10},{9,11},{10,... | collective-permute-start | bytes 2985992 | tf_op jit(solution)/shard_map/ppermute | solution.py:60
  228.7 5.5 %collective-permute-start.17 = (f32[3,192]{1,0:T(4,128)S(1)}, f32[3,192]{1,0:T(4,128)S(1)}, u32[]{:S(2)}, u32[]{:S(2)}) collective-permute-start(f32[3,192]{1,0:T(4,128)S(1)} %fusion.8), channel_id=1, source_target_pairs={{0,2},{1,3},{2,0},{3,1},{4,6},{5,7},{6,4},{7,5},{8,10},{9,11},{10,... | collective-permute-start | bytes 6920 | tf_op jit(solution)/shard_map/ppermute | solution.py:27
  234.2 7.0 %collective-permute-start.18 = (f32[3,192]{1,0:T(4,128)S(1)}, f32[3,192]{1,0:T(4,128)S(1)}, u32[]{:S(2)}, u32[]{:S(2)}) collective-permute-start(f32[3,192]{1,0:T(4,128)S(1)} %fusion.22), channel_id=1, source_target_pairs={{0,4},{1,5},{2,6},{3,7},{4,0},{5,1},{6,2},{7,3},{8,12},{9,13},{10,... | collective-permute-start | bytes 6920 | tf_op jit(solution)/shard_map/ppermute | solution.py:27
  241.2 11.8 %collective-permute-start.19 = (f32[3,192]{1,0:T(4,128)S(1)}, f32[3,192]{1,0:T(4,128)S(1)}, u32[]{:S(2)}, u32[]{:S(2)}) collective-permute-start(f32[3,192]{1,0:T(4,128)S(1)} %add.237), channel_id=1, source_target_pairs={{0,8},{1,9},{2,10},{3,11},{4,12},{5,13},{6,14},{7,15},{8,0},{9,1},... | collective-permute-start | bytes 6920 | tf_op jit(solution)/shard_map/ppermute | solution.py:27
  253.0 5.5 %collective-permute-start.20 = (f32[3,192]{1,0:T(4,128)S(1)}, f32[3,192]{1,0:T(4,128)S(1)}, u32[]{:S(2)}, u32[]{:S(2)}) collective-permute-start(f32[3,192]{1,0:T(4,128)S(1)} %add.238), channel_id=1, source_target_pairs={{0,16},{16,0},{32,48},{48,32},{64,80},{80,64},{1,17},{17,1},{33,49... | collective-permute-start | bytes 6920 | tf_op jit(solution)/shard_map/ppermute | solution.py:34
  258.5 11.3 %collective-permute-start.21 = (f32[3,192]{1,0:T(4,128)S(1)}, f32[3,192]{1,0:T(4,128)S(1)}, u32[]{:S(2)}, u32[]{:S(2)}) collective-permute-start(f32[3,192]{1,0:T(4,128)S(1)} %add.239), channel_id=1, source_target_pairs={{0,32},{16,48},{32,64},{48,80},{64,0},{80,16},{1,33},{17,49},{33,6... | collective-permute-start | bytes 6920 | tf_op jit(solution)/shard_map/ppermute | solution.py:36
  261.7 8.2 %collective-permute-start.22 = (f32[3,192]{1,0:T(4,128)S(1)}, f32[3,192]{1,0:T(4,128)S(1)}, u32[]{:S(2)}, u32[]{:S(2)}) collective-permute-start(f32[3,192]{1,0:T(4,128)S(1)} %add.239), channel_id=1, source_target_pairs={{0,64},{16,80},{32,0},{48,16},{64,32},{80,48},{1,65},{17,81},{33,1... | collective-permute-start | bytes 6920 | tf_op jit(solution)/shard_map/ppermute | solution.py:37
  269.9 11.6 %collective-permute-start.23 = (f32[3,192]{1,0:T(4,128)S(1)}, f32[3,192]{1,0:T(4,128)S(1)}, u32[]{:S(2)}, u32[]{:S(2)}) collective-permute-start(f32[3,192]{1,0:T(4,128)S(1)} %select_add_fusion), channel_id=1, source_target_pairs={{0,96},{96,0},{192,288},{288,192},{384,480},{480,384},{576,672},{6... | collective-permute-start | bytes 6920 | tf_op jit(solution)/shard_map/ppermute | solution.py:27
  274.4 22.8 %collective-permute-start.28 = (f32[6,2,54,192]{3,1,2,0:T(2,128)}, f32[6,2,54,192]{3,1,2,0:T(2,128)}, u32[]{:S(2)}, u32[]{:S(2)}) collective-permute-start(f32[6,2,54,192]{3,1,2,0:T(2,128)} %copy.59), channel_id=1, source_target_pairs={{0,4},{1,5},{2,6},{3,7},{4,0},{5,1},{6,2},{7,3},{8,12},{9,13},{10,... | collective-permute-start | bytes 1493000 | tf_op jit(solution)/shard_map/ppermute | solution.py:60
  281.5 10.4 %collective-permute-start.24 = (f32[3,192]{1,0:T(4,128)S(1)}, f32[3,192]{1,0:T(4,128)S(1)}, u32[]{:S(2)}, u32[]{:S(2)}) collective-permute-start(f32[3,192]{1,0:T(4,128)S(1)} %add.242), channel_id=1, source_target_pairs={{0,192},{96,288},{192,0},{288,96},{384,576},{480,672},{576,384},{6... | collective-permute-start | bytes 6920 | tf_op jit(solution)/shard_map/ppermute | solution.py:27
  292.0 15.5 %collective-permute-start.25 = (f32[3,192]{1,0:T(4,128)S(1)}, f32[3,192]{1,0:T(4,128)S(1)}, u32[]{:S(2)}, u32[]{:S(2)}) collective-permute-start(f32[3,192]{1,0:T(4,128)S(1)} %add.243), channel_id=1, source_target_pairs={{0,384},{96,480},{192,576},{288,672},{384,0},{480,96},{576,192},{6... | collective-permute-start | bytes 6920 | tf_op jit(solution)/shard_map/ppermute | solution.py:27
  298.6 23.8 %collective-permute-start.29 = (f32[6,54,192]{2,1,0:T(8,128)S(1)}, f32[6,54,192]{2,1,0:T(8,128)S(1)}, u32[]{:S(2)}, u32[]{:S(2)}) collective-permute-start(f32[6,54,192]{2,1,0:T(8,128)S(1)} %dynamic-slice_bitcast_fusion.3), channel_id=1, source_target_pairs={{0,8},{1,9},{2,10},{3,11},{4,12},{5,13},{6,14},{7,15},{8,0},{9,1},... | collective-permute-start | bytes 746504 | tf_op jit(solution)/shard_map/ppermute | solution.py:60
  322.5 7.3 %collective-permute-start.30 = (f32[3,54,192]{2,1,0:T(8,128)S(1)}, f32[3,54,192]{2,1,0:T(8,128)S(1)}, u32[]{:S(2)}, u32[]{:S(2)}) collective-permute-start(f32[3,54,192]{2,1,0:T(8,128)S(1)} %dynamic-slice_bitcast_fusion.4), channel_id=1, source_target_pairs={{0,16},{16,0},{32,48},{48,32},{64,80},{80,64},{1,17},{17,1},{33,49... | collective-permute-start | bytes 373256 | tf_op jit(solution)/shard_map/ppermute | solution.py:72
  329.8 12.9 %collective-permute-start.31 = (f32[54,192]{1,0:T(8,128)S(1)}, f32[54,192]{1,0:T(8,128)S(1)}, u32[]{:S(2)}, u32[]{:S(2)}) collective-permute-start(f32[54,192]{1,0:T(8,128)S(1)} %get-tuple-element.74), channel_id=1, source_target_pairs={{0,32},{16,48},{32,64},{48,80},{64,0},{80,16},{1,33},{17,49},{33,6... | collective-permute-start | bytes 124424 | tf_op jit(solution)/shard_map/ppermute | solution.py:76
  340.5 7.0 %collective-permute-start.32 = (f32[54,192]{1,0:T(8,128)S(1)}, f32[54,192]{1,0:T(8,128)S(1)}, u32[]{:S(2)}, u32[]{:S(2)}) collective-permute-start(f32[54,192]{1,0:T(8,128)S(1)} %get-tuple-element.75), channel_id=1, source_target_pairs={{0,64},{16,80},{32,0},{48,16},{64,32},{80,48},{1,65},{17,81},{33,1... | collective-permute-start | bytes 124424 | tf_op jit(solution)/shard_map/ppermute | solution.py:77
  347.5 6.3 %collective-permute-start.33 = (f32[54,192]{1,0:T(8,128)S(1)}, f32[54,192]{1,0:T(8,128)S(1)}, u32[]{:S(2)}, u32[]{:S(2)}) collective-permute-start(f32[54,192]{1,0:T(8,128)S(1)} %fusion.6), channel_id=1, source_target_pairs={{0,96},{96,0},{192,288},{288,192},{384,480},{480,384},{576,672},{6... | collective-permute-start | bytes 124424 | tf_op jit(solution)/shard_map/ppermute | solution.py:27
  353.9 8.0 %collective-permute-start.34 = (f32[54,192]{1,0:T(8,128)S(1)}, f32[54,192]{1,0:T(8,128)S(1)}, u32[]{:S(2)}, u32[]{:S(2)}) collective-permute-start(f32[54,192]{1,0:T(8,128)S(1)} %add.275), channel_id=1, source_target_pairs={{0,192},{96,288},{192,0},{288,96},{384,576},{480,672},{576,384},{6... | collective-permute-start | bytes 124424 | tf_op jit(solution)/shard_map/ppermute | solution.py:27
  361.9 10.1 %collective-permute-start.35 = (f32[54,192]{1,0:T(8,128)S(1)}, f32[54,192]{1,0:T(8,128)S(1)}, u32[]{:S(2)}, u32[]{:S(2)}) collective-permute-start(f32[54,192]{1,0:T(8,128)S(1)} %add.276), channel_id=1, source_target_pairs={{0,384},{96,480},{192,576},{288,672},{384,0},{480,96},{576,192},{6... | collective-permute-start | bytes 124424 | tf_op jit(solution)/shard_map/ppermute | solution.py:27
  (24 other events, 343.6 us)
Sparse Core Ops, SparseCore 0:
  29.4 178.1 all-gather.2

commit v6 on v5

--- a/solution.py
+++ b/solution.py
@@ -139,7 +139,9 @@
         & ((col_pos < local_cols + 1) | (col_index < lax.axis_size("cols") - 1))
     )
     padded = jnp.where(valid, jax.nn.silu(pre_ext), 0.0).astype(jnp.bfloat16)
-    whole = lax.all_gather(weight, ("rows", "cols"), axis=0, tiled=True)
+    whole = lax.all_gather(
+        lax.all_gather(weight, "cols", axis=0, tiled=True), "rows", axis=0, tiled=True
+    )
     cells = local_frames * local_rows * local_cols
     windows = []
     grad_windows = []

time: 383 us -> 412 us (1.076)
  the two profiles are of different devices: /device:TPU:2 before, /device:TPU:1 now
where the time goes in v6:
time: 412 us; the launch traced here: 404 us
  starting transfers between devices  169 us (41%)
  local copies, waits for them, and re-layouts  74.7 us (18%)
  waiting for transfers between devices  65.9 us (16%)
  blocking collectives  40.6 us (10%)
  other arithmetic  24.5 us (6%)
  between operations  15.3 us (4%)
  matrix products  13.9 us (3%)
    ppermute x17, starting transfers between devices, xor_sum(): x = x + lax.ppermute(x, axis, [(i, i ^ step) for i in range(n)])  86.9 us
    all_gather x1, blocking collectives, per_device(): lax.all_gather(weight, 'cols', axis=0, tiled=True)  40.6 us
    ppermute x17, waiting for transfers between devices, xor_sum(): x = x + lax.ppermute(x, axis, [(i, i ^ step) for i in range(n)])  36.5 us
    ppermute x1, starting transfers between devices, six_scatter(): q = keep + lax.ppermute(send, axis, [(i, i ^ 1) for i in range(n)])  16.6 us
    ppermute x4, starting transfers between devices, halve_scatter(): q = keep + lax.ppermute(send, axis, [(i, i ^ step) for i in range(n)])  12.2 us
    ppermute x1, starting transfers between devices, six_scatter(): far = lax.ppermute(to_after, axis, [(i, (i + 4) % n) for i in range(n)])  11.8 us
    ppermute x4, waiting for transfers between devices, halve_scatter(): q = keep + lax.ppermute(send, axis, [(i, i ^ step) for i in range(n)])  10.8 us
    ppermute x2, starting transfers between devices, six_sum(): behind = lax.ppermute(x, axis, [(i, (i + 4) % n) for i in range(n)])  10.6 us
  transfers between devices with their start and end apart: 37, of which 21 were waited for; matrix products, arithmetic and copies ran while one was open for 27% of the time, Pallas kernels for 0%

profile of v6, /device:TPU:1, one launch (start us, length us, event | category | flops | bytes accessed | tf_op | source)
XLA Modules:
  0.0 404.1 jit_solution(15883942645309252397)
XLA Ops:
  8.3 12.4 %collective-permute-start.6 = (f32[2,192]{1,0:T(2,128)S(1)}, f32[2,192]{1,0:T(2,128)S(1)}, u32[]{:S(2)}, u32[]{:S(2)}) collective-permute-start(f32[2,192]{1,0:T(2,128)S(1)} %pad_maximum_fusion.33), channel_id=1, source_target_pairs={{0,1},{1,0},{2,3},{3,2},{4,5},{5,4},{6,7},{7,6},{8,9},{9,8},{10,11... | collective-permute-start | bytes 4616 | tf_op jit(solution)/shard_map/ppermute | solution.py:27
  29.2 40.6 %all-gather = bf16[16,54,192]{2,1,0:T(8,128)(2,1)S(1)} all-gather(bf16[1,54,192]{2,1,0:T(8,128)(2,1)S(1)} %bitcast.83), channel_id=1, replica_groups=mesh['tm'=8,'rows'=6,'cols'=16] {'cols'}, dimensions={0}, use_global_device_ids=true | all-gather | bytes 352512 | tf_op jit(solution)/shard_map/all_gather | solution.py:143
  74.1 7.5 %collective-permute-done.9 = f32[2,192]{1,0:T(2,128)S(1)} collective-permute-done((f32[2,192]{1,0:T(2,128)S(1)}, f32[2,192]{1,0:T(2,128)S(1)}, u32[]{:S(2)}, u32[]{:S(2)}) %collective-permute-start.9) | collective-permute-done | bytes 1568 | tf_op jit(solution)/shard_map/ppermute | solution.py:27
  85.9 4.6 %collective-permute-start.11 = (f32[2,192]{1,0:T(2,128)S(1)}, f32[2,192]{1,0:T(2,128)S(1)}, u32[]{:S(2)}, u32[]{:S(2)}) collective-permute-start(f32[2,192]{1,0:T(2,128)S(1)} %add.219), channel_id=1, source_target_pairs={{0,32},{16,48},{32,64},{48,80},{64,0},{80,16},{1,33},{17,49},{33,6... | collective-permute-start | bytes 4616 | tf_op jit(solution)/shard_map/ppermute | solution.py:36
  90.5 4.6 %collective-permute-start.12 = (f32[2,192]{1,0:T(2,128)S(1)}, f32[2,192]{1,0:T(2,128)S(1)}, u32[]{:S(2)}, u32[]{:S(2)}) collective-permute-start(f32[2,192]{1,0:T(2,128)S(1)} %add.219), channel_id=1, source_target_pairs={{0,64},{16,80},{32,0},{48,16},{64,32},{80,48},{1,65},{17,81},{33,1... | collective-permute-start | bytes 4616 | tf_op jit(solution)/shard_map/ppermute | solution.py:37
  96.2 4.7 %collective-permute-start.13 = (f32[2,192]{1,0:T(2,128)S(1)}, f32[2,192]{1,0:T(2,128)S(1)}, u32[]{:S(2)}, u32[]{:S(2)}) collective-permute-start(f32[2,192]{1,0:T(2,128)S(1)} %select_add_fusion.1), channel_id=1, source_target_pairs={{0,96},{96,0},{192,288},{288,192},{384,480},{480,384},{576,672},{6... | collective-permute-start | bytes 4616 | tf_op jit(solution)/shard_map/ppermute | solution.py:27
  102.3 5.2 %collective-permute-start.14 = (f32[2,192]{1,0:T(2,128)S(1)}, f32[2,192]{1,0:T(2,128)S(1)}, u32[]{:S(2)}, u32[]{:S(2)}) collective-permute-start(f32[2,192]{1,0:T(2,128)S(1)} %add.222), channel_id=1, source_target_pairs={{0,192},{96,288},{192,0},{288,96},{384,576},{480,672},{576,384},{6... | collective-permute-start | bytes 4616 | tf_op jit(solution)/shard_map/ppermute | solution.py:27
  108.9 8.2 %collective-permute-start.15 = (f32[2,192]{1,0:T(2,128)S(1)}, f32[2,192]{1,0:T(2,128)S(1)}, u32[]{:S(2)}, u32[]{:S(2)}) collective-permute-start(f32[2,192]{1,0:T(2,128)S(1)} %add.223), channel_id=1, source_target_pairs={{0,384},{96,480},{192,576},{288,672},{384,0},{480,96},{576,192},{6... | collective-permute-start | bytes 4616 | tf_op jit(solution)/shard_map/ppermute | solution.py:27
  122.8 5.5 %collective-permute-done.3 = bf16[3,1,16,768]{3,2,1,0:T(8,128)(2,1)S(1)} collective-permute-done((bf16[3,1,16,768]{3,2,1,0:T(8,128)(2,1)S(1)}, bf16[3,1,16,768]{3,2,1,0:T(8,128)(2,1)S(1)}, u32[]{:S(2)}, u32[]{:S(2)}) %collective-permute-start.3) | collective-permute-done | bytes 73760 | tf_op jit(solution)/shard_map/ppermute | solution.py:18
  131.9 6.2 %collective-permute-start.5 = (bf16[3,18,1,768]{3,2,1,0:T(2,128)(2,1)S(1)}, bf16[3,18,1,768]{3,2,1,0:T(2,128)(2,1)S(1)}, u32[]{:S(2)}, u32[]{:S(2)}) collective-permute-start(bf16[3,18,1,768]{3,2,1,0:T(2,128)(2,1)S(1)} %get-tuple-element.14), channel_id=1, source_target_pairs={{1,0},{2,1},{3,2},{4,3},{5,4},{6,5},{7,6},{8,7},{9,8},{10,9},{11,1... | collective-permute-start | bytes 248840 | tf_op jit(solution)/shard_map/ppermute | solution.py:18
  139.1 4.3 %fusion.2 = bf16[2,36,18,192]{3,2,1,0:T(8,128)(2,1)S(1)} fusion(bf16[3,18,1,768]{3,2,1,0:T(2,128)(2,1)S(1)} %collective-permute-done.5, bf16[3,18,1,768]{3,2,1,0:T(2,128)(2,1)S(1)} %collective-permute-done.4, bf16[3,1,16,768]{3,2,1,0:T(8,128)(2,1)S(1)} %collective-permute-done.3, bf16[3,1,16,768]{3,2,1,0:T(8,128)(2,1)S(1)} %collective-permute-done.2, ...), kind=kLoop, calls=%fused_computation.24 | loop fusion | flops 6967296 | bytes 1990656 | tf_op jit(solution)/shard_map/concatenate
  149.1 9.7 %concatenate.29 = bf16[2,16,16,5184]{3,2,1,0:T(8,128)(2,1)} concatenate(bf16[2,16,16,192]{3,2,1,0:T(8,128)(2,1)} %get-tuple-element.73, bf16[2,16,16,192]{3,2,1,0:T(8,128)(2,1)} %get-tuple-element.72, bf16[2,16,16,192]{3,2,1,0:T(8,128)(2,1)} %get-tuple-element.71, bf16[2,16,16,192]{3,2,1,0:T(8,128)(2,1)} %get-tuple-element.70, bf16[2,16,16,192]{3,2,1,0:T(8,128)(2,1)} %get-tuple-element.69, ...), dimensions={3} | concatenate | bytes 10616832 | tf_op jit(solution)/shard_map/concatenate | solution.py:165
  158.8 8.1 %copy.56 = bf16[512,5184]{0,1:T(8,128)(2,1)} copy(bf16[512,5184]{1,0:T(8,128)(2,1)} %bitcast.70) | data formatting | bytes 10616832 | tf_op jit(solution)/shard_map/reshape | solution.py:165
  166.9 7.7 %dot_general.16 = bf16[6,2,2,2,2,54,512]{6,5,4,3,2,1,0:T(8,128)(2,1)} reshape(bf16[5184,512]{1,0:T(8,128)(2,1)} %bitcast.73) | data formatting | bytes 10616832 | tf_op jit(solution)/shard_map/dot_general | solution.py:172
  193.2 9.9 %concatenate.31 = bf16[2,16,16,5184]{3,2,1,0:T(8,128)(2,1)} concatenate(bf16[2,16,16,192]{3,2,1,0:T(8,128)(2,1)S(1)} %get-tuple-element.46, bf16[2,16,16,192]{3,2,1,0:T(8,128)(2,1)S(1)} %get-tuple-element.45, bf16[2,16,16,192]{3,2,1,0:T(8,128)(2,1)S(1)} %get-tuple-element.44, bf16[2,16,16,192]{3,2,1,0:T(8,128)(2,1)S(1)} %get-tuple-element.43, ...), dimensions={3} | concatenate | bytes 10616832 | tf_op jit(solution)/shard_map/concatenate | solution.py:166
  210.0 4.3 %copy.53 = bf16[6,864,192]{2,1,0:T(8,128)(2,1)} copy(bf16[6,864,192]{1,2,0:T(8,128)(2,1)} %all-gather.4.cloned.1.call-done) | data formatting | bytes 3981312 | tf_op jit(solution)/shard_map/all_gather | solution.py:142
  214.3 4.5 %copy.54 = bf16[27,192,192]{2,1,0:T(8,128)(2,1)} copy(bf16[27,192,192]{1,2,0:T(8,128)(2,1)} %bitcast.74) | data formatting | bytes 3981312 | tf_op jit(solution)/shard_map/transpose | solution.py:176
  218.8 5.3 %convolution_convert_fusion = bf16[512,192]{0,1:T(8,128)(2,1)S(1)} fusion(bf16[512,5184]{1,0:T(8,128)(2,1)} %bitcast.72, bf16[5184,192]{1,0:T(8,128)(2,1)} %bitcast.75), kind=kOutput, calls=%fused_computation.9 | convolution fusion | flops 1019314176 | bytes 7495680 | tf_op jit(solution)/shard_map/dot_general | solution.py:178
  233.4 7.4 %collective-permute-done.17 = f32[3,192]{1,0:T(4,128)S(1)} collective-permute-done((f32[3,192]{1,0:T(4,128)S(1)}, f32[3,192]{1,0:T(4,128)S(1)}, u32[]{:S(2)}, u32[]{:S(2)}) %collective-permute-start.17) | collective-permute-done | bytes 2336 | tf_op jit(solution)/shard_map/ppermute | solution.py:27
  240.9 18.4 %collective-permute-start.18 = (f32[3,192]{1,0:T(4,128)S(1)}, f32[3,192]{1,0:T(4,128)S(1)}, u32[]{:S(2)}, u32[]{:S(2)}) collective-permute-start(f32[3,192]{1,0:T(4,128)S(1)} %fusion.22), channel_id=1, source_target_pairs={{0,4},{1,5},{2,6},{3,7},{4,0},{5,1},{6,2},{7,3},{8,12},{9,13},{10,... | collective-permute-start | bytes 6920 | tf_op jit(solution)/shard_map/ppermute | solution.py:27
  263.1 7.8 %collective-permute-done.19 = f32[3,192]{1,0:T(4,128)S(1)} collective-permute-done((f32[3,192]{1,0:T(4,128)S(1)}, f32[3,192]{1,0:T(4,128)S(1)}, u32[]{:S(2)}, u32[]{:S(2)}) %collective-permute-start.19) | collective-permute-done | bytes 2336 | tf_op jit(solution)/shard_map/ppermute | solution.py:27
  275.3 4.3 %collective-permute-start.21 = (f32[3,192]{1,0:T(4,128)S(1)}, f32[3,192]{1,0:T(4,128)S(1)}, u32[]{:S(2)}, u32[]{:S(2)}) collective-permute-start(f32[3,192]{1,0:T(4,128)S(1)} %add.239), channel_id=1, source_target_pairs={{0,32},{16,48},{32,64},{48,80},{64,0},{80,16},{1,33},{17,49},{33,6... | collective-permute-start | bytes 6920 | tf_op jit(solution)/shard_map/ppermute | solution.py:36
  279.6 6.1 %collective-permute-start.22 = (f32[3,192]{1,0:T(4,128)S(1)}, f32[3,192]{1,0:T(4,128)}, u32[]{:S(2)}, u32[]{:S(2)}) collective-permute-start(f32[3,192]{1,0:T(4,128)S(1)} %add.239), channel_id=1, source_target_pairs={{0,64},{16,80},{32,0},{48,16},{64,32},{80,48},{1,65},{17,81},{33,1... | collective-permute-start | bytes 6920 | tf_op jit(solution)/shard_map/ppermute | solution.py:37
  291.2 4.3 %copy.51 = bf16[6,864,192]{1,0,2:T(8,128)(2,1)} copy(bf16[6,864,192]{1,2,0:T(8,128)(2,1)} %all-gather.4.cloned.1.call-done) | data formatting | bytes 3981312 | tf_op jit(solution)/shard_map/all_gather | solution.py:142
  295.5 4.8 %reshape.219 = bf16[5184,192]{0,1:T(8,128)(2,1)} reshape(bf16[6,864,192]{1,0,2:T(8,128)(2,1)} %copy.51) | data formatting | bytes 3981312
  307.5 5.0 %collective-permute-start.28 = (f32[6,2,54,192]{3,1,2,0:T(2,128)S(1)}, f32[6,2,54,192]{3,1,2,0:T(2,128)}, u32[]{:S(2)}, u32[]{:S(2)}) collective-permute-start(f32[6,2,54,192]{3,1,2,0:T(2,128)S(1)} %copy.62), channel_id=1, source_target_pairs={{0,4},{1,5},{2,6},{3,7},{4,0},{5,1},{6,2},{7,3},{8,12},{9,13},{10,... | collective-permute-start | bytes 1493000 | tf_op jit(solution)/shard_map/ppermute | solution.py:60
  312.5 4.4 %convolution_add_fusion = f32[512,192]{0,1:T(8,128)S(1)} fusion(bf16[512,5184]{1,0:T(8,128)(2,1)} %bitcast.71, bf16[5184,192]{0,1:T(8,128)(2,1)S(1)} %copy-done.6, f32[192]{0:T(256)S(1)} %copy-done.22), kind=kOutput, calls=%fused_computation.8 | convolution fusion | flops 1019314176 | bytes 7693056 | tf_op jit(solution)/shard_map/dot_general | solution.py:167
  317.9 4.5 %collective-permute-start.25 = (f32[3,192]{1,0:T(4,128)S(1)}, f32[3,192]{1,0:T(4,128)S(1)}, u32[]{:S(2)}, u32[]{:S(2)}) collective-permute-start(f32[3,192]{1,0:T(4,128)S(1)} %add.243), channel_id=1, source_target_pairs={{0,384},{96,480},{192,576},{288,672},{384,0},{480,96},{576,192},{6... | collective-permute-start | bytes 6920 | tf_op jit(solution)/shard_map/ppermute | solution.py:27
  327.4 10.8 %collective-permute-done.29 = f32[6,54,192]{2,1,0:T(8,128)S(1)} collective-permute-done((f32[6,54,192]{2,1,0:T(8,128)S(1)}, f32[6,54,192]{2,1,0:T(8,128)S(1)}, u32[]{:S(2)}, u32[]{:S(2)}) %collective-permute-start.29) | collective-permute-done | bytes 248864 | tf_op jit(solution)/shard_map/ppermute | solution.py:60
  338.3 16.6 %collective-permute-start.30 = (f32[3,54,192]{2,1,0:T(8,128)S(1)}, f32[3,54,192]{2,1,0:T(8,128)S(1)}, u32[]{:S(2)}, u32[]{:S(2)}) collective-permute-start(f32[3,54,192]{2,1,0:T(8,128)S(1)} %dynamic-slice_bitcast_fusion.4), channel_id=1, source_target_pairs={{0,16},{16,0},{32,48},{48,32},{64,80},{80,64},{1,17},{17,1},{33,49... | collective-permute-start | bytes 373256 | tf_op jit(solution)/shard_map/ppermute | solution.py:72
  360.5 11.8 %collective-permute-start.32 = (f32[54,192]{1,0:T(8,128)S(1)}, f32[54,192]{1,0:T(8,128)S(1)}, u32[]{:S(2)}, u32[]{:S(2)}) collective-permute-start(f32[54,192]{1,0:T(8,128)S(1)} %get-tuple-element.75), channel_id=1, source_target_pairs={{0,64},{16,80},{32,0},{48,16},{64,32},{80,48},{1,65},{17,81},{33,1... | collective-permute-start | bytes 124424 | tf_op jit(solution)/shard_map/ppermute | solution.py:77
  375.5 4.9 %collective-permute-start.33 = (f32[54,192]{1,0:T(8,128)S(1)}, f32[54,192]{1,0:T(8,128)S(1)}, u32[]{:S(2)}, u32[]{:S(2)}) collective-permute-start(f32[54,192]{1,0:T(8,128)S(1)} %fusion.6), channel_id=1, source_target_pairs={{0,96},{96,0},{192,288},{288,192},{384,480},{480,384},{576,672},{6... | collective-permute-start | bytes 124424 | tf_op jit(solution)/shard_map/ppermute | solution.py:27
  (193 shorter events, 124.5 us)
Async XLA Ops:
  7.2 202.8 %all-gather.4.cloned.1.call-start = ((), (), s32[]{:S(2)}) async-start(), calls=%async_computation | async-start | bytes 2408448 | tf_op jit(solution)/shard_map/all_gather | solution.py:142
  8.3 14.3 %collective-permute-start.6 = (f32[2,192]{1,0:T(2,128)S(1)}, f32[2,192]{1,0:T(2,128)S(1)}, u32[]{:S(2)}, u32[]{:S(2)}) collective-permute-start(f32[2,192]{1,0:T(2,128)S(1)} %pad_maximum_fusion.33), channel_id=1, source_target_pairs={{0,1},{1,0},{2,3},{3,2},{4,5},{5,4},{6,7},{7,6},{8,9},{9,8},{10,11... | collective-permute-start | bytes 4616 | tf_op jit(solution)/shard_map/ppermute | solution.py:27
  24.6 94.3 %collective-permute-start = (bf16[1,16,16,768]{3,2,1,0:T(8,128)(2,1)S(1)}, bf16[1,16,16,768]{3,2,1,0:T(8,128)(2,1)S(1)}, u32[]{:S(2)}, u32[]{:S(2)}) collective-permute-start(bf16[1,16,16,768]{3,2,1,0:T(8,128)(2,1)S(1)} %constant_dynamic-update-slice_fusion), channel_id=1, source_target_pairs={{0,96},{96,192},{192,288},{288,384},{384,480},{480,576},{576,672},... | collective-permute-start | bytes 1179656 | tf_op jit(solution)/shard_map/ppermute | solution.py:15
  25.9 93.0 %collective-permute-start.1 = (bf16[1,16,16,768]{3,2,1,0:T(8,128)(2,1)S(1)}, bf16[1,16,16,768]{3,2,1,0:T(8,128)(2,1)S(1)}, u32[]{:S(2)}, u32[]{:S(2)}) collective-permute-start(bf16[1,16,16,768]{3,2,1,0:T(8,128)(2,1)S(1)} %constant_dynamic-update-slice_fusion), channel_id=1, source_target_pairs={{96,0},{192,96},{288,192},{384,288},{480,384},{576,480},{672,576},... | collective-permute-start | bytes 1179656 | tf_op jit(solution)/shard_map/ppermute | solution.py:18
  27.3 43.7 %collective-permute-start.8 = (f32[2,192]{1,0:T(2,128)S(1)}, f32[2,192]{1,0:T(2,128)S(1)}, u32[]{:S(2)}, u32[]{:S(2)}) collective-permute-start(f32[2,192]{1,0:T(2,128)S(1)} %fusion.23), channel_id=1, source_target_pairs={{0,4},{1,5},{2,6},{3,7},{4,0},{5,1},{6,2},{7,3},{8,12},{9,13},{10,... | collective-permute-start | bytes 4616 | tf_op jit(solution)/shard_map/ppermute | solution.py:27
  71.0 10.6 %collective-permute-start.9 = (f32[2,192]{1,0:T(2,128)S(1)}, f32[2,192]{1,0:T(2,128)S(1)}, u32[]{:S(2)}, u32[]{:S(2)}) collective-permute-start(f32[2,192]{1,0:T(2,128)S(1)} %add.217), channel_id=1, source_target_pairs={{0,8},{1,9},{2,10},{3,11},{4,12},{5,13},{6,14},{7,15},{8,0},{9,1},... | collective-permute-start | bytes 4616 | tf_op jit(solution)/shard_map/ppermute | solution.py:27
  85.9 9.3 %collective-permute-start.11 = (f32[2,192]{1,0:T(2,128)S(1)}, f32[2,192]{1,0:T(2,128)S(1)}, u32[]{:S(2)}, u32[]{:S(2)}) collective-permute-start(f32[2,192]{1,0:T(2,128)S(1)} %add.219), channel_id=1, source_target_pairs={{0,32},{16,48},{32,64},{48,80},{64,0},{80,16},{1,33},{17,49},{33,6... | collective-permute-start | bytes 4616 | tf_op jit(solution)/shard_map/ppermute | solution.py:36
  90.5 5.7 %collective-permute-start.12 = (f32[2,192]{1,0:T(2,128)S(1)}, f32[2,192]{1,0:T(2,128)S(1)}, u32[]{:S(2)}, u32[]{:S(2)}) collective-permute-start(f32[2,192]{1,0:T(2,128)S(1)} %add.219), channel_id=1, source_target_pairs={{0,64},{16,80},{32,0},{48,16},{64,32},{80,48},{1,65},{17,81},{33,1... | collective-permute-start | bytes 4616 | tf_op jit(solution)/shard_map/ppermute | solution.py:37
  96.2 6.1 %collective-permute-start.13 = (f32[2,192]{1,0:T(2,128)S(1)}, f32[2,192]{1,0:T(2,128)S(1)}, u32[]{:S(2)}, u32[]{:S(2)}) collective-permute-start(f32[2,192]{1,0:T(2,128)S(1)} %select_add_fusion.1), channel_id=1, source_target_pairs={{0,96},{96,0},{192,288},{288,192},{384,480},{480,384},{576,672},{6... | collective-permute-start | bytes 4616 | tf_op jit(solution)/shard_map/ppermute | solution.py:27
  102.3 6.6 %collective-permute-start.14 = (f32[2,192]{1,0:T(2,128)S(1)}, f32[2,192]{1,0:T(2,128)S(1)}, u32[]{:S(2)}, u32[]{:S(2)}) collective-permute-start(f32[2,192]{1,0:T(2,128)S(1)} %add.222), channel_id=1, source_target_pairs={{0,192},{96,288},{192,0},{288,96},{384,576},{480,672},{576,384},{6... | collective-permute-start | bytes 4616 | tf_op jit(solution)/shard_map/ppermute | solution.py:27
  108.9 9.6 %collective-permute-start.15 = (f32[2,192]{1,0:T(2,128)S(1)}, f32[2,192]{1,0:T(2,128)S(1)}, u32[]{:S(2)}, u32[]{:S(2)}) collective-permute-start(f32[2,192]{1,0:T(2,128)S(1)} %add.223), channel_id=1, source_target_pairs={{0,384},{96,480},{192,576},{288,672},{384,0},{480,96},{576,192},{6... | collective-permute-start | bytes 4616 | tf_op jit(solution)/shard_map/ppermute | solution.py:27
  120.3 8.0 %collective-permute-start.3 = (bf16[3,1,16,768]{3,2,1,0:T(8,128)(2,1)S(1)}, bf16[3,1,16,768]{3,2,1,0:T(8,128)(2,1)S(1)}, u32[]{:S(2)}, u32[]{:S(2)}) collective-permute-start(bf16[3,1,16,768]{3,2,1,0:T(8,128)(2,1)S(1)} %get-tuple-element.16), channel_id=1, source_target_pairs={{16,0},{32,16},{48,32},{64,48},{80,64},{17,1},{33,17},{49,33},{65,... | collective-permute-start | bytes 221192 | tf_op jit(solution)/shard_map/ppermute | solution.py:18
  128.5 9.6 %collective-permute-start.4 = (bf16[3,18,1,768]{3,2,1,0:T(2,128)(2,1)S(1)}, bf16[3,18,1,768]{3,2,1,0:T(2,128)(2,1)S(1)}, u32[]{:S(2)}, u32[]{:S(2)}) collective-permute-start(bf16[3,18,1,768]{3,2,1,0:T(2,128)(2,1)S(1)} %get-tuple-element.13), channel_id=1, source_target_pairs={{0,1},{1,2},{2,3},{3,4},{4,5},{5,6},{6,7},{7,8},{8,9},{9,10},{10,1... | collective-permute-start | bytes 248840 | tf_op jit(solution)/shard_map/ppermute | solution.py:15
  131.9 7.2 %collective-permute-start.5 = (bf16[3,18,1,768]{3,2,1,0:T(2,128)(2,1)S(1)}, bf16[3,18,1,768]{3,2,1,0:T(2,128)(2,1)S(1)}, u32[]{:S(2)}, u32[]{:S(2)}) collective-permute-start(bf16[3,18,1,768]{3,2,1,0:T(2,128)(2,1)S(1)} %get-tuple-element.14), channel_id=1, source_target_pairs={{1,0},{2,1},{3,2},{4,3},{5,4},{6,5},{7,6},{8,7},{9,8},{10,9},{11,1... | collective-permute-start | bytes 248840 | tf_op jit(solution)/shard_map/ppermute | solution.py:18
  184.4 18.8 %collective-permute-start.26 = (f32[6,2,2,2,54,192]{5,3,4,2,1,0:T(2,128)}, f32[6,2,2,2,54,192]{5,3,4,2,1,0:T(2,128)}, u32[]{:S(2)}, u32[]{:S(2)}) collective-permute-start(f32[6,2,2,2,54,192]{5,3,4,2,1,0:T(2,128)} %copy.58), channel_id=1, source_target_pairs={{0,1},{1,0},{2,3},{3,2},{4,5},{5,4},{6,7},{7,6},{8,9},{9,8},{10,11... | collective-permute-start | bytes 5971976 | tf_op jit(solution)/shard_map/ppermute | solution.py:60
  208.1 96.3 %collective-permute-start.27 = (f32[6,2,2,54,192]{4,2,3,1,0:T(2,128)}, f32[6,2,2,54,192]{4,2,3,1,0:T(2,128)}, u32[]{:S(2)}, u32[]{:S(2)}) collective-permute-start(f32[6,2,2,54,192]{4,2,3,1,0:T(2,128)} %copy.60), channel_id=1, source_target_pairs={{0,2},{1,3},{2,0},{3,1},{4,6},{5,7},{6,4},{7,5},{8,10},{9,11},{10,... | collective-permute-start | bytes 2985992 | tf_op jit(solution)/shard_map/ppermute | solution.py:60
  229.9 10.9 %collective-permute-start.17 = (f32[3,192]{1,0:T(4,128)S(1)}, f32[3,192]{1,0:T(4,128)S(1)}, u32[]{:S(2)}, u32[]{:S(2)}) collective-permute-start(f32[3,192]{1,0:T(4,128)S(1)} %fusion.8), channel_id=1, source_target_pairs={{0,2},{1,3},{2,0},{3,1},{4,6},{5,7},{6,4},{7,5},{8,10},{9,11},{10,... | collective-permute-start | bytes 6920 | tf_op jit(solution)/shard_map/ppermute | solution.py:27
  240.9 19.4 %collective-permute-start.18 = (f32[3,192]{1,0:T(4,128)S(1)}, f32[3,192]{1,0:T(4,128)S(1)}, u32[]{:S(2)}, u32[]{:S(2)}) collective-permute-start(f32[3,192]{1,0:T(4,128)S(1)} %fusion.22), channel_id=1, source_target_pairs={{0,4},{1,5},{2,6},{3,7},{4,0},{5,1},{6,2},{7,3},{8,12},{9,13},{10,... | collective-permute-start | bytes 6920 | tf_op jit(solution)/shard_map/ppermute | solution.py:27
  260.3 10.7 %collective-permute-start.19 = (f32[3,192]{1,0:T(4,128)S(1)}, f32[3,192]{1,0:T(4,128)S(1)}, u32[]{:S(2)}, u32[]{:S(2)}) collective-permute-start(f32[3,192]{1,0:T(4,128)S(1)} %add.237), channel_id=1, source_target_pairs={{0,8},{1,9},{2,10},{3,11},{4,12},{5,13},{6,14},{7,15},{8,0},{9,1},... | collective-permute-start | bytes 6920 | tf_op jit(solution)/shard_map/ppermute | solution.py:27
  275.3 10.4 %collective-permute-start.21 = (f32[3,192]{1,0:T(4,128)S(1)}, f32[3,192]{1,0:T(4,128)S(1)}, u32[]{:S(2)}, u32[]{:S(2)}) collective-permute-start(f32[3,192]{1,0:T(4,128)S(1)} %add.239), channel_id=1, source_target_pairs={{0,32},{16,48},{32,64},{48,80},{64,0},{80,16},{1,33},{17,49},{33,6... | collective-permute-start | bytes 6920 | tf_op jit(solution)/shard_map/ppermute | solution.py:36
  279.6 7.4 %collective-permute-start.22 = (f32[3,192]{1,0:T(4,128)S(1)}, f32[3,192]{1,0:T(4,128)}, u32[]{:S(2)}, u32[]{:S(2)}) collective-permute-start(f32[3,192]{1,0:T(4,128)S(1)} %add.239), channel_id=1, source_target_pairs={{0,64},{16,80},{32,0},{48,16},{64,32},{80,48},{1,65},{17,81},{33,1... | collective-permute-start | bytes 6920 | tf_op jit(solution)/shard_map/ppermute | solution.py:37
  287.7 12.6 %collective-permute-start.23 = (f32[3,192]{1,0:T(4,128)S(1)}, f32[3,192]{1,0:T(4,128)S(1)}, u32[]{:S(2)}, u32[]{:S(2)}) collective-permute-start(f32[3,192]{1,0:T(4,128)S(1)} %select_add_fusion), channel_id=1, source_target_pairs={{0,96},{96,0},{192,288},{288,192},{384,480},{480,384},{576,672},{6... | collective-permute-start | bytes 6920 | tf_op jit(solution)/shard_map/ppermute | solution.py:27
  300.2 17.7 %collective-permute-start.24 = (f32[3,192]{1,0:T(4,128)S(1)}, f32[3,192]{1,0:T(4,128)S(1)}, u32[]{:S(2)}, u32[]{:S(2)}) collective-permute-start(f32[3,192]{1,0:T(4,128)S(1)} %add.242), channel_id=1, source_target_pairs={{0,192},{96,288},{192,0},{288,96},{384,576},{480,672},{576,384},{6... | collective-permute-start | bytes 6920 | tf_op jit(solution)/shard_map/ppermute | solution.py:27
  307.5 15.0 %collective-permute-start.28 = (f32[6,2,54,192]{3,1,2,0:T(2,128)S(1)}, f32[6,2,54,192]{3,1,2,0:T(2,128)}, u32[]{:S(2)}, u32[]{:S(2)}) collective-permute-start(f32[6,2,54,192]{3,1,2,0:T(2,128)S(1)} %copy.62), channel_id=1, source_target_pairs={{0,4},{1,5},{2,6},{3,7},{4,0},{5,1},{6,2},{7,3},{8,12},{9,13},{10,... | collective-permute-start | bytes 1493000 | tf_op jit(solution)/shard_map/ppermute | solution.py:60
  317.9 9.5 %collective-permute-start.25 = (f32[3,192]{1,0:T(4,128)S(1)}, f32[3,192]{1,0:T(4,128)S(1)}, u32[]{:S(2)}, u32[]{:S(2)}) collective-permute-start(f32[3,192]{1,0:T(4,128)S(1)} %add.243), channel_id=1, source_target_pairs={{0,384},{96,480},{192,576},{288,672},{384,0},{480,96},{576,192},{6... | collective-permute-start | bytes 6920 | tf_op jit(solution)/shard_map/ppermute | solution.py:27
  323.7 14.5 %collective-permute-start.29 = (f32[6,54,192]{2,1,0:T(8,128)S(1)}, f32[6,54,192]{2,1,0:T(8,128)S(1)}, u32[]{:S(2)}, u32[]{:S(2)}) collective-permute-start(f32[6,54,192]{2,1,0:T(8,128)S(1)} %dynamic-slice_bitcast_fusion.3), channel_id=1, source_target_pairs={{0,8},{1,9},{2,10},{3,11},{4,12},{5,13},{6,14},{7,15},{8,0},{9,1},... | collective-permute-start | bytes 746504 | tf_op jit(solution)/shard_map/ppermute | solution.py:60
  338.3 19.4 %collective-permute-start.30 = (f32[3,54,192]{2,1,0:T(8,128)S(1)}, f32[3,54,192]{2,1,0:T(8,128)S(1)}, u32[]{:S(2)}, u32[]{:S(2)}) collective-permute-start(f32[3,54,192]{2,1,0:T(8,128)S(1)} %dynamic-slice_bitcast_fusion.4), channel_id=1, source_target_pairs={{0,16},{16,0},{32,48},{48,32},{64,80},{80,64},{1,17},{17,1},{33,49... | collective-permute-start | bytes 373256 | tf_op jit(solution)/shard_map/ppermute | solution.py:72
  357.7 14.8 %collective-permute-start.31 = (f32[54,192]{1,0:T(8,128)S(1)}, f32[54,192]{1,0:T(8,128)S(1)}, u32[]{:S(2)}, u32[]{:S(2)}) collective-permute-start(f32[54,192]{1,0:T(8,128)S(1)} %get-tuple-element.74), channel_id=1, source_target_pairs={{0,32},{16,48},{32,64},{48,80},{64,0},{80,16},{1,33},{17,49},{33,6... | collective-permute-start | bytes 124424 | tf_op jit(solution)/shard_map/ppermute | solution.py:76
  360.5 15.0 %collective-permute-start.32 = (f32[54,192]{1,0:T(8,128)S(1)}, f32[54,192]{1,0:T(8,128)S(1)}, u32[]{:S(2)}, u32[]{:S(2)}) collective-permute-start(f32[54,192]{1,0:T(8,128)S(1)} %get-tuple-element.75), channel_id=1, source_target_pairs={{0,64},{16,80},{32,0},{48,16},{64,32},{80,48},{1,65},{17,81},{33,1... | collective-permute-start | bytes 124424 | tf_op jit(solution)/shard_map/ppermute | solution.py:77
  375.5 6.5 %collective-permute-start.33 = (f32[54,192]{1,0:T(8,128)S(1)}, f32[54,192]{1,0:T(8,128)S(1)}, u32[]{:S(2)}, u32[]{:S(2)}) collective-permute-start(f32[54,192]{1,0:T(8,128)S(1)} %fusion.6), channel_id=1, source_target_pairs={{0,96},{96,0},{192,288},{288,192},{384,480},{480,384},{576,672},{6... | collective-permute-start | bytes 124424 | tf_op jit(solution)/shard_map/ppermute | solution.py:27
  382.0 5.8 %collective-permute-start.34 = (f32[54,192]{1,0:T(8,128)S(1)}, f32[54,192]{1,0:T(8,128)S(1)}, u32[]{:S(2)}, u32[]{:S(2)}) collective-permute-start(f32[54,192]{1,0:T(8,128)S(1)} %add.275), channel_id=1, source_target_pairs={{0,192},{96,288},{192,0},{288,96},{384,576},{480,672},{576,384},{6... | collective-permute-start | bytes 124424 | tf_op jit(solution)/shard_map/ppermute | solution.py:27
  387.8 8.8 %collective-permute-start.35 = (f32[54,192]{1,0:T(8,128)S(1)}, f32[54,192]{1,0:T(8,128)S(1)}, u32[]{:S(2)}, u32[]{:S(2)}) collective-permute-start(f32[54,192]{1,0:T(8,128)S(1)} %add.276), channel_id=1, source_target_pairs={{0,384},{96,480},{192,576},{288,672},{384,0},{480,96},{576,192},{6... | collective-permute-start | bytes 124424 | tf_op jit(solution)/shard_map/ppermute | solution.py:27
  (28 other events, 375.9 us)
Sparse Core Ops, SparseCore 0:
  71.0 59.8 all-gather.3
